TPU v7x, 128 devices: a whole 4x4x4 slice. The times are simulated.
128 devices in a mesh: kv: 2 (over core), page: 64 (over z, y, x).
Axes of the slice: x: 4, y: 4, z: 4, core: 2. Of those that a mesh axis runs over, the one named last changes fastest.
Arguments:
- tokens: bfloat16 [16384, 2048], P('page'), may hold values from -6 to 6
- in_gain: float32 [2048], replicated, may hold values from 0.4 to 1.6
- w_query: bfloat16 [2048, 2048], P(None, 'kv'), may hold values from -0.125 to 0.125
- key_projection_weight: bfloat16 [2048, 512], P(None, 'kv'), may hold values from -0.125 to 0.125
- value_projection_weight: bfloat16 [2048, 512], P(None, 'kv'), may hold values from -0.125 to 0.125
- q_gain: float32 [256], replicated, may hold values from 0.5 to 6
- k_gain: float32 [256], replicated, may hold values from 0.4 to 1.6
- w_out: bfloat16 [2048, 2048], P('kv'), may hold values from -0.125 to 0.125
- post_gain: float32 [2048], replicated, may hold values from 0.25 to 1.75
- laurel_left: bfloat16 [2048, 64], replicated, may hold values from -0.125 to 0.125
- laurel_right: bfloat16 [64, 2048], replicated, may hold values from -0.75 to 0.75
- laurel_gain: float32 [2048], replicated, may hold values from 0.25 to 1.75
- prefix_key_slots: bfloat16 [16384, 512], P('page', 'kv'), may hold values from -20 to 20
- prefix_value_slots: bfloat16 [16384, 512], P('page', 'kv'), may hold values from -6 to 6
- prefix_slot_map: int32 [128], replicated, may hold values from 0 to 127, each once
- page_lengths: int32 [32], replicated, may hold values from 1 to 8, 128 in all
- request_group: int32 [32], replicated, may hold values from 0 to 3
- suffix_page_map: int32 [128], P('page'), may hold values from 0 to 127, as said below
Outputs:
- layer_out: bfloat16 [16384, 2048], P('page', 'kv')
- suffix_key_cache: bfloat16 [16384, 512], P('page', 'kv')
- suffix_value_cache: bfloat16 [16384, 512], P('page', 'kv')
Inputs may be any that keep to these rules, and one draw needn't show every extreme that they name: `prefix_slot_map`: A permutation: entry g * 32 + j names the page slot (rows of 128 tokens of prefix_key_slots and prefix_value_slots) that holds page j of prefix g. `page_lengths`: they sum to 128; some request has exactly 8 pages. `suffix_page_map`: A permutation that keeps every logical page within the aligned block of 2 pages that contains it.
All inputs are finite; a program needn't handle non-finite values.
Results may differ from a plain program's by a relative error of at most 0.01.
The roundings to bfloat16 on the way count: a program that leaves them out, or rounds other values in their place, can miss the bound.
Values may be sent and summed in bfloat16 or wider, within the bound.
No kernel may reach another device: no remote copies, remote signals or barrier semaphores. Data moves between devices by JAX's collectives and lax.ppermute only.
A program may use at most 128 MiB of HBM per device.

v0:
```python
import jax
import jax.numpy as jnp
from jax import lax
from jax.sharding import PartitionSpec as P

HEAD_SIZE = 256
PAGE_TOKENS = 128
PREFIX_TOKENS = 4096
PREFIX_COUNT = 4
MAXP = 8
PREFIX_PAGES = 32


epsilon = 1e-06
rope_base = 1000000.0
masked_low = -1e30


def passed_along(block, axis, distance):
    devices = range(lax.axis_size(axis))
    route = [(i - distance, i) for i in devices if i - distance in devices]
    return lax.ppermute(block, axis, route)


def rms_scale(values):
    return lax.rsqrt(jnp.mean(values * values, axis=-1, keepdims=True) + epsilon)


def rotate(values, positions):
    half_dim = values.shape[-1] // 2
    inv_freq = rope_base ** (-(jnp.arange(half_dim).astype(jnp.float32) * 2.0 / values.shape[-1]))
    angles = positions.astype(jnp.float32)[:, None] * inv_freq[None, :]
    cosine = jnp.cos(angles)[:, None, :]
    sines = jnp.sin(angles)[:, None, :]
    first_half = values[..., :half_dim]
    second_half = values[..., half_dim:]
    return jnp.concatenate(
        [first_half * cosine - second_half * sines, second_half * cosine + first_half * sines],
        axis=-1,
    )


def project(
    tokens,
    in_gain,
    w_query,
    key_projection_weight,
    value_projection_weight,
    q_gain,
    k_gain,
    positions,
):
    tok_count = tokens.shape[0]
    tokens_wide = tokens.astype(jnp.float32)
    normed = (tokens_wide * rms_scale(tokens_wide) * in_gain).astype(jnp.bfloat16)
    queries = jnp.dot(normed, w_query, preferred_element_type=jnp.float32).reshape(
        tok_count, -1, HEAD_SIZE
    )
    queries = rotate(queries * rms_scale(queries) * q_gain, positions).astype(jnp.bfloat16)
    fresh_key_rows = jnp.dot(
        normed, key_projection_weight, preferred_element_type=jnp.float32
    ).reshape(tok_count, -1, HEAD_SIZE)
    fresh_key_rows = rotate(fresh_key_rows * rms_scale(fresh_key_rows) * k_gain, positions).astype(
        jnp.bfloat16
    )
    fresh_value_rows = jnp.dot(
        normed, value_projection_weight, preferred_element_type=jnp.float32
    ).reshape(tok_count, -1, HEAD_SIZE)
    fresh_value_rows = (fresh_value_rows * rms_scale(fresh_value_rows)).astype(jnp.bfloat16)
    return (
        normed,
        queries,
        fresh_key_rows.reshape(tok_count, HEAD_SIZE),
        fresh_value_rows.reshape(tok_count, HEAD_SIZE),
    )


def token_places(first_index, tok_count, page_lengths, request_group):
    tok_ids = first_index + jnp.arange(tok_count, dtype=jnp.int32)
    page_of = tok_ids // PAGE_TOKENS
    page_starts = jnp.cumsum(page_lengths) - page_lengths
    belongs = (page_of[:, None] >= page_starts[None, :]) & (
        page_of[:, None] < (page_starts + page_lengths)[None, :]
    )
    belongs = (belongs & (tok_ids[:, None] >= 0)).astype(jnp.int32)
    request_ids = jnp.arange(page_starts.shape[0], dtype=jnp.int32)
    requests = jnp.sum(belongs * request_ids[None, :], axis=1) - (1 - jnp.sum(belongs, axis=1))
    position = tok_ids - jnp.sum(belongs * page_starts[None, :], axis=1) * PAGE_TOKENS
    groups = jnp.sum(belongs * request_group[None, :], axis=1)
    return (requests, position, groups)


def attend(queries, keys_block, values_block, key_mask):
    scores = jnp.einsum("qhd,kd->qhk", queries, keys_block, preferred_element_type=jnp.float32)
    wide_mask = key_mask[:, None, :]
    scores = jnp.where(wide_mask, scores, masked_low)
    row_top = jnp.max(scores, axis=-1)
    weights = jnp.where(wide_mask, jnp.exp(scores - row_top[..., None]), 0.0)
    row_total = jnp.sum(weights, axis=-1)
    mixture = jnp.einsum(
        "qhk,kd->qhd",
        weights.astype(jnp.bfloat16),
        values_block,
        preferred_element_type=jnp.float32,
    )
    return (row_top, row_total, mixture)


def combine(carried, incoming):
    row_top = jnp.maximum(carried[0], incoming[0])
    old_factor = jnp.exp(carried[0] - row_top)
    new_factor = jnp.exp(incoming[0] - row_top)
    row_total = carried[1] * old_factor + incoming[1] * new_factor
    mixture = carried[2] * old_factor[..., None] + incoming[2] * new_factor[..., None]
    return (row_top, row_total, mixture)


def local(
    tokens,
    in_gain,
    w_query,
    key_projection_weight,
    value_projection_weight,
    q_gain,
    k_gain,
    w_out,
    post_gain,
    laurel_left,
    laurel_right,
    laurel_gain,
    prefix_key_slots,
    prefix_value_slots,
    prefix_slot_map,
    page_lengths,
    request_group,
    suffix_page_map,
):
    tok_count = tokens.shape[0]
    pages_here = tok_count // PAGE_TOKENS
    device = lax.axis_index("page")
    first_index = device * tok_count
    prefix_both = jnp.concatenate([prefix_key_slots, prefix_value_slots], axis=1)
    every_slot = lax.all_gather(prefix_both, "page", axis=0, tiled=True)
    requests, position, groups = token_places(first_index, tok_count, page_lengths, request_group)
    normed, queries, fresh_key_rows, fresh_value_rows = project(
        tokens,
        in_gain,
        w_query,
        key_projection_weight,
        value_projection_weight,
        q_gain,
        k_gain,
        position + PREFIX_TOKENS,
    )
    local_slot = suffix_page_map - device * pages_here
    placing = (local_slot[:, None] == jnp.arange(pages_here, dtype=jnp.int32)[None, :]).astype(
        jnp.bfloat16
    )
    both_pages = jnp.concatenate(
        [
            fresh_key_rows.reshape(pages_here, PAGE_TOKENS * HEAD_SIZE),
            fresh_value_rows.reshape(pages_here, PAGE_TOKENS * HEAD_SIZE),
        ],
        axis=1,
    )
    placed = jnp.dot(placing.T, both_pages, preferred_element_type=jnp.float32).astype(jnp.bfloat16)
    suffix_key_cache = placed[:, : PAGE_TOKENS * HEAD_SIZE].reshape(tok_count, HEAD_SIZE)
    suffix_value_cache = placed[:, PAGE_TOKENS * HEAD_SIZE :].reshape(tok_count, HEAD_SIZE)

    reach = (MAXP + pages_here - 2) // pages_here
    fresh_both = jnp.concatenate([fresh_key_rows, fresh_value_rows], axis=1)
    window = fresh_both
    covered = 1
    while covered < reach + 1:
        step = min(covered, reach + 1 - covered)
        moved = passed_along(window[: step * tok_count], "page", covered)
        window = jnp.concatenate([window, moved], axis=0)
        covered += step
    window_requests = []
    window_positions = []
    for shift_step in range(reach + 1):
        far_requests, far_position, _ = token_places(
            first_index - shift_step * tok_count, tok_count, page_lengths, request_group
        )
        window_requests.append(far_requests)
        window_positions.append(far_position)
    key_requests = jnp.concatenate(window_requests, axis=0)
    key_positions = jnp.concatenate(window_positions, axis=0)
    suffix_keys = window[:, :HEAD_SIZE]
    suffix_values = window[:, HEAD_SIZE:]

    heads = queries.shape[1]
    page_queries = queries.reshape(pages_here, PAGE_TOKENS, heads, HEAD_SIZE)
    page_requests = requests.reshape(pages_here, PAGE_TOKENS)
    page_positions = position.reshape(pages_here, PAGE_TOKENS)
    page_groups = groups.reshape(pages_here, PAGE_TOKENS)[:, 0]
    chosen = jnp.take(
        prefix_slot_map.reshape(PREFIX_COUNT, PREFIX_PAGES), page_groups, axis=0
    )
    slot_pages = every_slot.reshape(-1, PAGE_TOKENS, 2 * HEAD_SIZE)
    group_rows = jnp.take(slot_pages, chosen.reshape(-1), axis=0).reshape(
        pages_here, PREFIX_PAGES * PAGE_TOKENS, 2 * HEAD_SIZE
    )
    prefix_keys = group_rows[..., :HEAD_SIZE]
    prefix_values = group_rows[..., HEAD_SIZE:]
    prefix_scores = jnp.einsum(
        "pqhd,pkd->pqhk", page_queries, prefix_keys, preferred_element_type=jnp.float32
    )
    suffix_scores = jnp.einsum(
        "pqhd,kd->pqhk", page_queries, suffix_keys, preferred_element_type=jnp.float32
    )
    suffix_mask = (page_requests[:, :, None] == key_requests[None, None, :]) & (
        key_positions[None, None, :] <= page_positions[:, :, None]
    )
    suffix_mask = suffix_mask[:, :, None, :]
    suffix_scores = jnp.where(suffix_mask, suffix_scores, masked_low)
    row_top = jnp.maximum(
        jnp.max(prefix_scores, axis=-1), jnp.max(suffix_scores, axis=-1)
    )[..., None]
    prefix_weights = jnp.exp(prefix_scores - row_top)
    suffix_weights = jnp.where(suffix_mask, jnp.exp(suffix_scores - row_top), 0.0)
    row_total = jnp.sum(prefix_weights, axis=-1) + jnp.sum(suffix_weights, axis=-1)
    mixture = jnp.einsum(
        "pqhk,pkd->pqhd",
        prefix_weights.astype(jnp.bfloat16),
        prefix_values,
        preferred_element_type=jnp.float32,
    ) + jnp.einsum(
        "pqhk,kd->pqhd",
        suffix_weights.astype(jnp.bfloat16),
        suffix_values,
        preferred_element_type=jnp.float32,
    )
    attended = (mixture / row_total[..., None]).astype(jnp.bfloat16).reshape(tok_count, -1)
    attn_part = jnp.dot(attended, w_out, preferred_element_type=jnp.float32)
    kv_index = lax.axis_index("kv")
    model_width = tokens.shape[1]
    half_width = model_width // lax.axis_size("kv")

    def columns(source):
        return lax.dynamic_slice_in_dim(source, kv_index * half_width, half_width, source.ndim - 1)

    partner_part = lax.ppermute(attn_part.astype(jnp.bfloat16), "kv", [(0, 1), (1, 0)])
    summed_out = attn_part + partner_part.astype(jnp.float32)
    low_rank = jnp.dot(normed, laurel_left, preferred_element_type=jnp.float32).astype(jnp.bfloat16)
    laurel_full = jnp.dot(low_rank, laurel_right, preferred_element_type=jnp.float32)
    attn_half = columns(summed_out)
    attn_branch = attn_half * rms_scale(summed_out) * columns(post_gain)
    laurel = columns(normed).astype(jnp.float32) + columns(laurel_full) * rms_scale(
        laurel_full
    ) * columns(laurel_gain)
    layer_out = (
        (columns(tokens).astype(jnp.float32) + attn_branch + laurel) * 2.0 ** (-0.5)
    ).astype(jnp.bfloat16)
    return (layer_out, suffix_key_cache, suffix_value_cache)


def solution(mesh):
    placed = (
        P("page", None),
        P(),
        P(None, "kv"),
        P(None, "kv"),
        P(None, "kv"),
        P(),
        P(),
        P("kv", None),
        P(),
        P(),
        P(),
        P(),
        P("page", "kv"),
        P("page", "kv"),
        P(),
        P(),
        P(),
        P("page"),
    )
    return jax.shard_map(
        local,
        mesh=mesh,
        in_specs=placed,
        out_specs=(P("page", "kv"), P("page", "kv"), P("page", "kv")),
        check_vma=False,
    )
```

profile of v0, /device:TPU:1, one launch (start us, length us, event | category | flops | bytes accessed | tf_op | source)
XLA Modules:
  0.0 201.1 jit_solution(15715828985698280633)
XLA Ops:
  7.2 1.8 pad_maximum_fusion.3
  9.1 0.7 copy.64
  10.8 1.5 convert_reduce_fusion
  12.3 1.5 fusion.14
  13.8 1.5 fusion.16
  17.2 0.7 pad_maximum_fusion.4
  17.9 4.6 %collective-permute-start = (bf16[256,512]{0,1:T(8,128)(2,1)}, bf16[256,512]{0,1:T(8,128)(2,1)}, u32[]{:S(2)}, u32[]{:S(2)}) collective-permute-start(bf16[256,512]{0,1:T(8,128)(2,1)} %pad_maximum_fusion.4), channel_id=1, source_target_pairs={{0,1},{1,2},{2,3},{3,4},{4,5},{5,6},{6,7},{7,8},{8,9},{9,10},{10,1... | collective-permute-start | bytes 786440 | tf_op jit(solution)/shard_map/ppermute | solution.py:22
  22.5 3.2 %collective-permute-start.2 = (bf16[256,512]{0,1:T(8,128)(2,1)}, bf16[256,512]{0,1:T(8,128)(2,1)}, u32[]{:S(2)}, u32[]{:S(2)}) collective-permute-start(bf16[256,512]{0,1:T(8,128)(2,1)} %pad_maximum_fusion.4), channel_id=1, source_target_pairs={{0,4},{1,5},{2,6},{3,7},{4,8},{5,9},{6,10},{7,11},{8,12},{9,13},{1... | collective-permute-start | bytes 786440 | tf_op jit(solution)/shard_map/ppermute | solution.py:22
  25.8 0.8 copy.71
  26.5 3.4 %fusion.54 = f32[256,1024]{1,0:T(8,128)S(1)} fusion(bf16[256,2048]{1,0:T(8,128)(2,1)S(1)} %fusion.16, bf16[2048,1024]{1,0:T(8,128)(2,1)} %param.20), kind=kOutput, calls=%fused_computation.164 | convolution fusion | flops 1073741824 | bytes 6291456 | tf_op jit(solution)/shard_map/dot_general | solution.py:56
  30.9 0.7 reshape.469
  31.6 0.8 fusion.46
  33.0 0.8 and_reduce_fusion
  34.1 0.9 reshape_reshape.4
  35.7 0.7 constant_dynamic-update-slice_fusion.7
  37.0 0.7 constant_dynamic-update-slice_fusion.3
  37.7 0.7 constant_dynamic-update-slice_fusion.1
  38.4 1.3 fusion.47
  39.7 1.3 constant_dynamic-update-slice_fusion.6
  41.0 1.3 constant_dynamic-update-slice_fusion.4
  42.3 1.3 constant_dynamic-update-slice_fusion.2
  43.6 1.3 constant_dynamic-update-slice_fusion
  45.0 1.3 convolution_convert_fusion
  46.3 1.2 multiply_cosine_fusion.1
  47.5 1.0 compare_and_fusion
  48.6 0.9 fusion.21
  49.5 1.0 pad_maximum_fusion.2
  50.5 4.4 %collective-permute-start.1 = (bf16[512,512]{0,1:T(8,128)(2,1)S(1)}, bf16[512,512]{0,1:T(8,128)(2,1)S(1)}, u32[]{:S(2)}, u32[]{:S(2)}) collective-permute-start(bf16[512,512]{0,1:T(8,128)(2,1)S(1)} %pad_maximum_fusion.2), channel_id=1, source_target_pairs={{0,2},{1,3},{2,4},{3,5},{4,6},{5,7},{6,8},{7,9},{8,10},{9,11},{10,... | collective-permute-start | bytes 1572872 | tf_op jit(solution)/shard_map/ppermute | solution.py:22
  55.1 17.1 %collective-permute-done.1 = bf16[512,512]{0,1:T(8,128)(2,1)S(1)} collective-permute-done((bf16[512,512]{0,1:T(8,128)(2,1)S(1)}, bf16[512,512]{0,1:T(8,128)(2,1)S(1)}, u32[]{:S(2)}, u32[]{:S(2)}) %collective-permute-start.1) | collective-permute-done | bytes 524320 | tf_op jit(solution)/shard_map/ppermute | solution.py:22
  72.2 1.1 pad_maximum_fusion
  73.4 1.0 copy-done.6
  74.4 3.3 %select_reduce_fusion = (f32[2,128,4]{1,2,0:T(4,128)S(1)}, f32[2,128,4,1280]{3,1,2,0:T(8,128)}) fusion(pred[2,128,1280]{2,1,0:T(8,128)(4,1)S(1)} %compare_and_fusion, bf16[1280,512]{0,1:T(8,128)(2,1)S(1)} %pad_maximum_fusion, bf16[2,128,4,128]{3,1,0,2:T(8,128)(2,1)S(1)} %bitcast.77, bf16[2,128,4,128]{3,1,0,2:T(8,128)(2,1)S(1)} %bitcast.75), kind=kOutput, calls=%fused_computation.10 | convolution fusion | flops 674757632 | bytes 6754304 | tf_op jit(solution)/shard_map/pqhd,kd->pqhk/dot_general | solution.py:209
  77.7 54.2 %all-gather.2.cloned.1.call-done = bf16[16384,512]{1,0:T(8,128)(2,1)} async-done(((bf16[256,512]{1,0:T(8,128)(2,1)}), bf16[16384,512]{1,0:T(8,128)(2,1)}) %all-gather.2.cloned.1.call-update) | async-done | bytes 16777232 | tf_op jit(solution)/shard_map/all_gather | solution.py:143
  131.9 11.2 %gather_fusion.1 = bf16[64,128,512]{2,1,0:T(8,128)(2,1)} fusion(bf16[128,128,512]{2,1,0:T(8,128)(2,1)} %bitcast.65, s32[1024]{0:T(1024)S(1)} %pad_clamp_fusion), kind=kCustom, calls=%fused_computation.1 | custom fusion | bytes 16777472 | tf_op jit(solution)/shard_map/jit(_take)/gather | solution.py:201
  143.0 4.7 %bitcast_select_fusion = bf16[2,4096,512]{2,1,0:T(8,128)(2,1)S(1)} fusion(pred[2,4096]{1,0:T(4,128)(4,1)S(1)} %bitcast.79, bf16[2,4096,512]{2,1,0:T(8,128)(2,1)} %bitcast.64), kind=kLoop, calls=%fused_computation.7 | loop fusion | flops 4194304 | bytes 16785408 | tf_op jit(solution)/shard_map/jit(_take)/select_n | solution.py:201
  147.7 7.5 %fusion.52 = (f32[2,128,4]{1,2,0:T(4,128)S(1)}, f32[2,128,4,4096]{3,1,2,0:T(8,128)}) fusion(bf16[2,4096,512]{2,1,0:T(8,128)(2,1)S(1)} %bitcast_select_fusion, bf16[2,128,4,128]{3,1,0,2:T(8,128)(2,1)S(1)} %bitcast.78, bf16[2,128,4,128]{3,1,0,2:T(8,128)(2,1)S(1)} %bitcast.76), kind=kOutput, calls=%fused_computation.162 | convolution fusion | flops 2152725504 | bytes 21499904 | tf_op jit(solution)/shard_map/pqhd,pkd->pqhk/dot_general | solution.py:206
  155.2 0.8 copy-done.2
  155.9 8.1 %fusion = f32[2,128,4]{1,2,0:T(4,128)S(1)} fusion(f32[2,128,4,4096]{3,1,2,0:T(8,128)} %get-tuple-element.49, f32[2,128,4]{1,2,0:T(4,128)S(1)} %max.7), kind=kLoop, calls=%fused_computation.4 | loop fusion | flops 8387584 | bytes 16785408 | tf_op jit(solution)/shard_map/reduce_sum | solution.py:222
  164.0 8.4 %fusion.2 = f32[2,128,4,256]{3,1,2,0:T(8,128)S(1)} fusion(f32[2,128,4,4096]{3,1,2,0:T(8,128)} %get-tuple-element.49, f32[2,128,4]{1,2,0:T(4,128)S(1)} %max.7, bf16[2,4096,512]{2,1,0:T(8,128)(2,1)} %copy-done.2), kind=kOutput, calls=%fused_computation.6 | convolution fusion | flops 2155872256 | bytes 22024192 | tf_op jit(solution)/shard_map/pqhk,pkd->pqhd/dot_general | solution.py:223
  172.4 4.0 %fusion.6 = f32[2,128,4]{1,2,0:T(4,128)S(1)} fusion(f32[2,128,4,1280]{3,1,2,0:T(8,128)} %get-tuple-element.55, f32[2,128,4]{1,2,0:T(4,128)S(1)} %max.7, pred[2,128,1280]{2,1,0:T(8,128)(4,1)S(1)} %copy-done.9), kind=kLoop, calls=%fused_computation.14 | loop fusion | flops 5241856 | bytes 5578752 | tf_op jit(solution)/shard_map/reduce_sum | solution.py:222
  176.5 4.2 %divide_convert_fusion = bf16[2,128,4,256]{3,1,2,0:T(8,128)(2,1)S(1)} fusion(f32[2,128,4,256]{3,1,2,0:T(8,128)S(1)} %fusion.2, f32[2,128,4,1280]{3,1,2,0:T(8,128)} %get-tuple-element.55, f32[2,128,4]{1,2,0:T(4,128)S(1)} %max.7, pred[2,128,1280]{2,1,0:T(8,128)(4,1)S(1)} %copy-done.9, bf16[1280,512]{0,1:T(8,128)(2,1)S(1)} %copy-done.7, f32[2,128,4]{1,2,0:T(4,128)S(1)} %add.270), kind=kOutput, calls=%fused_computation.37 | convolution fusion | flops 677117952 | bytes 7806976 | tf_op jit(solution)/shard_map/pqhk,kd->pqhd/dot_general | solution.py:228
  181.2 3.0 %fusion.53 = (bf16[256,2048]{1,0:T(8,128)(2,1)}, f32[256,2048]{1,0:T(8,128)}) fusion(bf16[256,1024]{1,0:T(8,128)(2,1)S(1)} %bitcast.68, bf16[1024,2048]{1,0:T(8,128)(2,1)S(1)} %copy-done.5), kind=kOutput, calls=%fused_computation.163 | convolution fusion | flops 1074266112 | bytes 7864320 | tf_op jit(solution)/shard_map/dot_general | solution.py:235
  184.2 0.8 collective-permute-start.3
  185.2 0.7 reshape.472
  186.0 0.7 reshape.473
  186.7 3.7 %multiply_reduce_fusion = (f32[256]{0:T(256)S(1)}, f32[256,2048]{1,0:T(8,128)}) fusion(bf16[64,2048]{1,0:T(8,128)(2,1)S(1)} %copy-done.12, bf16[256,2048]{1,0:T(8,128)(2,1)S(1)} %fusion.16, bf16[2048,64]{0,1:T(8,128)(2,1)} %param.27), kind=kOutput, calls=%fused_computation.26 | convolution fusion | flops 135282432 | bytes 3671040 | tf_op jit(solution)/shard_map/dot_general | solution.py:246
  190.5 2.4 %multiply_reduce_fusion.1 = (f32[256]{0:T(256)S(1)}, f32[256,2048]{1,0:T(8,128)S(1)}) fusion(f32[256,2048]{1,0:T(8,128)} %get-tuple-element.57, bf16[256,2048]{1,0:T(8,128)(2,1)} %collective-permute-done.3), kind=kLoop, calls=%fused_computation.27 | loop fusion | flops 2096896 | bytes 5243904 | tf_op jit(solution)/shard_map/reduce_sum | solution.py:26
  193.0 1.3 multiply_convert_fusion
  (84 shorter events, 7.0 us)
Async XLA Ops:
  7.2 8.2 %copy-start = (bf16[2048,256]{1,0:T(8,128)(2,1)S(1)}, bf16[2048,256]{1,0:T(8,128)(2,1)}, u32[]{:S(2)}) copy-start(bf16[2048,256]{1,0:T(8,128)(2,1)} %param.21) | copy-start | bytes 3145732
  7.2 8.7 %copy-start.10 = (bf16[2048,256]{1,0:T(8,128)(2,1)S(1)}, bf16[2048,256]{1,0:T(8,128)(2,1)}, u32[]{:S(2)}) copy-start(bf16[2048,256]{1,0:T(8,128)(2,1)} %param.22) | copy-start | bytes 3145732
  7.2 124.7 %all-gather.2.cloned.1.call-start = ((), (), s32[]{:S(2)}) async-start(), calls=%async_computation | async-start | bytes 17039360 | tf_op jit(solution)/shard_map/all_gather | solution.py:143
  9.1 7.4 %copy-start.14 = (f32[256]{0:T(256)S(1)}, f32[256]{0:T(256)}, u32[]{:S(2)}) copy-start(f32[256]{0:T(256)} %param.24) | copy-start | bytes 3076
  10.7 5.9 %copy-start.13 = (f32[128]{0:T(128)}, f32[128]{0:T(128)S(1)}, u32[]{:S(2)}) copy-start(f32[128]{0:T(128)S(1)} %negate_power_fusion) | copy-start | bytes 1540
  17.9 31.6 %collective-permute-start = (bf16[256,512]{0,1:T(8,128)(2,1)}, bf16[256,512]{0,1:T(8,128)(2,1)}, u32[]{:S(2)}, u32[]{:S(2)}) collective-permute-start(bf16[256,512]{0,1:T(8,128)(2,1)} %pad_maximum_fusion.4), channel_id=1, source_target_pairs={{0,1},{1,2},{2,3},{3,4},{4,5},{5,6},{6,7},{7,8},{8,9},{9,10},{10,1... | collective-permute-start | bytes 786440 | tf_op jit(solution)/shard_map/ppermute | solution.py:22
  22.5 32.6 %collective-permute-start.2 = (bf16[256,512]{0,1:T(8,128)(2,1)}, bf16[256,512]{0,1:T(8,128)(2,1)}, u32[]{:S(2)}, u32[]{:S(2)}) collective-permute-start(bf16[256,512]{0,1:T(8,128)(2,1)} %pad_maximum_fusion.4), channel_id=1, source_target_pairs={{0,4},{1,5},{2,6},{3,7},{4,8},{5,9},{6,10},{7,11},{8,12},{9,13},{1... | collective-permute-start | bytes 786440 | tf_op jit(solution)/shard_map/ppermute | solution.py:22
  48.6 24.8 %copy-start.8 = (pred[2,128,1280]{2,1,0:T(8,128)(4,1)}, pred[2,128,1280]{2,1,0:T(8,128)(4,1)S(1)}, u32[]{:S(2)}) copy-start(pred[2,128,1280]{2,1,0:T(8,128)(4,1)S(1)} %compare_and_fusion) | copy-start | bytes 983044
  50.5 21.7 %collective-permute-start.1 = (bf16[512,512]{0,1:T(8,128)(2,1)S(1)}, bf16[512,512]{0,1:T(8,128)(2,1)S(1)}, u32[]{:S(2)}, u32[]{:S(2)}) collective-permute-start(bf16[512,512]{0,1:T(8,128)(2,1)S(1)} %pad_maximum_fusion.2), channel_id=1, source_target_pairs={{0,2},{1,3},{2,4},{3,5},{4,6},{5,7},{6,8},{7,9},{8,10},{9,11},{10,... | collective-permute-start | bytes 1572872 | tf_op jit(solution)/shard_map/ppermute | solution.py:22
  73.3 1.1 copy-start.6
  147.7 8.2 %copy-start.2 = (bf16[2,4096,512]{2,1,0:T(8,128)(2,1)}, bf16[2,4096,512]{2,1,0:T(8,128)(2,1)S(1)}, u32[]{:S(2)}) copy-start(bf16[2,4096,512]{2,1,0:T(8,128)(2,1)S(1)} %bitcast_select_fusion) | copy-start | bytes 25165828
  164.0 8.4 %copy-start.9 = (pred[2,128,1280]{2,1,0:T(8,128)(4,1)S(1)}, pred[2,128,1280]{2,1,0:T(8,128)(4,1)}, u32[]{:S(2)}) copy-start(pred[2,128,1280]{2,1,0:T(8,128)(4,1)} %copy-done.8) | copy-start | bytes 983044
  172.4 4.0 %copy-start.7 = (bf16[1280,512]{0,1:T(8,128)(2,1)S(1)}, bf16[1280,512]{0,1:T(8,128)(2,1)}, u32[]{:S(2)}) copy-start(bf16[1280,512]{0,1:T(8,128)(2,1)} %copy-done.6) | copy-start | bytes 3932164
  176.5 4.7 %copy-start.5 = (bf16[1024,2048]{1,0:T(8,128)(2,1)S(1)}, bf16[1024,2048]{1,0:T(8,128)(2,1)}, u32[]{:S(2)}) copy-start(bf16[1024,2048]{1,0:T(8,128)(2,1)} %param.25) | copy-start | bytes 12582916
  181.2 3.9 %copy-start.11 = (bf16[2,65536]{1,0:T(2,128)(2,1)S(1)}, bf16[2,65536]{1,0:T(2,128)(2,1)}, u32[]{:S(2)}) copy-start(bf16[2,65536]{1,0:T(2,128)(2,1)} %convolution_convert_fusion) | copy-start | bytes 786436
  181.2 5.6 %copy-start.12 = (bf16[64,2048]{1,0:T(8,128)(2,1)S(1)}, bf16[64,2048]{1,0:T(8,128)(2,1)}, u32[]{:S(2)}) copy-start(bf16[64,2048]{1,0:T(8,128)(2,1)} %param.28) | copy-start | bytes 786436
  184.2 6.3 %collective-permute-start.3 = (bf16[256,2048]{1,0:T(8,128)(2,1)}, bf16[256,2048]{1,0:T(8,128)(2,1)}, u32[]{:S(2)}, u32[]{:S(2)}) collective-permute-start(bf16[256,2048]{1,0:T(8,128)(2,1)} %get-tuple-element.56), channel_id=1, source_target_pairs={{0,64},{64,0},{1,65},{65,1},{2,66},{66,2},{3,67},{67,3},{4,68},{68... | collective-permute-start | bytes 3145736 | tf_op jit(solution)/shard_map/ppermute | solution.py:243
  186.7 6.1 %copy-start.3 = (bf16[256,2048]{1,0:T(8,128)(2,1)S(1)}, bf16[256,2048]{1,0:T(8,128)(2,1)}, u32[]{:S(2)}) copy-start(bf16[256,2048]{1,0:T(8,128)(2,1)} %param.18) | copy-start | bytes 3145732
  186.7 6.1 %dynamic-slice-start = ((f32[2048]{0:T(1024)}, s32[]{:T(128)}), f32[1024]{0:T(1024)S(1)}, s32[]{:S(2)}) async-start(f32[2048]{0:T(1024)} %param.26, s32[]{:T(128)} %select_n.100), calls=%async_computation.1 | async-start | bytes 8704 | tf_op jit(solution)/shard_map/dynamic_slice | solution.py:241
  186.7 6.1 %dynamic-slice-start.1 = ((f32[2048]{0:T(1024)}, s32[]{:T(128)}), f32[1024]{0:T(1024)S(1)}, s32[]{:S(2)}) async-start(f32[2048]{0:T(1024)} %param.29, s32[]{:T(128)} %select_n.100), calls=%async_computation.2 | async-start | bytes 8704 | tf_op jit(solution)/shard_map/dynamic_slice | solution.py:241
  190.4 2.5 %copy-start.4 = (f32[256,2048]{1,0:T(8,128)S(1)}, f32[256,2048]{1,0:T(8,128)}, u32[]{:S(2)}) copy-start(f32[256,2048]{1,0:T(8,128)} %get-tuple-element.59) | copy-start | bytes 6291460
  190.5 3.8 %copy-start.1 = (bf16[2048,256]{1,0:T(8,128)(2,1)S(1)}, bf16[2048,256]{1,0:T(8,128)(2,1)}, u32[]{:S(2)}) copy-start(bf16[2048,256]{1,0:T(8,128)(2,1)} %param.21) | copy-start | bytes 3145732
Sparse Core Ops, SparseCore 0:
  10.9 120.9 all-gather.1
where the time goes:
time: 202 us; the launch traced here: 201 us
  waiting for transfers between devices  71.3 us (35%)
  other arithmetic  46.4 us (23%)
  matrix products  35.8 us (18%)
  local copies, waits for them, and re-layouts  19.9 us (10%)
  between operations  14.5 us (7%)
  starting transfers between devices  13.1 us (6%)
    all_gather x1, waiting for transfers between devices, local(): every_slot = lax.all_gather(prefix_both, 'page', axis=0, tiled=True)  54.2 us
    ppermute x3, waiting for transfers between devices, passed_along(): return lax.ppermute(block, axis, route)  17.1 us
    ppermute x3, starting transfers between devices, passed_along(): return lax.ppermute(block, axis, route)  12.2 us
    gather x1, local copies, waits for them, and re-layouts, local(): jnp.take(slot_pages, chosen.reshape(-1), axis=0)  11.2 us
    dot_general x1, matrix products, local(): jnp.einsum('pqhk,pkd->pqhd', prefix_weights.astype(jnp.bfloat16), prefix_...  8.37 us
    reduce_sum x1, other arithmetic, local(): jnp.sum(prefix_weights, axis=-1) + jnp.sum(suffix_weights, axis=-1)  8.09 us
    dot_general x1, matrix products, local(): jnp.einsum('pqhd,pkd->pqhk', page_queries, prefix_keys, preferred_element...  7.46 us
    unnamed x9, other arithmetic  5.95 us
  transfers between devices with their start and end apart: 5, of which 2 were waited for; matrix products, arithmetic and copies ran while one was open for 22% of the time, Pallas kernels for 0%

commit v1 on v0

--- a/solution.py
+++ b/solution.py
@@ -2,6 +2,8 @@
 import jax.numpy as jnp
 from jax import lax
 from jax.sharding import PartitionSpec as P
+from jax.experimental import pallas as pl
+from jax.experimental.pallas import tpu as pltpu
 
 HEAD_SIZE = 256
 PAGE_TOKENS = 128
@@ -113,6 +115,110 @@
     row_total = carried[1] * old_factor + incoming[1] * new_factor
     mixture = carried[2] * old_factor[..., None] + incoming[2] * new_factor[..., None]
     return (row_top, row_total, mixture)
+
+
+PAGES_PER_STEP = 8
+
+
+def page_attention_kernel(
+    table_ref, q_ref, row_req_ref, row_pos_ref, key_req_ref, key_pos_ref,
+    suffix_keys_ref, suffix_values_ref, *rest,
+):
+    slot_refs = rest[:PAGES_PER_STEP]
+    out_ref = rest[PAGES_PER_STEP]
+    scores_buf, values_buf = rest[PAGES_PER_STEP + 1 :]
+    step = pl.program_id(1)
+    last = pl.num_programs(1) - 1
+    contract_last = (((1,), (1,)), ((), ()))
+
+    @pl.when(step < last)
+    def _():
+        q = q_ref[0]
+        for i in range(PAGES_PER_STEP):
+            page = slot_refs[i][0]
+            at = pl.multiple_of((step * PAGES_PER_STEP + i) * PAGE_TOKENS, PAGE_TOKENS)
+            scores_buf[:, pl.ds(at, PAGE_TOKENS)] = lax.dot_general(
+                q, page[:, :HEAD_SIZE], contract_last, preferred_element_type=jnp.float32
+            )
+            values_buf[pl.ds(at, PAGE_TOKENS), :] = page[:, HEAD_SIZE:]
+
+    @pl.when(step == last)
+    def _():
+        rows = q_ref.shape[1]
+        chunk = 128
+        for r in range(0, rows, chunk):
+            q = q_ref[0, r : r + chunk, :]
+            mask = (row_req_ref[0, r : r + chunk, :] == key_req_ref[...]) & (
+                key_pos_ref[...] <= row_pos_ref[0, r : r + chunk, :]
+            )
+            suffix_scores = lax.dot_general(
+                q, suffix_keys_ref[...], contract_last, preferred_element_type=jnp.float32
+            )
+            suffix_scores = jnp.where(mask, suffix_scores, masked_low)
+            prefix_scores = scores_buf[r : r + chunk, :]
+            row_top = jnp.maximum(
+                jnp.max(prefix_scores, axis=1, keepdims=True),
+                jnp.max(suffix_scores, axis=1, keepdims=True),
+            )
+            prefix_weights = jnp.exp(prefix_scores - row_top)
+            suffix_weights = jnp.where(mask, jnp.exp(suffix_scores - row_top), 0.0)
+            row_total = jnp.sum(prefix_weights, axis=1, keepdims=True) + jnp.sum(
+                suffix_weights, axis=1, keepdims=True
+            )
+            mixture = jnp.dot(
+                prefix_weights.astype(jnp.bfloat16), values_buf[...],
+                preferred_element_type=jnp.float32,
+            ) + jnp.dot(
+                suffix_weights.astype(jnp.bfloat16), suffix_values_ref[...],
+                preferred_element_type=jnp.float32,
+            )
+            out_ref[0, r : r + chunk, :] = (mixture / row_total).astype(out_ref.dtype)
+
+
+def page_attention(table, q, row_req, row_pos, key_req, key_pos, suffix_keys, suffix_values, slot_pages):
+    pages, rows, _ = q.shape
+    steps = PREFIX_PAGES // PAGES_PER_STEP
+    suffix_rows = suffix_keys.shape[0]
+
+    def slot_spec(i):
+        return pl.BlockSpec(
+            (1, PAGE_TOKENS, 2 * HEAD_SIZE),
+            lambda p, j, t, i=i: (t[p, jnp.minimum(j * PAGES_PER_STEP + i, PREFIX_PAGES - 1)], 0, 0),
+        )
+
+    grid_spec = pltpu.PrefetchScalarGridSpec(
+        num_scalar_prefetch=1,
+        grid=(pages, steps + 1),
+        in_specs=[
+            pl.BlockSpec((1, rows, HEAD_SIZE), lambda p, j, t: (p, 0, 0)),
+            pl.BlockSpec((1, rows, 1), lambda p, j, t: (p, 0, 0)),
+            pl.BlockSpec((1, rows, 1), lambda p, j, t: (p, 0, 0)),
+            pl.BlockSpec((1, suffix_rows), lambda p, j, t: (0, 0)),
+            pl.BlockSpec((1, suffix_rows), lambda p, j, t: (0, 0)),
+            pl.BlockSpec((suffix_rows, HEAD_SIZE), lambda p, j, t: (0, 0)),
+            pl.BlockSpec((suffix_rows, HEAD_SIZE), lambda p, j, t: (0, 0)),
+        ]
+        + [slot_spec(i) for i in range(PAGES_PER_STEP)],
+        out_specs=pl.BlockSpec((1, rows, HEAD_SIZE), lambda p, j, t: (p, 0, 0)),
+        scratch_shapes=[
+            pltpu.VMEM((rows, PREFIX_PAGES * PAGE_TOKENS), jnp.float32),
+            pltpu.VMEM((PREFIX_PAGES * PAGE_TOKENS, HEAD_SIZE), jnp.bfloat16),
+        ],
+    )
+    keys_total = PREFIX_PAGES * PAGE_TOKENS + suffix_rows
+    flops = pages * rows * keys_total * HEAD_SIZE * 4
+    bytes_accessed = pages * (PREFIX_PAGES * PAGE_TOKENS * 2 * HEAD_SIZE * 2 + rows * HEAD_SIZE * 4)
+    return pl.pallas_call(
+        page_attention_kernel,
+        grid_spec=grid_spec,
+        out_shape=jax.ShapeDtypeStruct((pages, rows, HEAD_SIZE), jnp.bfloat16),
+        compiler_params=pltpu.CompilerParams(
+            dimension_semantics=("arbitrary", "arbitrary"), vmem_limit_bytes=48 * 1024 * 1024
+        ),
+        cost_estimate=pl.CostEstimate(
+            flops=flops, transcendentals=pages * rows * keys_total, bytes_accessed=bytes_accessed
+        ),
+    )(table, q, row_req, row_pos, key_req, key_pos, suffix_keys, suffix_values, *([slot_pages] * PAGES_PER_STEP))
 
 
 def local(
@@ -198,40 +304,18 @@
         prefix_slot_map.reshape(PREFIX_COUNT, PREFIX_PAGES), page_groups, axis=0
     )
     slot_pages = every_slot.reshape(-1, PAGE_TOKENS, 2 * HEAD_SIZE)
-    group_rows = jnp.take(slot_pages, chosen.reshape(-1), axis=0).reshape(
-        pages_here, PREFIX_PAGES * PAGE_TOKENS, 2 * HEAD_SIZE
-    )
-    prefix_keys = group_rows[..., :HEAD_SIZE]
-    prefix_values = group_rows[..., HEAD_SIZE:]
-    prefix_scores = jnp.einsum(
-        "pqhd,pkd->pqhk", page_queries, prefix_keys, preferred_element_type=jnp.float32
-    )
-    suffix_scores = jnp.einsum(
-        "pqhd,kd->pqhk", page_queries, suffix_keys, preferred_element_type=jnp.float32
-    )
-    suffix_mask = (page_requests[:, :, None] == key_requests[None, None, :]) & (
-        key_positions[None, None, :] <= page_positions[:, :, None]
-    )
-    suffix_mask = suffix_mask[:, :, None, :]
-    suffix_scores = jnp.where(suffix_mask, suffix_scores, masked_low)
-    row_top = jnp.maximum(
-        jnp.max(prefix_scores, axis=-1), jnp.max(suffix_scores, axis=-1)
-    )[..., None]
-    prefix_weights = jnp.exp(prefix_scores - row_top)
-    suffix_weights = jnp.where(suffix_mask, jnp.exp(suffix_scores - row_top), 0.0)
-    row_total = jnp.sum(prefix_weights, axis=-1) + jnp.sum(suffix_weights, axis=-1)
-    mixture = jnp.einsum(
-        "pqhk,pkd->pqhd",
-        prefix_weights.astype(jnp.bfloat16),
-        prefix_values,
-        preferred_element_type=jnp.float32,
-    ) + jnp.einsum(
-        "pqhk,kd->pqhd",
-        suffix_weights.astype(jnp.bfloat16),
+    heads_rows = PAGE_TOKENS * heads
+    attended = page_attention(
+        chosen,
+        page_queries.reshape(pages_here, heads_rows, HEAD_SIZE),
+        jnp.repeat(page_requests, heads, axis=1)[..., None],
+        jnp.repeat(page_positions, heads, axis=1)[..., None],
+        key_requests[None, :],
+        key_positions[None, :],
+        suffix_keys,
         suffix_values,
-        preferred_element_type=jnp.float32,
-    )
-    attended = (mixture / row_total[..., None]).astype(jnp.bfloat16).reshape(tok_count, -1)
+        slot_pages,
+    ).reshape(tok_count, -1)
     attn_part = jnp.dot(attended, w_out, preferred_element_type=jnp.float32)
     kv_index = lax.axis_index("kv")
     model_width = tokens.shape[1]

time: 202 us -> 171 us (0.85)
  other arithmetic: 46.4 us -> 17 us
  Pallas kernels: 0 us -> 21 us
  matrix products: 35.8 us -> 14.8 us
  local copies, waits for them, and re-layouts: 19.9 us -> 9.2 us
  waiting for transfers between devices: 71.3 us -> 80.7 us
    dot_general x4 -> x0, matrix products: 23.3 us -> none  [the longest x1 8.37 us: local(): jnp.einsum('pqhk,pkd->pqhd', prefix_weights.astype(jnp.bfloat16), prefix_...]
    pallas_call x0 -> x1, Pallas kernels: none -> 21 us  [page_attention(): pl.pallas_call(page_attention_kernel, grid_spec=grid_spec, out_shape=jax....]
    all_gather x1, waiting for transfers between devices: 54.2 us -> 70.8 us  [local(): every_slot = lax.all_gather(prefix_both, 'page', axis=0, tiled=True)]
    reduce_sum x3 -> x1, other arithmetic: 13.6 us -> 0.18 us  [token_places(): jnp.sum(belongs * page_starts[None, :], axis=1) * PAGE_TOKENS]
    gather x1 -> x0, local copies, waits for them, and re-layouts: 11.2 us -> none  [local(): jnp.take(slot_pages, chosen.reshape(-1), axis=0)]
    ppermute x3, waiting for transfers between devices: 17.1 us -> 9.82 us  [passed_along(): return lax.ppermute(block, axis, route)]
    unnamed x9 -> x10, other arithmetic: 5.95 us -> 0.06 us
    select_n x2 -> x0, other arithmetic: 4.67 us -> none  [local(): jnp.take(slot_pages, chosen.reshape(-1), axis=0)]
  transfers between devices with their start and end apart: 5 -> 5, of which waited for: 2 -> 2; matrix products, arithmetic and copies ran while one was open for 22% -> 16% of each run, Pallas kernels for 0% -> 0%
where the time goes in v1:
time: 171 us; the launch traced here: 170 us
  waiting for transfers between devices  80.7 us (47%)
  Pallas kernels  21 us (12%)
  other arithmetic  17 us (10%)
  matrix products  14.8 us (9%)
  between operations  14.5 us (8%)
  starting transfers between devices  13.3 us (8%)
  local copies, waits for them, and re-layouts  9.2 us (5%)
    all_gather x1, waiting for transfers between devices, local(): every_slot = lax.all_gather(prefix_both, 'page', axis=0, tiled=True)  70.8 us
    pallas_call x1, Pallas kernels, page_attention(): pl.pallas_call(page_attention_kernel, grid_spec=grid_spec, out_shape=jax....  21 us
    ppermute x3, starting transfers between devices, passed_along(): return lax.ppermute(block, axis, route)  12.4 us
    ppermute x3, waiting for transfers between devices, passed_along(): return lax.ppermute(block, axis, route)  9.82 us
    dot_general x1, matrix products, local(): attn_part = jnp.dot(attended, w_out, preferred_element_type=jnp.float32)  5.26 us
    reduce_sum x3, other arithmetic, rms_scale(): jnp.mean(values * values, axis=-1, keepdims=True) + epsilon  3.96 us
    dot_general x1, matrix products, local(): jnp.dot(low_rank, laurel_right, preferred_element_type=jnp.float32)  3.7 us
    dot_general x1, matrix products, project(): jnp.dot(normed, w_query, preferred_element_type=jnp.float32)  3.43 us
  transfers between devices with their start and end apart: 5, of which 2 were waited for; matrix products, arithmetic and copies ran while one was open for 16% of the time, Pallas kernels for 0%

profile of v1, /device:TPU:1, one launch (start us, length us, event | category | flops | bytes accessed | tf_op | source)
XLA Modules:
  0.0 170.5 jit_solution(13757507941842655642)
XLA Ops:
  7.2 1.8 %pad_maximum_fusion.4 = bf16[256,512]{1,0:T(8,128)(2,1)} fusion(bf16[256,256]{1,0:T(8,128)(2,1)} %param.31, bf16[256,256]{1,0:T(8,128)(2,1)} %param.30), kind=kLoop, calls=%fused_computation.21 | loop fusion | flops 524288 | bytes 524288 | tf_op jit(solution)/shard_map/concatenate | solution.py:248
  9.1 0.7 copy.45
  9.9 0.1 reduce.4
  10.0 0.7 sub.118
  10.7 1.5 fusion
  12.2 1.0 fusion.2
  13.3 0.5 multiply_reduce_fusion.4
  13.8 0.8 copy.48
  14.7 0.2 copy-done.8
  14.9 0.5 multiply_reduce_fusion.3
  15.4 0.1 copy.49
  15.7 0.2 select_reduce_fusion
  15.9 1.1 multiply_bitcast_fusion
  16.9 0.6 fusion.10
  17.6 0.7 pad_maximum_fusion.3
  18.4 4.6 %collective-permute-start = (bf16[256,512]{1,0:T(8,128)(2,1)}, bf16[256,512]{1,0:T(8,128)(2,1)}, u32[]{:S(2)}, u32[]{:S(2)}) collective-permute-start(bf16[256,512]{1,0:T(8,128)(2,1)} %pad_maximum_fusion.3), channel_id=1, source_target_pairs={{0,1},{1,2},{2,3},{3,4},{4,5},{5,6},{6,7},{7,8},{8,9},{9,10},{10,1... | collective-permute-start | bytes 786440 | tf_op jit(solution)/shard_map/ppermute | solution.py:24
  23.0 3.2 %collective-permute-start.2 = (bf16[256,512]{1,0:T(8,128)(2,1)}, bf16[256,512]{1,0:T(8,128)(2,1)}, u32[]{:S(2)}, u32[]{:S(2)}) collective-permute-start(bf16[256,512]{1,0:T(8,128)(2,1)} %pad_maximum_fusion.3), channel_id=1, source_target_pairs={{0,4},{1,5},{2,6},{3,7},{4,8},{5,9},{6,10},{7,11},{8,12},{9,13},{1... | collective-permute-start | bytes 786440 | tf_op jit(solution)/shard_map/ppermute | solution.py:24
  26.2 3.4 %fusion.28 = f32[256,1024]{1,0:T(8,128)S(1)} fusion(bf16[256,2048]{1,0:T(8,128)(2,1)S(1)} %fusion.2, bf16[2048,1024]{1,0:T(8,128)(2,1)} %param.20), kind=kOutput, calls=%fused_computation.127 | convolution fusion | flops 1073741824 | bytes 6291456 | tf_op jit(solution)/shard_map/dot_general | solution.py:58
  29.7 0.5 reshape.391
  30.2 0.1 copy-done.13
  30.5 0.6 gather_fusion
  31.1 0.1 and_reduce_fusion
  31.2 0.3 multiply_reduce_fusion.2
  31.8 0.5 multiply_cosine_fusion.1
  32.3 0.4 multiply_multiply_fusion
  32.7 0.3 subtract_convert_fusion
  33.0 0.9 pad_maximum_fusion.1.q_ref
  33.8 1.8 %pad_maximum_fusion.2 = bf16[512,512]{1,0:T(8,128)(2,1)} fusion(bf16[256,512]{1,0:T(8,128)(2,1)} %collective-permute-done, bf16[256,256]{1,0:T(8,128)(2,1)S(1)} %multiply_convert_fusion.1, bf16[256,128]{1,0:T(8,128)(2,1)S(1)} %bitcast.38, bf16[256,128]{1,0:T(8,128)(2,1)S(1)} %bitcast.35), kind=kLoop, calls=%fused_computation.17 | loop fusion | flops 2097152 | bytes 1048576 | tf_op jit(solution)/shard_map/concatenate | solution.py:283
  35.7 4.6 %collective-permute-start.1 = (bf16[512,512]{1,0:T(8,128)(2,1)}, bf16[512,512]{1,0:T(8,128)(2,1)S(1)}, u32[]{:S(2)}, u32[]{:S(2)}) collective-permute-start(bf16[512,512]{1,0:T(8,128)(2,1)} %pad_maximum_fusion.2), channel_id=1, source_target_pairs={{0,2},{1,3},{2,4},{3,5},{4,6},{5,7},{6,8},{7,9},{8,10},{9,11},{10,... | collective-permute-start | bytes 1572872 | tf_op jit(solution)/shard_map/ppermute | solution.py:24
  40.4 0.2 broadcast_in_dim_reshape.8.row_req_ref
  40.7 0.2 broadcast_in_dim_reshape.9.row_pos_ref
  40.9 1.3 convolution_convert_fusion
  42.3 9.8 %collective-permute-done.1 = bf16[512,512]{1,0:T(8,128)(2,1)S(1)} collective-permute-done((bf16[512,512]{1,0:T(8,128)(2,1)}, bf16[512,512]{1,0:T(8,128)(2,1)S(1)}, u32[]{:S(2)}, u32[]{:S(2)}) %collective-permute-start.1) | collective-permute-done | bytes 524320 | tf_op jit(solution)/shard_map/ppermute | solution.py:24
  52.1 1.1 pad_maximum_fusion
  53.3 70.8 %all-gather.2.cloned.1.call-done = bf16[16384,512]{1,0:T(8,128)(2,1)} async-done(((bf16[256,512]{1,0:T(8,128)(2,1)}), bf16[16384,512]{1,0:T(8,128)(2,1)}) %all-gather.2.cloned.1.call-update) | async-done | bytes 16777232 | tf_op jit(solution)/shard_map/all_gather | solution.py:249
  124.1 1.0 copy-done.1
  125.2 21.0 %shard_map.193 = bf16[2,512,256]{2,1,0:T(8,128)(2,1)S(1)} custom-call(s32[2,32]{1,0:T(2,128)S(1)} %broadcast_select_fusion.table_ref, bf16[2,512,256]{2,1,0:T(8,128)(2,1)S(1)} %copy-done.1, s32[2,512,1]{2,1,0:T(8,128)S(1)} %broadcast_in_dim_reshape.8.row_req_ref, s32[2,512,1]{2,1,0:T(8,128)S(1)} %broadcast_in_dim_reshape.9.row_pos_ref, ...), custom_call_target="tpu_custom_call" | custom-call | flops 5637144576 | bytes 9437184 | tf_op jit(solution)/shard_map/pallas_call | solution.py:211
  146.2 0.8 copy-done.2
  146.9 1.4 reshape.393
  148.3 5.3 %fusion.27 = (bf16[256,2048]{1,0:T(8,128)(2,1)}, f32[256,2048]{1,0:T(8,128)}) fusion(bf16[256,1024]{1,0:T(8,128)(2,1)S(1)} %reshape.393, bf16[1024,2048]{1,0:T(8,128)(2,1)} %param.25), kind=kOutput, calls=%fused_computation.126 | convolution fusion | flops 1074266112 | bytes 7864320 | tf_op jit(solution)/shard_map/dot_general | solution.py:319
  153.6 0.8 collective-permute-start.3
  154.4 0.2 fusion.26
  154.6 0.7 reshape.394
  155.4 0.7 reshape.395
  156.1 3.7 %multiply_reduce_fusion = (f32[256]{0:T(256)S(1)}, f32[256,2048]{1,0:T(8,128)}) fusion(bf16[64,2048]{1,0:T(8,128)(2,1)} %param.28, bf16[256,2048]{1,0:T(8,128)(2,1)S(1)} %copy-done.4, bf16[2048,64]{0,1:T(8,128)(2,1)} %param.27), kind=kOutput, calls=%fused_computation.7 | convolution fusion | flops 135282432 | bytes 3671040 | tf_op jit(solution)/shard_map/dot_general | solution.py:330
  159.9 2.1 %multiply_reduce_fusion.1 = (f32[256]{0:T(256)S(1)}, f32[256,2048]{1,0:T(8,128)S(1)}) fusion(f32[256,2048]{1,0:T(8,128)} %get-tuple-element.53, bf16[256,2048]{1,0:T(8,128)(2,1)S(1)} %collective-permute-done.3), kind=kLoop, calls=%fused_computation.8 | loop fusion | flops 2096896 | bytes 5243904 | tf_op jit(solution)/shard_map/reduce_sum | solution.py:28
  162.0 0.4 copy-done.7
  162.4 1.2 multiply_convert_fusion
  (75 shorter events, 1.2 us)
Async XLA Ops:
  7.2 6.1 %copy-start = (bf16[2048,256]{1,0:T(8,128)(2,1)S(1)}, bf16[2048,256]{1,0:T(8,128)(2,1)}, u32[]{:S(2)}) copy-start(bf16[2048,256]{1,0:T(8,128)(2,1)} %param.21) | copy-start | bytes 3145732
  7.2 5.0 %copy-start.5 = (bf16[256,2048]{1,0:T(8,128)(2,1)S(1)}, bf16[256,2048]{1,0:T(8,128)(2,1)}, u32[]{:S(2)}) copy-start(bf16[256,2048]{1,0:T(8,128)(2,1)} %param.18) | copy-start | bytes 3145732
  7.2 116.9 %all-gather.2.cloned.1.call-start = ((), (), s32[]{:S(2)}) async-start(), calls=%async_computation | async-start | bytes 17039360 | tf_op jit(solution)/shard_map/all_gather | solution.py:249
  13.2 13.0 %copy-start.3 = (bf16[256,2048]{1,0:T(8,128)(2,1)}, bf16[256,2048]{1,0:T(8,128)(2,1)S(1)}, u32[]{:S(2)}) copy-start(bf16[256,2048]{1,0:T(8,128)(2,1)S(1)} %fusion.2) | copy-start | bytes 3145732
  13.3 1.6 copy-start.8
  13.8 1.8 %copy-start.12 = (s32[32]{0:T(128)S(1)}, s32[32]{0:T(128)}, u32[]{:S(2)}) copy-start(s32[32]{0:T(128)} %param.34) | copy-start | bytes 388
  13.8 2.1 %copy-start.10 = (f32[256]{0:T(256)S(1)}, f32[256]{0:T(256)}, u32[]{:S(2)}) copy-start(f32[256]{0:T(256)} %param.24) | copy-start | bytes 3076
  18.4 15.5 %collective-permute-start = (bf16[256,512]{1,0:T(8,128)(2,1)}, bf16[256,512]{1,0:T(8,128)(2,1)}, u32[]{:S(2)}, u32[]{:S(2)}) collective-permute-start(bf16[256,512]{1,0:T(8,128)(2,1)} %pad_maximum_fusion.3), channel_id=1, source_target_pairs={{0,1},{1,2},{2,3},{3,4},{4,5},{5,6},{6,7},{7,8},{8,9},{9,10},{10,1... | collective-permute-start | bytes 786440 | tf_op jit(solution)/shard_map/ppermute | solution.py:24
  23.0 19.3 %collective-permute-start.2 = (bf16[256,512]{1,0:T(8,128)(2,1)}, bf16[256,512]{1,0:T(8,128)(2,1)}, u32[]{:S(2)}, u32[]{:S(2)}) collective-permute-start(bf16[256,512]{1,0:T(8,128)(2,1)} %pad_maximum_fusion.3), channel_id=1, source_target_pairs={{0,4},{1,5},{2,6},{3,7},{4,8},{5,9},{6,10},{7,11},{8,12},{9,13},{1... | collective-permute-start | bytes 786440 | tf_op jit(solution)/shard_map/ppermute | solution.py:24
  29.7 0.7 copy-start.13
  29.7 2.6 %copy-start.11 = (f32[256]{0:T(256)S(1)}, f32[256]{0:T(256)}, u32[]{:S(2)}) copy-start(f32[256]{0:T(256)} %param.23) | copy-start | bytes 3076
  32.7 7.5 %copy-start.14 = (s32[2]{0:T(128)S(1)}, s32[2]{0:T(128)}, u32[]{:S(2)}) copy-start(s32[2]{0:T(128)} %param.35) | copy-start | bytes 28
  35.7 16.4 %collective-permute-start.1 = (bf16[512,512]{1,0:T(8,128)(2,1)}, bf16[512,512]{1,0:T(8,128)(2,1)S(1)}, u32[]{:S(2)}, u32[]{:S(2)}) collective-permute-start(bf16[512,512]{1,0:T(8,128)(2,1)} %pad_maximum_fusion.2), channel_id=1, source_target_pairs={{0,2},{1,3},{2,4},{3,5},{4,6},{5,7},{6,8},{7,9},{8,10},{9,11},{10,... | collective-permute-start | bytes 1572872 | tf_op jit(solution)/shard_map/ppermute | solution.py:24
  124.1 1.0 copy-start.1
  146.1 0.8 copy-start.2
  148.3 6.1 %copy-start.9 = (bf16[2,65536]{1,0:T(2,128)(2,1)S(1)}, bf16[2,65536]{1,0:T(2,128)(2,1)}, u32[]{:S(2)}) copy-start(bf16[2,65536]{1,0:T(2,128)(2,1)} %convolution_convert_fusion) | copy-start | bytes 786436
  148.3 7.8 %copy-start.4 = (bf16[256,2048]{1,0:T(8,128)(2,1)S(1)}, bf16[256,2048]{1,0:T(8,128)(2,1)}, u32[]{:S(2)}) copy-start(bf16[256,2048]{1,0:T(8,128)(2,1)} %copy-done.3) | copy-start | bytes 3145732
  153.6 6.2 %collective-permute-start.3 = (bf16[256,2048]{1,0:T(8,128)(2,1)}, bf16[256,2048]{1,0:T(8,128)(2,1)S(1)}, u32[]{:S(2)}, u32[]{:S(2)}) collective-permute-start(bf16[256,2048]{1,0:T(8,128)(2,1)} %get-tuple-element.52), channel_id=1, source_target_pairs={{0,64},{64,0},{1,65},{65,1},{2,66},{66,2},{3,67},{67,3},{4,68},{68... | collective-permute-start | bytes 3145736 | tf_op jit(solution)/shard_map/ppermute | solution.py:327
  159.8 2.2 %copy-start.6 = (bf16[256,2048]{1,0:T(8,128)(2,1)S(1)}, bf16[256,2048]{1,0:T(8,128)(2,1)}, u32[]{:S(2)}) copy-start(bf16[256,2048]{1,0:T(8,128)(2,1)} %param.18) | copy-start | bytes 3145732
  159.8 2.5 %copy-start.7 = (f32[256,2048]{1,0:T(8,128)S(1)}, f32[256,2048]{1,0:T(8,128)}, u32[]{:S(2)}) copy-start(f32[256,2048]{1,0:T(8,128)} %get-tuple-element.55) | copy-start | bytes 6291460
  159.8 2.5 %dynamic-slice-start = ((f32[2048]{0:T(1024)}, s32[]{:T(128)}), f32[1024]{0:T(1024)S(1)}, s32[]{:S(2)}) async-start(f32[2048]{0:T(1024)} %param.26, s32[]{:T(128)} %select_n.57), calls=%async_computation.1 | async-start | bytes 8704 | tf_op jit(solution)/shard_map/dynamic_slice | solution.py:325
  159.8 2.5 %dynamic-slice-start.1 = ((f32[2048]{0:T(1024)}, s32[]{:T(128)}), f32[1024]{0:T(1024)S(1)}, s32[]{:S(2)}) async-start(f32[2048]{0:T(1024)} %param.29, s32[]{:T(128)} %select_n.57), calls=%async_computation.2 | async-start | bytes 8704 | tf_op jit(solution)/shard_map/dynamic_slice | solution.py:325
Sparse Core Ops, SparseCore 0:
  10.9 113.1 all-gather.1

commit v2 on v1

--- a/solution.py
+++ b/solution.py
@@ -122,46 +122,50 @@
 
 def page_attention_kernel(
     table_ref, q_ref, row_req_ref, row_pos_ref, key_req_ref, key_pos_ref,
-    suffix_keys_ref, suffix_values_ref, *rest,
+    suffix_keys_ref, suffix_values_ref, w_out_ref, *rest,
 ):
     slot_refs = rest[:PAGES_PER_STEP]
-    out_ref = rest[PAGES_PER_STEP]
-    scores_buf, values_buf = rest[PAGES_PER_STEP + 1 :]
+    out_ref, out_low_ref = rest[PAGES_PER_STEP : PAGES_PER_STEP + 2]
+    scores_buf, values_buf, suffix_buf, top_buf = rest[PAGES_PER_STEP + 2 :]
     step = pl.program_id(1)
     last = pl.num_programs(1) - 1
     contract_last = (((1,), (1,)), ((), ()))
 
+    @pl.when(step == 0)
+    def _():
+        mask = (row_req_ref[0] == key_req_ref[...]) & (key_pos_ref[...] <= row_pos_ref[0])
+        suffix_scores = lax.dot_general(
+            q_ref[0], suffix_keys_ref[...], contract_last, preferred_element_type=jnp.float32
+        )
+        suffix_scores = jnp.where(mask, suffix_scores, masked_low)
+        suffix_buf[...] = suffix_scores
+        top_buf[...] = jnp.max(suffix_scores, axis=1, keepdims=True)
+
     @pl.when(step < last)
     def _():
         q = q_ref[0]
+        top = top_buf[...]
         for i in range(PAGES_PER_STEP):
             page = slot_refs[i][0]
             at = pl.multiple_of((step * PAGES_PER_STEP + i) * PAGE_TOKENS, PAGE_TOKENS)
-            scores_buf[:, pl.ds(at, PAGE_TOKENS)] = lax.dot_general(
+            scores = lax.dot_general(
                 q, page[:, :HEAD_SIZE], contract_last, preferred_element_type=jnp.float32
             )
+            scores_buf[:, pl.ds(at, PAGE_TOKENS)] = scores
             values_buf[pl.ds(at, PAGE_TOKENS), :] = page[:, HEAD_SIZE:]
+            top = jnp.maximum(top, jnp.max(scores, axis=1, keepdims=True))
+        top_buf[...] = top
 
     @pl.when(step == last)
     def _():
         rows = q_ref.shape[1]
-        chunk = 128
-        for r in range(0, rows, chunk):
-            q = q_ref[0, r : r + chunk, :]
-            mask = (row_req_ref[0, r : r + chunk, :] == key_req_ref[...]) & (
-                key_pos_ref[...] <= row_pos_ref[0, r : r + chunk, :]
-            )
-            suffix_scores = lax.dot_general(
-                q, suffix_keys_ref[...], contract_last, preferred_element_type=jnp.float32
-            )
-            suffix_scores = jnp.where(mask, suffix_scores, masked_low)
-            prefix_scores = scores_buf[r : r + chunk, :]
-            row_top = jnp.maximum(
-                jnp.max(prefix_scores, axis=1, keepdims=True),
-                jnp.max(suffix_scores, axis=1, keepdims=True),
-            )
-            prefix_weights = jnp.exp(prefix_scores - row_top)
-            suffix_weights = jnp.where(mask, jnp.exp(suffix_scores - row_top), 0.0)
+        heads = rows // PAGE_TOKENS
+        total_out = None
+        for h in range(heads):
+            r = h * PAGE_TOKENS
+            row_top = top_buf[r : r + PAGE_TOKENS, :]
+            prefix_weights = jnp.exp(scores_buf[r : r + PAGE_TOKENS, :] - row_top)
+            suffix_weights = jnp.exp(suffix_buf[r : r + PAGE_TOKENS, :] - row_top)
             row_total = jnp.sum(prefix_weights, axis=1, keepdims=True) + jnp.sum(
                 suffix_weights, axis=1, keepdims=True
             )
@@ -172,13 +176,20 @@
                 suffix_weights.astype(jnp.bfloat16), suffix_values_ref[...],
                 preferred_element_type=jnp.float32,
             )
-            out_ref[0, r : r + chunk, :] = (mixture / row_total).astype(out_ref.dtype)
-
-
-def page_attention(table, q, row_req, row_pos, key_req, key_pos, suffix_keys, suffix_values, slot_pages):
+            attended = (mixture / row_total).astype(jnp.bfloat16)
+            part = jnp.dot(
+                attended, w_out_ref[r * 2 : r * 2 + HEAD_SIZE, :], preferred_element_type=jnp.float32
+            )
+            total_out = part if total_out is None else total_out + part
+        out_ref[0] = total_out
+        out_low_ref[0] = total_out.astype(out_low_ref.dtype)
+
+
+def page_attention(table, q, row_req, row_pos, key_req, key_pos, suffix_keys, suffix_values, w_out, slot_pages):
     pages, rows, _ = q.shape
     steps = PREFIX_PAGES // PAGES_PER_STEP
     suffix_rows = suffix_keys.shape[0]
+    width = w_out.shape[1]
 
     def slot_spec(i):
         return pl.BlockSpec(
@@ -197,28 +208,37 @@
             pl.BlockSpec((1, suffix_rows), lambda p, j, t: (0, 0)),
             pl.BlockSpec((suffix_rows, HEAD_SIZE), lambda p, j, t: (0, 0)),
             pl.BlockSpec((suffix_rows, HEAD_SIZE), lambda p, j, t: (0, 0)),
+            pl.BlockSpec(w_out.shape, lambda p, j, t: (0, 0)),
         ]
         + [slot_spec(i) for i in range(PAGES_PER_STEP)],
-        out_specs=pl.BlockSpec((1, rows, HEAD_SIZE), lambda p, j, t: (p, 0, 0)),
+        out_specs=[
+            pl.BlockSpec((1, PAGE_TOKENS, width), lambda p, j, t: (p, 0, 0)),
+            pl.BlockSpec((1, PAGE_TOKENS, width), lambda p, j, t: (p, 0, 0)),
+        ],
         scratch_shapes=[
             pltpu.VMEM((rows, PREFIX_PAGES * PAGE_TOKENS), jnp.float32),
             pltpu.VMEM((PREFIX_PAGES * PAGE_TOKENS, HEAD_SIZE), jnp.bfloat16),
+            pltpu.VMEM((rows, suffix_rows), jnp.float32),
+            pltpu.VMEM((rows, 1), jnp.float32),
         ],
     )
     keys_total = PREFIX_PAGES * PAGE_TOKENS + suffix_rows
-    flops = pages * rows * keys_total * HEAD_SIZE * 4
-    bytes_accessed = pages * (PREFIX_PAGES * PAGE_TOKENS * 2 * HEAD_SIZE * 2 + rows * HEAD_SIZE * 4)
+    flops = pages * rows * keys_total * HEAD_SIZE * 4 + pages * rows * HEAD_SIZE * width * 2
+    bytes_accessed = pages * (PREFIX_PAGES * PAGE_TOKENS * 2 * HEAD_SIZE * 2 + rows * HEAD_SIZE * 2 + PAGE_TOKENS * width * 6) + w_out.size * 2
     return pl.pallas_call(
         page_attention_kernel,
         grid_spec=grid_spec,
-        out_shape=jax.ShapeDtypeStruct((pages, rows, HEAD_SIZE), jnp.bfloat16),
+        out_shape=(
+            jax.ShapeDtypeStruct((pages, PAGE_TOKENS, width), jnp.float32),
+            jax.ShapeDtypeStruct((pages, PAGE_TOKENS, width), jnp.bfloat16),
+        ),
         compiler_params=pltpu.CompilerParams(
-            dimension_semantics=("arbitrary", "arbitrary"), vmem_limit_bytes=48 * 1024 * 1024
+            dimension_semantics=("arbitrary", "arbitrary"), vmem_limit_bytes=56 * 1024 * 1024
         ),
         cost_estimate=pl.CostEstimate(
             flops=flops, transcendentals=pages * rows * keys_total, bytes_accessed=bytes_accessed
         ),
-    )(table, q, row_req, row_pos, key_req, key_pos, suffix_keys, suffix_values, *([slot_pages] * PAGES_PER_STEP))
+    )(table, q, row_req, row_pos, key_req, key_pos, suffix_keys, suffix_values, w_out, *([slot_pages] * PAGES_PER_STEP))
 
 
 def local(
@@ -305,37 +325,60 @@
     )
     slot_pages = every_slot.reshape(-1, PAGE_TOKENS, 2 * HEAD_SIZE)
     heads_rows = PAGE_TOKENS * heads
-    attended = page_attention(
+    kv_index = lax.axis_index("kv")
+    model_width = tokens.shape[1]
+    half_width = model_width // lax.axis_size("kv")
+
+    def columns(source):
+        return lax.dynamic_slice_in_dim(source, kv_index * half_width, half_width, source.ndim - 1)
+
+    low_rank = jnp.dot(normed, laurel_left, preferred_element_type=jnp.float32).astype(jnp.bfloat16)
+    laurel_full = jnp.dot(low_rank, laurel_right, preferred_element_type=jnp.float32)
+    laurel = columns(normed).astype(jnp.float32) + columns(laurel_full) * rms_scale(
+        laurel_full
+    ) * columns(laurel_gain)
+    resident = columns(tokens).astype(jnp.float32) + laurel
+    head_queries = jnp.swapaxes(page_queries, 1, 2).reshape(pages_here, heads_rows, HEAD_SIZE)
+    row_requests = jnp.tile(page_requests, (1, heads))[..., None]
+    row_positions = jnp.tile(page_positions, (1, heads))[..., None]
+    (
+        resident,
+        suffix_key_cache,
+        suffix_value_cache,
+        head_queries,
+        row_requests,
+        row_positions,
+        suffix_keys,
+        suffix_values,
+    ) = lax.optimization_barrier(
+        (
+            resident,
+            suffix_key_cache,
+            suffix_value_cache,
+            head_queries,
+            row_requests,
+            row_positions,
+            suffix_keys,
+            suffix_values,
+        )
+    )
+    attn_part, attn_low = page_attention(
         chosen,
-        page_queries.reshape(pages_here, heads_rows, HEAD_SIZE),
-        jnp.repeat(page_requests, heads, axis=1)[..., None],
-        jnp.repeat(page_positions, heads, axis=1)[..., None],
+        head_queries,
+        row_requests,
+        row_positions,
         key_requests[None, :],
         key_positions[None, :],
         suffix_keys,
         suffix_values,
+        w_out,
         slot_pages,
-    ).reshape(tok_count, -1)
-    attn_part = jnp.dot(attended, w_out, preferred_element_type=jnp.float32)
-    kv_index = lax.axis_index("kv")
-    model_width = tokens.shape[1]
-    half_width = model_width // lax.axis_size("kv")
-
-    def columns(source):
-        return lax.dynamic_slice_in_dim(source, kv_index * half_width, half_width, source.ndim - 1)
-
-    partner_part = lax.ppermute(attn_part.astype(jnp.bfloat16), "kv", [(0, 1), (1, 0)])
+    )
+    attn_part = attn_part.reshape(tok_count, model_width)
+    partner_part = lax.ppermute(attn_low.reshape(tok_count, model_width), "kv", [(0, 1), (1, 0)])
     summed_out = attn_part + partner_part.astype(jnp.float32)
-    low_rank = jnp.dot(normed, laurel_left, preferred_element_type=jnp.float32).astype(jnp.bfloat16)
-    laurel_full = jnp.dot(low_rank, laurel_right, preferred_element_type=jnp.float32)
-    attn_half = columns(summed_out)
-    attn_branch = attn_half * rms_scale(summed_out) * columns(post_gain)
-    laurel = columns(normed).astype(jnp.float32) + columns(laurel_full) * rms_scale(
-        laurel_full
-    ) * columns(laurel_gain)
-    layer_out = (
-        (columns(tokens).astype(jnp.float32) + attn_branch + laurel) * 2.0 ** (-0.5)
-    ).astype(jnp.bfloat16)
+    attn_branch = columns(summed_out) * rms_scale(summed_out) * columns(post_gain)
+    layer_out = ((resident + attn_branch) * 2.0 ** (-0.5)).astype(jnp.bfloat16)
     return (layer_out, suffix_key_cache, suffix_value_cache)
 
 

time: 171 us -> 174 us (1.018)
  waiting for transfers between devices: 80.7 us -> 48 us
  other arithmetic: 17 us -> 38.6 us
  local copies, waits for them, and re-layouts: 9.2 us -> 19.1 us
  Pallas kernels: 21 us -> 26.7 us
  matrix products: 14.8 us -> 12 us
    all_gather x1, waiting for transfers between devices: 70.8 us -> 32.7 us  [local(): every_slot = lax.all_gather(prefix_both, 'page', axis=0, tiled=True)]
    unnamed x10, other arithmetic: 0.06 us -> 9.12 us
    pallas_call x1, Pallas kernels: 21 us -> 26.7 us  [page_attention(): pl.pallas_call(page_attention_kernel, grid_spec=grid_spec, out_shape=(jax...]
    dot_general x1 -> x0, matrix products: 5.26 us -> none  [local(): attn_part = jnp.dot(attended, w_out, preferred_element_type=jnp.float32)]
    ppermute x3, waiting for transfers between devices: 9.82 us -> 12.8 us  [passed_along(): return lax.ppermute(block, axis, route)]
    unnamed x30 -> x26, local copies, waits for them, and re-layouts: 2.61 us -> 0.06 us
    ppermute x1, waiting for transfers between devices: 0.01 us -> 2.5 us  [local(): lax.ppermute(attn_low.reshape(tok_count, model_width), 'kv', [(0, 1), (1,...]
    add x0 -> x1, other arithmetic: none -> 2.49 us  [local(): resident = columns(tokens).astype(jnp.float32) + laurel]
  transfers between devices with their start and end apart: 5 -> 5, of which waited for: 2 -> 3; matrix products, arithmetic and copies ran while one was open for 16% -> 37% of each run, Pallas kernels for 0% -> 0%
where the time goes in v2:
time: 174 us; the launch traced here: 173 us
  waiting for transfers between devices  48 us (28%)
  other arithmetic  38.6 us (22%)
  Pallas kernels  26.7 us (15%)
  local copies, waits for them, and re-layouts  19.1 us (11%)
  between operations  14.3 us (8%)
  starting transfers between devices  13.9 us (8%)
  matrix products  12 us (7%)
    all_gather x1, waiting for transfers between devices, local(): every_slot = lax.all_gather(prefix_both, 'page', axis=0, tiled=True)  32.7 us
    pallas_call x1, Pallas kernels, page_attention(): pl.pallas_call(page_attention_kernel, grid_spec=grid_spec, out_shape=(jax...  26.7 us
    ppermute x3, starting transfers between devices, passed_along(): return lax.ppermute(block, axis, route)  13 us
    ppermute x3, waiting for transfers between devices, passed_along(): return lax.ppermute(block, axis, route)  12.8 us
    unnamed x10, other arithmetic  9.12 us
    reduce_sum x3, other arithmetic, rms_scale(): jnp.mean(values * values, axis=-1, keepdims=True) + epsilon  5.16 us
    dot_general x1, matrix products, project(): jnp.dot(normed, w_query, preferred_element_type=jnp.float32)  4.42 us
    dot_general x1, matrix products, local(): jnp.dot(low_rank, laurel_right, preferred_element_type=jnp.float32)  3.76 us
  transfers between devices with their start and end apart: 5, of which 3 were waited for; matrix products, arithmetic and copies ran while one was open for 37% of the time, Pallas kernels for 0%

profile of v2, /device:TPU:1, one launch (start us, length us, event | category | flops | bytes accessed | tf_op | source)
XLA Modules:
  0.0 172.7 jit_solution(11683918431118875053)
XLA Ops:
  7.2 1.8 %pad_maximum_fusion.5 = bf16[256,512]{1,0:T(8,128)(2,1)} fusion(bf16[256,256]{1,0:T(8,128)(2,1)} %param.31, bf16[256,256]{1,0:T(8,128)(2,1)} %param.30), kind=kLoop, calls=%fused_computation.25 | loop fusion | flops 524288 | bytes 524288 | tf_op jit(solution)/shard_map/concatenate | solution.py:268
  10.7 1.5 fusion
  12.2 1.0 fusion.2
  13.8 0.8 copy.54
  14.6 1.8 %multiply_reduce_fusion.3 = (f32[256]{0:T(256)S(1)}, f32[256,256]{0,1:T(8,128)S(1)}) fusion(bf16[256,2048]{1,0:T(8,128)(2,1)S(1)} %fusion.2, bf16[2048,256]{1,0:T(8,128)(2,1)} %param.22), kind=kOutput, calls=%fused_computation.27 | convolution fusion | flops 268566272 | bytes 2360320 | tf_op jit(solution)/shard_map/dot_general | solution.py:68
  16.4 0.8 copy.56
  17.3 0.8 select_reduce_fusion
  18.1 1.3 constant_dynamic-update-slice_fusion.9
  19.4 1.0 multiply_bitcast_fusion
  21.1 1.1 multiply_convert_fusion.1
  22.9 4.6 %collective-permute-start = (bf16[256,512]{1,0:T(8,128)(2,1)}, bf16[256,512]{1,0:T(8,128)(2,1)}, u32[]{:S(2)}, u32[]{:S(2)}) collective-permute-start(bf16[256,512]{1,0:T(8,128)(2,1)} %pad_maximum_fusion.4), channel_id=1, source_target_pairs={{0,1},{1,2},{2,3},{3,4},{4,5},{5,6},{6,7},{7,8},{8,9},{9,10},{10,1... | collective-permute-start | bytes 786440 | tf_op jit(solution)/shard_map/ppermute | solution.py:24
  27.5 3.2 %collective-permute-start.2 = (bf16[256,512]{1,0:T(8,128)(2,1)}, bf16[256,512]{1,0:T(8,128)(2,1)}, u32[]{:S(2)}, u32[]{:S(2)}) collective-permute-start(bf16[256,512]{1,0:T(8,128)(2,1)} %pad_maximum_fusion.4), channel_id=1, source_target_pairs={{0,4},{1,5},{2,6},{3,7},{4,8},{5,9},{6,10},{7,11},{8,12},{9,13},{1... | collective-permute-start | bytes 786440 | tf_op jit(solution)/shard_map/ppermute | solution.py:24
  31.4 4.4 %fusion.28 = f32[256,1024]{1,0:T(8,128)} fusion(bf16[256,2048]{1,0:T(8,128)(2,1)S(1)} %fusion.2, bf16[2048,1024]{1,0:T(8,128)(2,1)} %param.20), kind=kOutput, calls=%fused_computation.128 | convolution fusion | flops 1073741824 | bytes 6291456 | tf_op jit(solution)/shard_map/dot_general | solution.py:58
  35.8 2.7 %reshape.424 = f32[256,4,256]{2,1,0:T(4,128)} reshape(f32[256,1024]{1,0:T(8,128)} %fusion.28) | data formatting | bytes 2097152 | tf_op jit(solution)/shard_map/reshape | solution.py:58
  38.5 1.6 multiply_reduce_fusion.2
  40.9 0.8 reshape.427
  43.0 1.3 gather_fusion
  44.3 1.3 and_reduce_fusion
  45.5 1.2 broadcast_subtract_fusion
  47.2 3.8 %multiply_reduce_fusion.1 = (f32[256]{0:T(256)S(1)}, f32[256,2048]{1,0:T(8,128)}) fusion(bf16[64,2048]{1,0:T(8,128)(2,1)} %param.28, bf16[256,2048]{1,0:T(8,128)(2,1)S(1)} %fusion.2, bf16[2048,64]{0,1:T(8,128)(2,1)} %param.27), kind=kOutput, calls=%fused_computation.9 | convolution fusion | flops 135282432 | bytes 3671040 | tf_op jit(solution)/shard_map/dot_general | solution.py:336
  51.6 1.3 constant_dynamic-update-slice_fusion.7
  52.9 1.3 constant_dynamic-update-slice_fusion.5
  54.2 1.3 broadcast_select_fusion.table_ref
  55.5 1.3 constant_dynamic-update-slice_fusion.8
  56.8 1.3 constant_dynamic-update-slice_fusion.6
  58.1 1.3 constant_dynamic-update-slice_fusion.4
  59.4 1.3 constant_dynamic-update-slice_fusion.2
  60.7 1.3 constant_dynamic-update-slice_fusion
  62.0 1.5 convolution_convert_fusion
  63.5 1.2 multiply_cosine_fusion
  64.7 0.9 fusion.4
  65.6 0.8 fusion.27
  66.7 1.8 %pad_maximum_fusion.1 = bf16[512,512]{1,0:T(8,128)(2,1)} fusion(bf16[256,512]{1,0:T(8,128)(2,1)} %collective-permute-done, bf16[256,256]{1,0:T(8,128)(2,1)S(1)} %multiply_convert_fusion.1, bf16[256,128]{1,0:T(8,128)(2,1)S(1)} %bitcast.50, bf16[256,128]{1,0:T(8,128)(2,1)S(1)} %bitcast.47), kind=kLoop, calls=%fused_computation.19 | loop fusion | flops 2097152 | bytes 1048576 | tf_op jit(solution)/shard_map/concatenate | solution.py:303
  68.5 5.1 %collective-permute-start.1 = (bf16[512,512]{1,0:T(8,128)(2,1)}, bf16[512,512]{1,0:T(8,128)(2,1)}, u32[]{:S(2)}, u32[]{:S(2)}) collective-permute-start(bf16[512,512]{1,0:T(8,128)(2,1)} %pad_maximum_fusion.1), channel_id=1, source_target_pairs={{0,2},{1,3},{2,4},{3,5},{4,6},{5,7},{6,8},{7,9},{8,10},{9,11},{10,... | collective-permute-start | bytes 1572872 | tf_op jit(solution)/shard_map/ppermute | solution.py:24
  73.7 0.8 copy.59
  74.5 1.7 reshape.422
  80.1 2.5 %add_add_fusion = f32[256,1024]{1,0:T(8,128)} fusion(f32[256,2048]{1,0:T(8,128)} %get-tuple-element.69, s32[]{:T(128)} %select_n.57, f32[1024]{0:T(1024)S(1)} %dynamic_slice.21, f32[256]{0:T(256)} %add_rsqrt_fusion.4, bf16[256,2048]{1,0:T(8,128)(2,1)S(1)} %fusion.2, bf16[256,2048]{1,0:T(8,128)(2,1)S(1)} %copy-done.1), kind=kLoop, calls=%fused_computation.17 | loop fusion | flops 1572864 | bytes 3150852 | tf_op jit(solution)/shard_map/add | solution.py:340
  82.6 12.8 %collective-permute-done.1 = bf16[512,512]{1,0:T(8,128)(2,1)} collective-permute-done((bf16[512,512]{1,0:T(8,128)(2,1)}, bf16[512,512]{1,0:T(8,128)(2,1)}, u32[]{:S(2)}, u32[]{:S(2)}) %collective-permute-start.1) | collective-permute-done | bytes 524320 | tf_op jit(solution)/shard_map/ppermute | solution.py:24
  95.4 1.3 pad_maximum_fusion
  96.7 1.1 fusion.26
  97.8 1.1 copy.60.row_req_ref
  98.9 1.0 copy.61.row_pos_ref
  99.9 32.7 %all-gather.2.cloned.1.call-done = bf16[16384,512]{1,0:T(8,128)(2,1)} async-done(((bf16[256,512]{1,0:T(8,128)(2,1)}), bf16[16384,512]{1,0:T(8,128)(2,1)}) %all-gather.2.cloned.1.call-update) | async-done | bytes 16777232 | tf_op jit(solution)/shard_map/all_gather | solution.py:269
  132.6 26.7 %shard_map.193 = (f32[2,128,2048]{2,1,0:T(8,128)}, bf16[2,128,2048]{2,1,0:T(8,128)(2,1)}) custom-call(s32[2,32]{1,0:T(2,128)} %broadcast_select_fusion.table_ref, bf16[2,512,256]{2,1,0:T(8,128)(2,1)} %bitcast.45, s32[2,512,1]{2,1,0:T(8,128)} %copy.60.row_req_ref, s32[2,512,1]{2,1,0:T(8,128)} %copy.61.row_pos_ref, s32[1,1280]{1,0:T(1,128)} %broadcast_in_dim.13.key_req_ref, ...), custom_call_target="tpu_custom_call" | custom-call | flops 6710886400 | bytes 16252928 | tf_op jit(solution)/shard_map/pallas_call | solution.py:228
  159.3 0.9 collective-permute-start.3
  160.2 2.5 %collective-permute-done.3 = bf16[256,2048]{1,0:T(8,128)(2,1)S(1)} collective-permute-done((bf16[256,2048]{1,0:T(8,128)(2,1)}, bf16[256,2048]{1,0:T(8,128)(2,1)S(1)}, u32[]{:S(2)}, u32[]{:S(2)}) %collective-permute-start.3) | collective-permute-done | bytes 1048608 | tf_op jit(solution)/shard_map/ppermute | solution.py:378
  162.7 2.1 %multiply_reduce_fusion = (f32[256]{0:T(256)S(1)}, f32[256,2048]{1,0:T(8,128)S(1)}) fusion(bf16[256,2048]{1,0:T(8,128)(2,1)S(1)} %collective-permute-done.3, f32[2,128,2048]{2,1,0:T(8,128)} %get-tuple-element.19), kind=kLoop, calls=%fused_computation.8 | loop fusion | flops 2096896 | bytes 5243904 | tf_op jit(solution)/shard_map/reduce_sum | solution.py:28
  164.8 1.0 multiply_convert_fusion
  (73 shorter events, 11.7 us)
Async XLA Ops:
  7.2 6.1 %copy-start = (bf16[2048,256]{1,0:T(8,128)(2,1)S(1)}, bf16[2048,256]{1,0:T(8,128)(2,1)}, u32[]{:S(2)}) copy-start(bf16[2048,256]{1,0:T(8,128)(2,1)} %param.21) | copy-start | bytes 3145732
  7.2 5.0 %copy-start.1 = (bf16[256,2048]{1,0:T(8,128)(2,1)S(1)}, bf16[256,2048]{1,0:T(8,128)(2,1)}, u32[]{:S(2)}) copy-start(bf16[256,2048]{1,0:T(8,128)(2,1)} %param.18) | copy-start | bytes 3145732
  7.2 125.4 %all-gather.2.cloned.1.call-start = ((), (), s32[]{:S(2)}) async-start(), calls=%async_computation | async-start | bytes 17039360 | tf_op jit(solution)/shard_map/all_gather | solution.py:269
  13.8 3.6 %copy-start.12 = (s32[32]{0:T(128)S(1)}, s32[32]{0:T(128)}, u32[]{:S(2)}) copy-start(s32[32]{0:T(128)} %param.34) | copy-start | bytes 388
  13.8 5.6 %copy-start.11 = (f32[256]{0:T(256)S(1)}, f32[256]{0:T(256)}, u32[]{:S(2)}) copy-start(f32[256]{0:T(256)} %param.24) | copy-start | bytes 3076
  17.2 18.6 %copy-start.10 = (f32[128]{0:T(128)}, f32[128]{0:T(128)S(1)}, u32[]{:S(2)}) copy-start(f32[128]{0:T(128)S(1)} %negate_power_fusion) | copy-start | bytes 1540
  22.9 43.8 %collective-permute-start = (bf16[256,512]{1,0:T(8,128)(2,1)}, bf16[256,512]{1,0:T(8,128)(2,1)}, u32[]{:S(2)}, u32[]{:S(2)}) collective-permute-start(bf16[256,512]{1,0:T(8,128)(2,1)} %pad_maximum_fusion.4), channel_id=1, source_target_pairs={{0,1},{1,2},{2,3},{3,4},{4,5},{5,6},{6,7},{7,8},{8,9},{9,10},{10,1... | collective-permute-start | bytes 786440 | tf_op jit(solution)/shard_map/ppermute | solution.py:24
  27.5 55.1 %collective-permute-start.2 = (bf16[256,512]{1,0:T(8,128)(2,1)}, bf16[256,512]{1,0:T(8,128)(2,1)}, u32[]{:S(2)}, u32[]{:S(2)}) collective-permute-start(bf16[256,512]{1,0:T(8,128)(2,1)} %pad_maximum_fusion.4), channel_id=1, source_target_pairs={{0,4},{1,5},{2,6},{3,7},{4,8},{5,9},{6,10},{7,11},{8,12},{9,13},{1... | collective-permute-start | bytes 786440 | tf_op jit(solution)/shard_map/ppermute | solution.py:24
  40.9 21.1 %copy-start.4 = (bf16[2,32768]{1,0:T(2,128)(2,1)S(1)}, bf16[2,32768]{1,0:T(2,128)(2,1)}, u32[]{:S(2)}) copy-start(bf16[2,32768]{1,0:T(2,128)(2,1)} %reshape_reshape.4) | copy-start | bytes 393220
  44.3 9.9 %copy-start.9 = (s32[2,32]{1,0:T(2,128)S(1)}, s32[2,32]{1,0:T(2,128)}, u32[]{:S(2)}) copy-start(s32[2,32]{1,0:T(2,128)} %gather_fusion) | copy-start | bytes 772
  51.0 13.7 %copy-start.3 = (f32[256,1024]{1,0:T(8,128)S(1)}, f32[256,1024]{1,0:T(8,128)}, u32[]{:S(2)}) copy-start(f32[256,1024]{1,0:T(8,128)} %fusion.28) | copy-start | bytes 3145732
  62.0 4.5 %copy-start.5 = (s32[1280]{0:T(1024)S(1)}, s32[1280]{0:T(1024)}, u32[]{:S(2)}) copy-start(s32[1280]{0:T(1024)} %constant_dynamic-update-slice_fusion.5) | copy-start | bytes 15364
  62.0 4.5 %copy-start.8 = (s32[256]{0:T(256)S(1)}, s32[256]{0:T(256)}, u32[]{:S(2)}) copy-start(s32[256]{0:T(256)} %get-tuple-element.51) | copy-start | bytes 3076
  65.6 8.0 %copy-start.7 = (s32[256]{0:T(256)S(1)}, s32[256]{0:T(256)}, u32[]{:S(2)}) copy-start(s32[256]{0:T(256)} %get-tuple-element.23) | copy-start | bytes 3076
  66.6 11.6 %copy-start.6 = (s32[1280]{0:T(1024)S(1)}, s32[1280]{0:T(1024)}, u32[]{:S(2)}) copy-start(s32[1280]{0:T(1024)} %constant_dynamic-update-slice_fusion) | copy-start | bytes 15364
  68.5 26.9 %collective-permute-start.1 = (bf16[512,512]{1,0:T(8,128)(2,1)}, bf16[512,512]{1,0:T(8,128)(2,1)}, u32[]{:S(2)}, u32[]{:S(2)}) collective-permute-start(bf16[512,512]{1,0:T(8,128)(2,1)} %pad_maximum_fusion.1), channel_id=1, source_target_pairs={{0,2},{1,3},{2,4},{3,5},{4,6},{5,7},{6,8},{7,9},{8,10},{9,11},{10,... | collective-permute-start | bytes 1572872 | tf_op jit(solution)/shard_map/ppermute | solution.py:24
  159.3 3.4 %collective-permute-start.3 = (bf16[256,2048]{1,0:T(8,128)(2,1)}, bf16[256,2048]{1,0:T(8,128)(2,1)S(1)}, u32[]{:S(2)}, u32[]{:S(2)}) collective-permute-start(bf16[256,2048]{1,0:T(8,128)(2,1)} %bitcast.57), channel_id=1, source_target_pairs={{0,64},{64,0},{1,65},{65,1},{2,66},{66,2},{3,67},{67,3},{4,68},{68... | collective-permute-start | bytes 3145736 | tf_op jit(solution)/shard_map/ppermute | solution.py:378
  162.7 2.1 %copy-start.2 = (f32[256,1024]{1,0:T(8,128)S(1)}, f32[256,1024]{1,0:T(8,128)}, u32[]{:S(2)}) copy-start(f32[256,1024]{1,0:T(8,128)} %add_add_fusion) | copy-start | bytes 3145732
  162.7 2.1 %dynamic-slice-start = ((f32[2048]{0:T(1024)}, s32[]{:T(128)}), f32[1024]{0:T(1024)S(1)}, s32[]{:S(2)}) async-start(f32[2048]{0:T(1024)} %param.26, s32[]{:T(128)} %select_n.57), calls=%async_computation.1 | async-start | bytes 8704 | tf_op jit(solution)/shard_map/dynamic_slice | solution.py:333
Sparse Core Ops, SparseCore 0:
  10.9 121.6 all-gather.1

commit v3 on v2

--- a/solution.py
+++ b/solution.py
@@ -126,7 +126,7 @@
 ):
     slot_refs = rest[:PAGES_PER_STEP]
     out_ref, out_low_ref = rest[PAGES_PER_STEP : PAGES_PER_STEP + 2]
-    scores_buf, values_buf, suffix_buf, top_buf = rest[PAGES_PER_STEP + 2 :]
+    scores_buf, keys_buf, values_buf, suffix_buf, top_buf = rest[PAGES_PER_STEP + 2 :]
     step = pl.program_id(1)
     last = pl.num_programs(1) - 1
     contract_last = (((1,), (1,)), ((), ()))
@@ -143,39 +143,48 @@
 
     @pl.when(step < last)
     def _():
-        q = q_ref[0]
-        top = top_buf[...]
+        base = pl.multiple_of(step * (PAGES_PER_STEP * PAGE_TOKENS), PAGES_PER_STEP * PAGE_TOKENS)
         for i in range(PAGES_PER_STEP):
             page = slot_refs[i][0]
-            at = pl.multiple_of((step * PAGES_PER_STEP + i) * PAGE_TOKENS, PAGE_TOKENS)
-            scores = lax.dot_general(
-                q, page[:, :HEAD_SIZE], contract_last, preferred_element_type=jnp.float32
-            )
-            scores_buf[:, pl.ds(at, PAGE_TOKENS)] = scores
+            at = pl.multiple_of(base + i * PAGE_TOKENS, PAGE_TOKENS)
+            keys_buf[pl.ds(at, PAGE_TOKENS), :] = page[:, :HEAD_SIZE]
             values_buf[pl.ds(at, PAGE_TOKENS), :] = page[:, HEAD_SIZE:]
-            top = jnp.maximum(top, jnp.max(scores, axis=1, keepdims=True))
-        top_buf[...] = top
+        scores = lax.dot_general(
+            q_ref[0], keys_buf[pl.ds(base, PAGES_PER_STEP * PAGE_TOKENS), :], contract_last,
+            preferred_element_type=jnp.float32,
+        )
+        scores_buf[:, pl.ds(base, PAGES_PER_STEP * PAGE_TOKENS)] = scores
+        top_buf[...] = jnp.maximum(top_buf[...], jnp.max(scores, axis=1, keepdims=True))
 
     @pl.when(step == last)
     def _():
         rows = q_ref.shape[1]
         heads = rows // PAGE_TOKENS
+        chunk = 512
+        chunks = PREFIX_PAGES * PAGE_TOKENS // chunk
         total_out = None
         for h in range(heads):
             r = h * PAGE_TOKENS
             row_top = top_buf[r : r + PAGE_TOKENS, :]
-            prefix_weights = jnp.exp(scores_buf[r : r + PAGE_TOKENS, :] - row_top)
             suffix_weights = jnp.exp(suffix_buf[r : r + PAGE_TOKENS, :] - row_top)
-            row_total = jnp.sum(prefix_weights, axis=1, keepdims=True) + jnp.sum(
-                suffix_weights, axis=1, keepdims=True
-            )
+            row_total = jnp.sum(suffix_weights, axis=1, keepdims=True)
             mixture = jnp.dot(
-                prefix_weights.astype(jnp.bfloat16), values_buf[...],
-                preferred_element_type=jnp.float32,
-            ) + jnp.dot(
                 suffix_weights.astype(jnp.bfloat16), suffix_values_ref[...],
                 preferred_element_type=jnp.float32,
             )
+
+            def one_chunk(c, carry, r=r, row_top=row_top):
+                row_total, mixture = carry
+                at = pl.multiple_of(c * chunk, chunk)
+                weights = jnp.exp(scores_buf[r : r + PAGE_TOKENS, pl.ds(at, chunk)] - row_top)
+                row_total = row_total + jnp.sum(weights, axis=1, keepdims=True)
+                mixture = mixture + jnp.dot(
+                    weights.astype(jnp.bfloat16), values_buf[pl.ds(at, chunk), :],
+                    preferred_element_type=jnp.float32,
+                )
+                return row_total, mixture
+
+            row_total, mixture = lax.fori_loop(0, chunks, one_chunk, (row_total, mixture))
             attended = (mixture / row_total).astype(jnp.bfloat16)
             part = jnp.dot(
                 attended, w_out_ref[r * 2 : r * 2 + HEAD_SIZE, :], preferred_element_type=jnp.float32
@@ -217,6 +226,7 @@
         ],
         scratch_shapes=[
             pltpu.VMEM((rows, PREFIX_PAGES * PAGE_TOKENS), jnp.float32),
+            pltpu.VMEM((PREFIX_PAGES * PAGE_TOKENS, HEAD_SIZE), jnp.bfloat16),
             pltpu.VMEM((PREFIX_PAGES * PAGE_TOKENS, HEAD_SIZE), jnp.bfloat16),
             pltpu.VMEM((rows, suffix_rows), jnp.float32),
             pltpu.VMEM((rows, 1), jnp.float32),

time: 174 us -> 180 us (1.034)
  Pallas kernels: 26.7 us -> 32.7 us
    pallas_call x1, Pallas kernels: 26.7 us -> 32.7 us  [page_attention(): pl.pallas_call(page_attention_kernel, grid_spec=grid_spec, out_shape=(jax...]
  transfers between devices with their start and end apart: 5 -> 5, of which waited for: 3 -> 3; matrix products, arithmetic and copies ran while one was open for 37% -> 36% of each run, Pallas kernels for 0% -> 0%
where the time goes in v3:
time: 180 us; the launch traced here: 179 us
  waiting for transfers between devices  48 us (27%)
  other arithmetic  38.6 us (21%)
  Pallas kernels  32.7 us (18%)
  local copies, waits for them, and re-layouts  19.1 us (11%)
  between operations  14.3 us (8%)
  starting transfers between devices  13.9 us (8%)
  matrix products  12 us (7%)
    pallas_call x1, Pallas kernels, page_attention(): pl.pallas_call(page_attention_kernel, grid_spec=grid_spec, out_shape=(jax...  32.7 us
    all_gather x1, waiting for transfers between devices, local(): every_slot = lax.all_gather(prefix_both, 'page', axis=0, tiled=True)  32.7 us
    ppermute x3, starting transfers between devices, passed_along(): return lax.ppermute(block, axis, route)  13 us
    ppermute x3, waiting for transfers between devices, passed_along(): return lax.ppermute(block, axis, route)  12.8 us
    unnamed x10, other arithmetic  9.12 us
    reduce_sum x3, other arithmetic, rms_scale(): jnp.mean(values * values, axis=-1, keepdims=True) + epsilon  5.16 us
    dot_general x1, matrix products, project(): jnp.dot(normed, w_query, preferred_element_type=jnp.float32)  4.42 us
    dot_general x1, matrix products, local(): jnp.dot(low_rank, laurel_right, preferred_element_type=jnp.float32)  3.76 us
  transfers between devices with their start and end apart: 5, of which 3 were waited for; matrix products, arithmetic and copies ran while one was open for 36% of the time, Pallas kernels for 0%

profile of v3, /device:TPU:1, one launch (start us, length us, event | category | flops | bytes accessed | tf_op | source)
XLA Modules:
  0.0 178.7 jit_solution(4059850958876064994)
XLA Ops:
  7.2 1.8 %pad_maximum_fusion.5 = bf16[256,512]{1,0:T(8,128)(2,1)} fusion(bf16[256,256]{1,0:T(8,128)(2,1)} %param.31, bf16[256,256]{1,0:T(8,128)(2,1)} %param.30), kind=kLoop, calls=%fused_computation.25 | loop fusion | flops 524288 | bytes 524288 | tf_op jit(solution)/shard_map/concatenate | solution.py:278
  10.7 1.5 fusion
  12.2 1.0 fusion.2
  13.8 0.8 copy.54
  14.6 1.8 multiply_reduce_fusion.3
  16.4 0.8 copy.56
  17.3 0.8 select_reduce_fusion
  18.1 1.3 constant_dynamic-update-slice_fusion.9
  19.4 1.0 multiply_bitcast_fusion
  21.1 1.1 multiply_convert_fusion.1
  22.9 4.6 %collective-permute-start = (bf16[256,512]{1,0:T(8,128)(2,1)}, bf16[256,512]{1,0:T(8,128)(2,1)}, u32[]{:S(2)}, u32[]{:S(2)}) collective-permute-start(bf16[256,512]{1,0:T(8,128)(2,1)} %pad_maximum_fusion.4), channel_id=1, source_target_pairs={{0,1},{1,2},{2,3},{3,4},{4,5},{5,6},{6,7},{7,8},{8,9},{9,10},{10,1... | collective-permute-start | bytes 786440 | tf_op jit(solution)/shard_map/ppermute | solution.py:24
  27.5 3.2 %collective-permute-start.2 = (bf16[256,512]{1,0:T(8,128)(2,1)}, bf16[256,512]{1,0:T(8,128)(2,1)}, u32[]{:S(2)}, u32[]{:S(2)}) collective-permute-start(bf16[256,512]{1,0:T(8,128)(2,1)} %pad_maximum_fusion.4), channel_id=1, source_target_pairs={{0,4},{1,5},{2,6},{3,7},{4,8},{5,9},{6,10},{7,11},{8,12},{9,13},{1... | collective-permute-start | bytes 786440 | tf_op jit(solution)/shard_map/ppermute | solution.py:24
  31.4 4.4 %fusion.28 = f32[256,1024]{1,0:T(8,128)} fusion(bf16[256,2048]{1,0:T(8,128)(2,1)S(1)} %fusion.2, bf16[2048,1024]{1,0:T(8,128)(2,1)} %param.20), kind=kOutput, calls=%fused_computation.128 | convolution fusion | flops 1073741824 | bytes 6291456 | tf_op jit(solution)/shard_map/dot_general | solution.py:58
  35.8 2.7 %reshape.424 = f32[256,4,256]{2,1,0:T(4,128)} reshape(f32[256,1024]{1,0:T(8,128)} %fusion.28) | data formatting | bytes 2097152 | tf_op jit(solution)/shard_map/reshape | solution.py:58
  38.5 1.6 multiply_reduce_fusion.2
  40.9 0.8 reshape.427
  43.0 1.3 gather_fusion
  44.3 1.3 and_reduce_fusion
  45.5 1.2 broadcast_subtract_fusion
  47.2 3.8 %multiply_reduce_fusion.1 = (f32[256]{0:T(256)S(1)}, f32[256,2048]{1,0:T(8,128)}) fusion(bf16[64,2048]{1,0:T(8,128)(2,1)} %param.28, bf16[256,2048]{1,0:T(8,128)(2,1)S(1)} %fusion.2, bf16[2048,64]{0,1:T(8,128)(2,1)} %param.27), kind=kOutput, calls=%fused_computation.9 | convolution fusion | flops 135282432 | bytes 3671040 | tf_op jit(solution)/shard_map/dot_general | solution.py:346
  51.6 1.3 constant_dynamic-update-slice_fusion.7
  52.9 1.3 constant_dynamic-update-slice_fusion.5
  54.2 1.3 broadcast_select_fusion.table_ref
  55.5 1.3 constant_dynamic-update-slice_fusion.8
  56.8 1.3 constant_dynamic-update-slice_fusion.6
  58.1 1.3 constant_dynamic-update-slice_fusion.4
  59.4 1.3 constant_dynamic-update-slice_fusion.2
  60.7 1.3 constant_dynamic-update-slice_fusion
  62.0 1.5 convolution_convert_fusion
  63.5 1.2 multiply_cosine_fusion
  64.7 0.9 fusion.4
  65.6 0.8 fusion.27
  66.7 1.8 %pad_maximum_fusion.1 = bf16[512,512]{1,0:T(8,128)(2,1)} fusion(bf16[256,512]{1,0:T(8,128)(2,1)} %collective-permute-done, bf16[256,256]{1,0:T(8,128)(2,1)S(1)} %multiply_convert_fusion.1, bf16[256,128]{1,0:T(8,128)(2,1)S(1)} %bitcast.50, bf16[256,128]{1,0:T(8,128)(2,1)S(1)} %bitcast.47), kind=kLoop, calls=%fused_computation.19 | loop fusion | flops 2097152 | bytes 1048576 | tf_op jit(solution)/shard_map/concatenate | solution.py:313
  68.5 5.1 %collective-permute-start.1 = (bf16[512,512]{1,0:T(8,128)(2,1)}, bf16[512,512]{1,0:T(8,128)(2,1)}, u32[]{:S(2)}, u32[]{:S(2)}) collective-permute-start(bf16[512,512]{1,0:T(8,128)(2,1)} %pad_maximum_fusion.1), channel_id=1, source_target_pairs={{0,2},{1,3},{2,4},{3,5},{4,6},{5,7},{6,8},{7,9},{8,10},{9,11},{10,... | collective-permute-start | bytes 1572872 | tf_op jit(solution)/shard_map/ppermute | solution.py:24
  73.7 0.8 copy.59
  74.5 1.7 reshape.422
  80.1 2.5 %add_add_fusion = f32[256,1024]{1,0:T(8,128)} fusion(f32[256,2048]{1,0:T(8,128)} %get-tuple-element.69, s32[]{:T(128)} %select_n.57, f32[1024]{0:T(1024)S(1)} %dynamic_slice.21, f32[256]{0:T(256)} %add_rsqrt_fusion.4, bf16[256,2048]{1,0:T(8,128)(2,1)S(1)} %fusion.2, bf16[256,2048]{1,0:T(8,128)(2,1)S(1)} %copy-done.1), kind=kLoop, calls=%fused_computation.17 | loop fusion | flops 1572864 | bytes 3150852 | tf_op jit(solution)/shard_map/add | solution.py:350
  82.6 12.8 %collective-permute-done.1 = bf16[512,512]{1,0:T(8,128)(2,1)} collective-permute-done((bf16[512,512]{1,0:T(8,128)(2,1)}, bf16[512,512]{1,0:T(8,128)(2,1)}, u32[]{:S(2)}, u32[]{:S(2)}) %collective-permute-start.1) | collective-permute-done | bytes 524320 | tf_op jit(solution)/shard_map/ppermute | solution.py:24
  95.4 1.3 pad_maximum_fusion
  96.7 1.1 fusion.26
  97.8 1.1 copy.60.row_req_ref
  98.9 1.0 copy.61.row_pos_ref
  99.9 32.7 %all-gather.2.cloned.1.call-done = bf16[16384,512]{1,0:T(8,128)(2,1)} async-done(((bf16[256,512]{1,0:T(8,128)(2,1)}), bf16[16384,512]{1,0:T(8,128)(2,1)}) %all-gather.2.cloned.1.call-update) | async-done | bytes 16777232 | tf_op jit(solution)/shard_map/all_gather | solution.py:279
  132.6 32.7 %shard_map.193 = (f32[2,128,2048]{2,1,0:T(8,128)}, bf16[2,128,2048]{2,1,0:T(8,128)(2,1)}) custom-call(s32[2,32]{1,0:T(2,128)} %broadcast_select_fusion.table_ref, bf16[2,512,256]{2,1,0:T(8,128)(2,1)} %bitcast.45, s32[2,512,1]{2,1,0:T(8,128)} %copy.60.row_req_ref, s32[2,512,1]{2,1,0:T(8,128)} %copy.61.row_pos_ref, s32[1,1280]{1,0:T(1,128)} %broadcast_in_dim.13.key_req_ref, ...), custom_call_target="tpu_custom_call" | custom-call | flops 6710886400 | bytes 16252928 | tf_op jit(solution)/shard_map/pallas_call | solution.py:238
  165.3 0.9 collective-permute-start.3
  166.2 2.5 %collective-permute-done.3 = bf16[256,2048]{1,0:T(8,128)(2,1)S(1)} collective-permute-done((bf16[256,2048]{1,0:T(8,128)(2,1)}, bf16[256,2048]{1,0:T(8,128)(2,1)S(1)}, u32[]{:S(2)}, u32[]{:S(2)}) %collective-permute-start.3) | collective-permute-done | bytes 1048608 | tf_op jit(solution)/shard_map/ppermute | solution.py:388
  168.7 2.1 %multiply_reduce_fusion = (f32[256]{0:T(256)S(1)}, f32[256,2048]{1,0:T(8,128)S(1)}) fusion(bf16[256,2048]{1,0:T(8,128)(2,1)S(1)} %collective-permute-done.3, f32[2,128,2048]{2,1,0:T(8,128)} %get-tuple-element.19), kind=kLoop, calls=%fused_computation.8 | loop fusion | flops 2096896 | bytes 5243904 | tf_op jit(solution)/shard_map/reduce_sum | solution.py:28
  170.8 1.0 multiply_convert_fusion
  (73 shorter events, 11.7 us)
Async XLA Ops:
  7.2 6.1 %copy-start = (bf16[2048,256]{1,0:T(8,128)(2,1)S(1)}, bf16[2048,256]{1,0:T(8,128)(2,1)}, u32[]{:S(2)}) copy-start(bf16[2048,256]{1,0:T(8,128)(2,1)} %param.21) | copy-start | bytes 3145732
  7.2 5.0 %copy-start.1 = (bf16[256,2048]{1,0:T(8,128)(2,1)S(1)}, bf16[256,2048]{1,0:T(8,128)(2,1)}, u32[]{:S(2)}) copy-start(bf16[256,2048]{1,0:T(8,128)(2,1)} %param.18) | copy-start | bytes 3145732
  7.2 125.4 %all-gather.2.cloned.1.call-start = ((), (), s32[]{:S(2)}) async-start(), calls=%async_computation | async-start | bytes 17039360 | tf_op jit(solution)/shard_map/all_gather | solution.py:279
  13.8 3.6 %copy-start.12 = (s32[32]{0:T(128)S(1)}, s32[32]{0:T(128)}, u32[]{:S(2)}) copy-start(s32[32]{0:T(128)} %param.34) | copy-start | bytes 388
  13.8 5.6 %copy-start.11 = (f32[256]{0:T(256)S(1)}, f32[256]{0:T(256)}, u32[]{:S(2)}) copy-start(f32[256]{0:T(256)} %param.24) | copy-start | bytes 3076
  17.2 18.6 %copy-start.10 = (f32[128]{0:T(128)}, f32[128]{0:T(128)S(1)}, u32[]{:S(2)}) copy-start(f32[128]{0:T(128)S(1)} %negate_power_fusion) | copy-start | bytes 1540
  22.9 43.8 %collective-permute-start = (bf16[256,512]{1,0:T(8,128)(2,1)}, bf16[256,512]{1,0:T(8,128)(2,1)}, u32[]{:S(2)}, u32[]{:S(2)}) collective-permute-start(bf16[256,512]{1,0:T(8,128)(2,1)} %pad_maximum_fusion.4), channel_id=1, source_target_pairs={{0,1},{1,2},{2,3},{3,4},{4,5},{5,6},{6,7},{7,8},{8,9},{9,10},{10,1... | collective-permute-start | bytes 786440 | tf_op jit(solution)/shard_map/ppermute | solution.py:24
  27.5 55.1 %collective-permute-start.2 = (bf16[256,512]{1,0:T(8,128)(2,1)}, bf16[256,512]{1,0:T(8,128)(2,1)}, u32[]{:S(2)}, u32[]{:S(2)}) collective-permute-start(bf16[256,512]{1,0:T(8,128)(2,1)} %pad_maximum_fusion.4), channel_id=1, source_target_pairs={{0,4},{1,5},{2,6},{3,7},{4,8},{5,9},{6,10},{7,11},{8,12},{9,13},{1... | collective-permute-start | bytes 786440 | tf_op jit(solution)/shard_map/ppermute | solution.py:24
  40.9 21.1 %copy-start.4 = (bf16[2,32768]{1,0:T(2,128)(2,1)S(1)}, bf16[2,32768]{1,0:T(2,128)(2,1)}, u32[]{:S(2)}) copy-start(bf16[2,32768]{1,0:T(2,128)(2,1)} %reshape_reshape.4) | copy-start | bytes 393220
  44.3 9.9 %copy-start.9 = (s32[2,32]{1,0:T(2,128)S(1)}, s32[2,32]{1,0:T(2,128)}, u32[]{:S(2)}) copy-start(s32[2,32]{1,0:T(2,128)} %gather_fusion) | copy-start | bytes 772
  51.0 13.7 %copy-start.3 = (f32[256,1024]{1,0:T(8,128)S(1)}, f32[256,1024]{1,0:T(8,128)}, u32[]{:S(2)}) copy-start(f32[256,1024]{1,0:T(8,128)} %fusion.28) | copy-start | bytes 3145732
  62.0 4.5 %copy-start.5 = (s32[1280]{0:T(1024)S(1)}, s32[1280]{0:T(1024)}, u32[]{:S(2)}) copy-start(s32[1280]{0:T(1024)} %constant_dynamic-update-slice_fusion.5) | copy-start | bytes 15364
  62.0 4.5 %copy-start.8 = (s32[256]{0:T(256)S(1)}, s32[256]{0:T(256)}, u32[]{:S(2)}) copy-start(s32[256]{0:T(256)} %get-tuple-element.51) | copy-start | bytes 3076
  65.6 8.0 %copy-start.7 = (s32[256]{0:T(256)S(1)}, s32[256]{0:T(256)}, u32[]{:S(2)}) copy-start(s32[256]{0:T(256)} %get-tuple-element.23) | copy-start | bytes 3076
  66.6 11.6 %copy-start.6 = (s32[1280]{0:T(1024)S(1)}, s32[1280]{0:T(1024)}, u32[]{:S(2)}) copy-start(s32[1280]{0:T(1024)} %constant_dynamic-update-slice_fusion) | copy-start | bytes 15364
  68.5 26.9 %collective-permute-start.1 = (bf16[512,512]{1,0:T(8,128)(2,1)}, bf16[512,512]{1,0:T(8,128)(2,1)}, u32[]{:S(2)}, u32[]{:S(2)}) collective-permute-start(bf16[512,512]{1,0:T(8,128)(2,1)} %pad_maximum_fusion.1), channel_id=1, source_target_pairs={{0,2},{1,3},{2,4},{3,5},{4,6},{5,7},{6,8},{7,9},{8,10},{9,11},{10,... | collective-permute-start | bytes 1572872 | tf_op jit(solution)/shard_map/ppermute | solution.py:24
  165.3 3.4 %collective-permute-start.3 = (bf16[256,2048]{1,0:T(8,128)(2,1)}, bf16[256,2048]{1,0:T(8,128)(2,1)S(1)}, u32[]{:S(2)}, u32[]{:S(2)}) collective-permute-start(bf16[256,2048]{1,0:T(8,128)(2,1)} %bitcast.57), channel_id=1, source_target_pairs={{0,64},{64,0},{1,65},{65,1},{2,66},{66,2},{3,67},{67,3},{4,68},{68... | collective-permute-start | bytes 3145736 | tf_op jit(solution)/shard_map/ppermute | solution.py:388
  168.7 2.1 %copy-start.2 = (f32[256,1024]{1,0:T(8,128)S(1)}, f32[256,1024]{1,0:T(8,128)}, u32[]{:S(2)}) copy-start(f32[256,1024]{1,0:T(8,128)} %add_add_fusion) | copy-start | bytes 3145732
  168.7 2.1 %dynamic-slice-start = ((f32[2048]{0:T(1024)}, s32[]{:T(128)}), f32[1024]{0:T(1024)S(1)}, s32[]{:S(2)}) async-start(f32[2048]{0:T(1024)} %param.26, s32[]{:T(128)} %select_n.57), calls=%async_computation.1 | async-start | bytes 8704 | tf_op jit(solution)/shard_map/dynamic_slice | solution.py:343
Sparse Core Ops, SparseCore 0:
  10.9 121.6 all-gather.1

commit v4 on v2

--- a/solution.py
+++ b/solution.py
@@ -362,23 +362,29 @@
             suffix_values,
         )
     )
-    attn_part, attn_low = page_attention(
-        chosen,
-        head_queries,
-        row_requests,
-        row_positions,
-        key_requests[None, :],
-        key_positions[None, :],
-        suffix_keys,
-        suffix_values,
-        w_out,
-        slot_pages,
-    )
-    attn_part = attn_part.reshape(tok_count, model_width)
-    partner_part = lax.ppermute(attn_low.reshape(tok_count, model_width), "kv", [(0, 1), (1, 0)])
-    summed_out = attn_part + partner_part.astype(jnp.float32)
-    attn_branch = columns(summed_out) * rms_scale(summed_out) * columns(post_gain)
-    layer_out = ((resident + attn_branch) * 2.0 ** (-0.5)).astype(jnp.bfloat16)
+    out_pages = []
+    for p in range(pages_here):
+        attn_part, attn_low = page_attention(
+            chosen[p : p + 1],
+            head_queries[p : p + 1],
+            row_requests[p : p + 1],
+            row_positions[p : p + 1],
+            key_requests[None, :],
+            key_positions[None, :],
+            suffix_keys,
+            suffix_values,
+            w_out,
+            slot_pages,
+        )
+        attn_part = attn_part.reshape(PAGE_TOKENS, model_width)
+        partner_part = lax.ppermute(
+            attn_low.reshape(PAGE_TOKENS, model_width), "kv", [(0, 1), (1, 0)]
+        )
+        summed_out = attn_part + partner_part.astype(jnp.float32)
+        attn_branch = columns(summed_out) * rms_scale(summed_out) * columns(post_gain)
+        rows_here = resident[p * PAGE_TOKENS : (p + 1) * PAGE_TOKENS]
+        out_pages.append(((rows_here + attn_branch) * 2.0 ** (-0.5)).astype(jnp.bfloat16))
+    layer_out = jnp.concatenate(out_pages, axis=0)
     return (layer_out, suffix_key_cache, suffix_value_cache)
 
 

time: 174 us -> 176 us (1.011)
  Pallas kernels: 26.7 us -> 30.9 us
  other arithmetic: 38.6 us -> 36.6 us
  waiting for transfers between devices: 48 us -> 46.2 us
    pallas_call x1 -> x2, Pallas kernels: 26.7 us -> 30.9 us  [page_attention(): pl.pallas_call(page_attention_kernel, grid_spec=grid_spec, out_shape=(jax...]
    slice x0 -> x4, local copies, waits for them, and re-layouts: none -> 3.11 us  [the longest x1 0.87 us: local(): row_positions[p:p + 1]]
    reduce_sum x3 -> x4, other arithmetic: 5.16 us -> 3.55 us  [rms_scale(): jnp.mean(values * values, axis=-1, keepdims=True) + epsilon]
  transfers between devices with their start and end apart: 5 -> 6, of which waited for: 3 -> 3; matrix products, arithmetic and copies ran while one was open for 37% -> 38% of each run, Pallas kernels for 0% -> 9%
where the time goes in v4:
time: 176 us; the launch traced here: 175 us
  waiting for transfers between devices  46.2 us (26%)
  other arithmetic  36.6 us (21%)
  Pallas kernels  30.9 us (18%)
  local copies, waits for them, and re-layouts  20.6 us (12%)
  between operations  14.4 us (8%)
  starting transfers between devices  14.2 us (8%)
  matrix products  12 us (7%)
    all_gather x1, waiting for transfers between devices, local(): every_slot = lax.all_gather(prefix_both, 'page', axis=0, tiled=True)  31.7 us
    pallas_call x2, Pallas kernels, page_attention(): pl.pallas_call(page_attention_kernel, grid_spec=grid_spec, out_shape=(jax...  30.9 us
    ppermute x3, starting transfers between devices, passed_along(): return lax.ppermute(block, axis, route)  13 us
    ppermute x3, waiting for transfers between devices, passed_along(): return lax.ppermute(block, axis, route)  12.6 us
    unnamed x10, other arithmetic  9.14 us
    dot_general x1, matrix products, project(): jnp.dot(normed, w_query, preferred_element_type=jnp.float32)  4.42 us
    dot_general x1, matrix products, local(): jnp.dot(low_rank, laurel_right, preferred_element_type=jnp.float32)  3.76 us
    reduce_sum x4, other arithmetic, rms_scale(): jnp.mean(values * values, axis=-1, keepdims=True) + epsilon  3.55 us
  transfers between devices with their start and end apart: 6, of which 3 were waited for; matrix products, arithmetic and copies ran while one was open for 38% of the time, Pallas kernels for 9%

profile of v4, /device:TPU:1, one launch (start us, length us, event | category | flops | bytes accessed | tf_op | source)
XLA Modules:
  0.0 174.9 jit_solution(1117432934774056953)
XLA Ops:
  7.2 1.8 %pad_maximum_fusion.6 = bf16[256,512]{1,0:T(8,128)(2,1)} fusion(bf16[256,256]{1,0:T(8,128)(2,1)} %param.31, bf16[256,256]{1,0:T(8,128)(2,1)} %param.30), kind=kLoop, calls=%fused_computation.29 | loop fusion | flops 524288 | bytes 524288 | tf_op jit(solution)/shard_map/concatenate | solution.py:268
  10.7 1.5 fusion
  12.2 1.0 fusion.2
  13.8 0.8 copy.62
  14.6 1.8 %multiply_reduce_fusion.4 = (f32[256]{0:T(256)S(1)}, f32[256,256]{0,1:T(8,128)S(1)}) fusion(bf16[256,2048]{1,0:T(8,128)(2,1)S(1)} %fusion.2, bf16[2048,256]{1,0:T(8,128)(2,1)} %param.22), kind=kOutput, calls=%fused_computation.31 | convolution fusion | flops 268566272 | bytes 2360320 | tf_op jit(solution)/shard_map/dot_general | solution.py:68
  16.4 0.8 copy.64
  17.3 0.8 select_reduce_fusion
  18.1 1.3 constant_dynamic-update-slice_fusion.9
  19.4 1.0 multiply_bitcast_fusion
  21.1 1.1 multiply_convert_fusion.2
  22.9 4.6 %collective-permute-start = (bf16[256,512]{1,0:T(8,128)(2,1)}, bf16[256,512]{1,0:T(8,128)(2,1)}, u32[]{:S(2)}, u32[]{:S(2)}) collective-permute-start(bf16[256,512]{1,0:T(8,128)(2,1)} %pad_maximum_fusion.5), channel_id=1, source_target_pairs={{0,1},{1,2},{2,3},{3,4},{4,5},{5,6},{6,7},{7,8},{8,9},{9,10},{10,1... | collective-permute-start | bytes 786440 | tf_op jit(solution)/shard_map/ppermute | solution.py:24
  27.5 3.2 %collective-permute-start.2 = (bf16[256,512]{1,0:T(8,128)(2,1)}, bf16[256,512]{1,0:T(8,128)(2,1)}, u32[]{:S(2)}, u32[]{:S(2)}) collective-permute-start(bf16[256,512]{1,0:T(8,128)(2,1)} %pad_maximum_fusion.5), channel_id=1, source_target_pairs={{0,4},{1,5},{2,6},{3,7},{4,8},{5,9},{6,10},{7,11},{8,12},{9,13},{1... | collective-permute-start | bytes 786440 | tf_op jit(solution)/shard_map/ppermute | solution.py:24
  31.4 4.4 %fusion.32 = f32[256,1024]{1,0:T(8,128)} fusion(bf16[256,2048]{1,0:T(8,128)(2,1)S(1)} %fusion.2, bf16[2048,1024]{1,0:T(8,128)(2,1)} %param.20), kind=kOutput, calls=%fused_computation.137 | convolution fusion | flops 1073741824 | bytes 6291456 | tf_op jit(solution)/shard_map/dot_general | solution.py:58
  35.8 2.7 %reshape.438 = f32[256,4,256]{2,1,0:T(4,128)} reshape(f32[256,1024]{1,0:T(8,128)} %fusion.32) | data formatting | bytes 2097152 | tf_op jit(solution)/shard_map/reshape | solution.py:58
  38.5 1.6 multiply_reduce_fusion.3
  40.9 0.8 reshape.441
  43.0 1.2 gather_fusion
  44.3 1.3 and_reduce_fusion
  45.5 1.2 broadcast_subtract_fusion
  47.4 3.8 %multiply_reduce_fusion = (f32[256]{0:T(256)S(1)}, f32[256,2048]{1,0:T(8,128)}) fusion(bf16[64,2048]{1,0:T(8,128)(2,1)} %param.28, bf16[256,2048]{1,0:T(8,128)(2,1)S(1)} %fusion.2, bf16[2048,64]{0,1:T(8,128)(2,1)} %param.27), kind=kOutput, calls=%fused_computation.7 | convolution fusion | flops 135282432 | bytes 3671040 | tf_op jit(solution)/shard_map/dot_general | solution.py:336
  53.0 1.3 constant_dynamic-update-slice_fusion.7
  54.3 1.3 constant_dynamic-update-slice_fusion.5
  55.6 1.3 constant_dynamic-update-slice_fusion.8
  56.9 1.3 constant_dynamic-update-slice_fusion.6
  58.2 1.3 constant_dynamic-update-slice_fusion.4
  59.5 1.3 constant_dynamic-update-slice_fusion.2
  60.9 1.3 constant_dynamic-update-slice_fusion
  62.2 1.5 convolution_convert_fusion
  63.7 1.2 multiply_cosine_fusion
  64.9 0.9 fusion.4
  65.8 0.8 fusion.30
  66.8 1.8 %pad_maximum_fusion.1 = bf16[512,512]{1,0:T(8,128)(2,1)} fusion(bf16[256,512]{1,0:T(8,128)(2,1)} %collective-permute-done, bf16[256,256]{1,0:T(8,128)(2,1)S(1)} %multiply_convert_fusion.2, bf16[256,128]{1,0:T(8,128)(2,1)S(1)} %bitcast.62, bf16[256,128]{1,0:T(8,128)(2,1)S(1)} %bitcast.59), kind=kLoop, calls=%fused_computation.20 | loop fusion | flops 2097152 | bytes 1048576 | tf_op jit(solution)/shard_map/concatenate | solution.py:303
  68.6 5.1 %collective-permute-start.1 = (bf16[512,512]{1,0:T(8,128)(2,1)}, bf16[512,512]{1,0:T(8,128)(2,1)}, u32[]{:S(2)}, u32[]{:S(2)}) collective-permute-start(bf16[512,512]{1,0:T(8,128)(2,1)} %pad_maximum_fusion.1), channel_id=1, source_target_pairs={{0,2},{1,3},{2,4},{3,5},{4,6},{5,7},{6,8},{7,9},{8,10},{9,11},{10,... | collective-permute-start | bytes 1572872 | tf_op jit(solution)/shard_map/ppermute | solution.py:24
  73.8 0.8 copy.67
  74.6 1.6 reshape.436
  80.2 2.5 %add_add_fusion = f32[256,1024]{1,0:T(8,128)} fusion(f32[256,2048]{1,0:T(8,128)} %get-tuple-element.85, s32[]{:T(128)} %select_n.59, f32[1024]{0:T(1024)S(1)} %dynamic_slice.25, f32[256]{0:T(256)} %add_rsqrt_fusion.3, bf16[256,2048]{1,0:T(8,128)(2,1)S(1)} %fusion.2, bf16[256,2048]{1,0:T(8,128)(2,1)S(1)} %copy-done.1), kind=kLoop, calls=%fused_computation.18 | loop fusion | flops 1572864 | bytes 3150852 | tf_op jit(solution)/shard_map/add | solution.py:340
  82.7 12.6 %collective-permute-done.1 = bf16[512,512]{1,0:T(8,128)(2,1)} collective-permute-done((bf16[512,512]{1,0:T(8,128)(2,1)}, bf16[512,512]{1,0:T(8,128)(2,1)}, u32[]{:S(2)}, u32[]{:S(2)}) %collective-permute-start.1) | collective-permute-done | bytes 524320 | tf_op jit(solution)/shard_map/ppermute | solution.py:24
  95.3 1.3 pad_maximum_fusion
  96.6 1.2 fusion.26
  98.2 0.9 fusion.27
  99.1 0.8 fusion.28
  100.0 0.8 fusion.29
  100.8 31.7 %all-gather.2.cloned.1.call-done = bf16[16384,512]{1,0:T(8,128)(2,1)} async-done(((bf16[256,512]{1,0:T(8,128)(2,1)}), bf16[16384,512]{1,0:T(8,128)(2,1)}) %all-gather.2.cloned.1.call-update) | async-done | bytes 16777232 | tf_op jit(solution)/shard_map/all_gather | solution.py:269
  132.5 15.4 %shard_map.194 = (f32[1,128,2048]{2,1,0:T(8,128)}, bf16[1,128,2048]{2,1,0:T(8,128)(2,1)}) custom-call(s32[1,32]{1,0:T(1,128)} %get-tuple-element.81.table_ref, bf16[1,512,256]{2,1,0:T(8,128)(2,1)} %get-tuple-element.71.q_ref, s32[1,512,1]{2,1,0:T(8,128)} %get-tuple-element.69.row_req_ref, s32[1,512,1]{2,1,0:T(8,128)} %get-tuple-element.67.row_pos_ref, ...), custom_call_target="tpu_custom_call" | custom-call | flops 3355443200 | bytes 10223616 | tf_op jit(solution)/shard_map/pallas_call | solution.py:228
  147.9 1.1 collective-permute-start.4
  149.0 15.5 %shard_map.193 = (f32[1,128,2048]{2,1,0:T(8,128)}, bf16[1,128,2048]{2,1,0:T(8,128)(2,1)}) custom-call(s32[1,32]{1,0:T(1,128)} %get-tuple-element.80.table_ref, bf16[1,512,256]{2,1,0:T(8,128)(2,1)} %get-tuple-element.70.q_ref, s32[1,512,1]{2,1,0:T(8,128)} %get-tuple-element.68.row_req_ref, s32[1,512,1]{2,1,0:T(8,128)} %get-tuple-element.66.row_pos_ref, ...), custom_call_target="tpu_custom_call" | custom-call | flops 3355443200 | bytes 10223616 | tf_op jit(solution)/shard_map/pallas_call | solution.py:228
  164.9 1.8 %collective-permute-done.3 = bf16[128,2048]{1,0:T(8,128)(2,1)S(1)} collective-permute-done((bf16[128,2048]{1,0:T(8,128)(2,1)}, bf16[128,2048]{1,0:T(8,128)(2,1)S(1)}, u32[]{:S(2)}, u32[]{:S(2)}) %collective-permute-start.3) | collective-permute-done | bytes 524320 | tf_op jit(solution)/shard_map/ppermute | solution.py:380
  167.2 0.8 pad_maximum_fusion.2
  (89 shorter events, 14.4 us)
Async XLA Ops:
  7.2 6.1 %copy-start = (bf16[2048,256]{1,0:T(8,128)(2,1)S(1)}, bf16[2048,256]{1,0:T(8,128)(2,1)}, u32[]{:S(2)}) copy-start(bf16[2048,256]{1,0:T(8,128)(2,1)} %param.21) | copy-start | bytes 3145732
  7.2 5.0 %copy-start.1 = (bf16[256,2048]{1,0:T(8,128)(2,1)S(1)}, bf16[256,2048]{1,0:T(8,128)(2,1)}, u32[]{:S(2)}) copy-start(bf16[256,2048]{1,0:T(8,128)(2,1)} %param.18) | copy-start | bytes 3145732
  7.2 125.3 %all-gather.2.cloned.1.call-start = ((), (), s32[]{:S(2)}) async-start(), calls=%async_computation | async-start | bytes 17039360 | tf_op jit(solution)/shard_map/all_gather | solution.py:269
  13.8 3.6 %copy-start.15 = (s32[32]{0:T(128)S(1)}, s32[32]{0:T(128)}, u32[]{:S(2)}) copy-start(s32[32]{0:T(128)} %param.34) | copy-start | bytes 388
  13.8 5.6 %copy-start.14 = (f32[256]{0:T(256)S(1)}, f32[256]{0:T(256)}, u32[]{:S(2)}) copy-start(f32[256]{0:T(256)} %param.24) | copy-start | bytes 3076
  17.2 18.6 %copy-start.13 = (f32[128]{0:T(128)}, f32[128]{0:T(128)S(1)}, u32[]{:S(2)}) copy-start(f32[128]{0:T(128)S(1)} %negate_power_fusion) | copy-start | bytes 1540
  22.9 43.9 %collective-permute-start = (bf16[256,512]{1,0:T(8,128)(2,1)}, bf16[256,512]{1,0:T(8,128)(2,1)}, u32[]{:S(2)}, u32[]{:S(2)}) collective-permute-start(bf16[256,512]{1,0:T(8,128)(2,1)} %pad_maximum_fusion.5), channel_id=1, source_target_pairs={{0,1},{1,2},{2,3},{3,4},{4,5},{5,6},{6,7},{7,8},{8,9},{9,10},{10,1... | collective-permute-start | bytes 786440 | tf_op jit(solution)/shard_map/ppermute | solution.py:24
  27.5 55.2 %collective-permute-start.2 = (bf16[256,512]{1,0:T(8,128)(2,1)}, bf16[256,512]{1,0:T(8,128)(2,1)}, u32[]{:S(2)}, u32[]{:S(2)}) collective-permute-start(bf16[256,512]{1,0:T(8,128)(2,1)} %pad_maximum_fusion.5), channel_id=1, source_target_pairs={{0,4},{1,5},{2,6},{3,7},{4,8},{5,9},{6,10},{7,11},{8,12},{9,13},{1... | collective-permute-start | bytes 786440 | tf_op jit(solution)/shard_map/ppermute | solution.py:24
  40.9 21.3 %copy-start.7 = (bf16[2,32768]{1,0:T(2,128)(2,1)S(1)}, bf16[2,32768]{1,0:T(2,128)(2,1)}, u32[]{:S(2)}) copy-start(bf16[2,32768]{1,0:T(2,128)(2,1)} %reshape_reshape.4) | copy-start | bytes 393220
  44.3 7.5 %copy-start.12 = (s32[2,32]{1,0:T(2,128)S(1)}, s32[2,32]{1,0:T(2,128)}, u32[]{:S(2)}) copy-start(s32[2,32]{1,0:T(2,128)} %gather_fusion) | copy-start | bytes 772
  51.1 13.7 %copy-start.3 = (f32[256,1024]{1,0:T(8,128)S(1)}, f32[256,1024]{1,0:T(8,128)}, u32[]{:S(2)}) copy-start(f32[256,1024]{1,0:T(8,128)} %fusion.32) | copy-start | bytes 3145732
  62.2 4.4 %copy-start.8 = (s32[1280]{0:T(1024)S(1)}, s32[1280]{0:T(1024)}, u32[]{:S(2)}) copy-start(s32[1280]{0:T(1024)} %constant_dynamic-update-slice_fusion.5) | copy-start | bytes 15364
  62.2 4.4 %copy-start.11 = (s32[256]{0:T(256)S(1)}, s32[256]{0:T(256)}, u32[]{:S(2)}) copy-start(s32[256]{0:T(256)} %get-tuple-element.55) | copy-start | bytes 3076
  65.7 8.0 %copy-start.10 = (s32[256]{0:T(256)S(1)}, s32[256]{0:T(256)}, u32[]{:S(2)}) copy-start(s32[256]{0:T(256)} %get-tuple-element.27) | copy-start | bytes 3076
  66.8 11.6 %copy-start.9 = (s32[1280]{0:T(1024)S(1)}, s32[1280]{0:T(1024)}, u32[]{:S(2)}) copy-start(s32[1280]{0:T(1024)} %constant_dynamic-update-slice_fusion) | copy-start | bytes 15364
  68.6 26.7 %collective-permute-start.1 = (bf16[512,512]{1,0:T(8,128)(2,1)}, bf16[512,512]{1,0:T(8,128)(2,1)}, u32[]{:S(2)}, u32[]{:S(2)}) collective-permute-start(bf16[512,512]{1,0:T(8,128)(2,1)} %pad_maximum_fusion.1), channel_id=1, source_target_pairs={{0,2},{1,3},{2,4},{3,5},{4,6},{5,7},{6,8},{7,9},{8,10},{9,11},{10,... | collective-permute-start | bytes 1572872 | tf_op jit(solution)/shard_map/ppermute | solution.py:24
  97.8 2.2 %copy-start.4 = (bf16[2,4,128,256]{3,2,1,0:T(8,128)(2,1)S(1)}, bf16[2,4,128,256]{3,2,1,0:T(8,128)(2,1)}, u32[]{:S(2)}) copy-start(bf16[2,4,128,256]{3,2,1,0:T(8,128)(2,1)} %copy.67) | copy-start | bytes 1572868
  147.9 16.8 %collective-permute-start.4 = (bf16[128,2048]{1,0:T(8,128)(2,1)}, bf16[128,2048]{1,0:T(8,128)(2,1)S(1)}, u32[]{:S(2)}, u32[]{:S(2)}) collective-permute-start(bf16[128,2048]{1,0:T(8,128)(2,1)} %bitcast.69), channel_id=1, source_target_pairs={{0,64},{64,0},{1,65},{65,1},{2,66},{66,2},{3,67},{67,3},{4,68},{68... | collective-permute-start | bytes 1572872 | tf_op jit(solution)/shard_map/ppermute | solution.py:380
  149.0 15.7 %copy-start.5 = (f32[1,128,2048]{2,1,0:T(8,128)S(1)}, f32[1,128,2048]{2,1,0:T(8,128)}, u32[]{:S(2)}) copy-start(f32[1,128,2048]{2,1,0:T(8,128)} %get-tuple-element.23) | copy-start | bytes 3145732
  164.5 2.2 %copy-start.6 = (f32[1,128,2048]{2,1,0:T(8,128)S(1)}, f32[1,128,2048]{2,1,0:T(8,128)}, u32[]{:S(2)}) copy-start(f32[1,128,2048]{2,1,0:T(8,128)} %get-tuple-element.21) | copy-start | bytes 3145732
  164.5 2.2 %collective-permute-start.3 = (bf16[128,2048]{1,0:T(8,128)(2,1)}, bf16[128,2048]{1,0:T(8,128)(2,1)S(1)}, u32[]{:S(2)}, u32[]{:S(2)}) collective-permute-start(bf16[128,2048]{1,0:T(8,128)(2,1)} %bitcast.70), channel_id=1, source_target_pairs={{0,64},{64,0},{1,65},{65,1},{2,66},{66,2},{3,67},{67,3},{4,68},{68... | collective-permute-start | bytes 1572872 | tf_op jit(solution)/shard_map/ppermute | solution.py:380
  164.7 2.3 %copy-start.2 = (f32[256,1024]{1,0:T(8,128)S(1)}, f32[256,1024]{1,0:T(8,128)}, u32[]{:S(2)}) copy-start(f32[256,1024]{1,0:T(8,128)} %add_add_fusion) | copy-start | bytes 3145732
  164.7 2.3 %dynamic-slice-start = ((f32[2048]{0:T(1024)}, s32[]{:T(128)}), f32[1024]{0:T(1024)S(1)}, s32[]{:S(2)}) async-start(f32[2048]{0:T(1024)} %param.26, s32[]{:T(128)} %select_n.59), calls=%async_computation.1 | async-start | bytes 8704 | tf_op jit(solution)/shard_map/dynamic_slice | solution.py:333
Sparse Core Ops, SparseCore 0:
  10.9 121.5 all-gather.1

commit v5 on v1

--- a/solution.py
+++ b/solution.py
@@ -305,9 +305,26 @@
     )
     slot_pages = every_slot.reshape(-1, PAGE_TOKENS, 2 * HEAD_SIZE)
     heads_rows = PAGE_TOKENS * heads
+    kv_index = lax.axis_index("kv")
+    model_width = tokens.shape[1]
+    half_width = model_width // lax.axis_size("kv")
+
+    def columns(source):
+        return lax.dynamic_slice_in_dim(source, kv_index * half_width, half_width, source.ndim - 1)
+
+    low_rank = jnp.dot(normed, laurel_left, preferred_element_type=jnp.float32).astype(jnp.bfloat16)
+    laurel_full = jnp.dot(low_rank, laurel_right, preferred_element_type=jnp.float32)
+    laurel = columns(normed).astype(jnp.float32) + columns(laurel_full) * rms_scale(
+        laurel_full
+    ) * columns(laurel_gain)
+    resident = columns(tokens).astype(jnp.float32) + laurel
+    flat_queries = page_queries.reshape(pages_here, heads_rows, HEAD_SIZE)
+    resident, suffix_key_cache, suffix_value_cache, flat_queries = lax.optimization_barrier(
+        (resident, suffix_key_cache, suffix_value_cache, flat_queries)
+    )
     attended = page_attention(
         chosen,
-        page_queries.reshape(pages_here, heads_rows, HEAD_SIZE),
+        flat_queries,
         jnp.repeat(page_requests, heads, axis=1)[..., None],
         jnp.repeat(page_positions, heads, axis=1)[..., None],
         key_requests[None, :],
@@ -317,25 +334,10 @@
         slot_pages,
     ).reshape(tok_count, -1)
     attn_part = jnp.dot(attended, w_out, preferred_element_type=jnp.float32)
-    kv_index = lax.axis_index("kv")
-    model_width = tokens.shape[1]
-    half_width = model_width // lax.axis_size("kv")
-
-    def columns(source):
-        return lax.dynamic_slice_in_dim(source, kv_index * half_width, half_width, source.ndim - 1)
-
     partner_part = lax.ppermute(attn_part.astype(jnp.bfloat16), "kv", [(0, 1), (1, 0)])
     summed_out = attn_part + partner_part.astype(jnp.float32)
-    low_rank = jnp.dot(normed, laurel_left, preferred_element_type=jnp.float32).astype(jnp.bfloat16)
-    laurel_full = jnp.dot(low_rank, laurel_right, preferred_element_type=jnp.float32)
-    attn_half = columns(summed_out)
-    attn_branch = attn_half * rms_scale(summed_out) * columns(post_gain)
-    laurel = columns(normed).astype(jnp.float32) + columns(laurel_full) * rms_scale(
-        laurel_full
-    ) * columns(laurel_gain)
-    layer_out = (
-        (columns(tokens).astype(jnp.float32) + attn_branch + laurel) * 2.0 ** (-0.5)
-    ).astype(jnp.bfloat16)
+    attn_branch = columns(summed_out) * rms_scale(summed_out) * columns(post_gain)
+    layer_out = ((resident + attn_branch) * 2.0 ** (-0.5)).astype(jnp.bfloat16)
     return (layer_out, suffix_key_cache, suffix_value_cache)
 
 

time: 171 us -> 166 us (0.971)
  waiting for transfers between devices: 80.7 us -> 57.6 us
  other arithmetic: 17 us -> 31.3 us
  local copies, waits for them, and re-layouts: 9.2 us -> 14.8 us
    all_gather x1, waiting for transfers between devices: 70.8 us -> 46.4 us  [local(): every_slot = lax.all_gather(prefix_both, 'page', axis=0, tiled=True)]
    unnamed x10, other arithmetic: 0.06 us -> 7.23 us
    add x0 -> x1, other arithmetic: none -> 2.53 us  [local(): resident = columns(tokens).astype(jnp.float32) + laurel]
    ppermute x1, waiting for transfers between devices: 0.01 us -> 2.29 us  [local(): lax.ppermute(attn_part.astype(jnp.bfloat16), 'kv', [(0, 1), (1, 0)])]
    dot_general x1, matrix products: 5.26 us -> 3.44 us  [local(): attn_part = jnp.dot(attended, w_out, preferred_element_type=jnp.float32)]
    reduce_sum x3, other arithmetic: 3.96 us -> 2.21 us  [rms_scale(): jnp.mean(values * values, axis=-1, keepdims=True) + epsilon]
  transfers between devices with their start and end apart: 5 -> 5, of which waited for: 2 -> 3; matrix products, arithmetic and copies ran while one was open for 16% -> 29% of each run, Pallas kernels for 0% -> 0%
where the time goes in v5:
time: 166 us; the launch traced here: 165 us
  waiting for transfers between devices  57.6 us (35%)
  other arithmetic  31.3 us (19%)
  Pallas kernels  20.8 us (13%)
  local copies, waits for them, and re-layouts  14.8 us (9%)
  between operations  14.5 us (9%)
  matrix products  13.2 us (8%)
  starting transfers between devices  13 us (8%)
    all_gather x1, waiting for transfers between devices, local(): every_slot = lax.all_gather(prefix_both, 'page', axis=0, tiled=True)  46.4 us
    pallas_call x1, Pallas kernels, page_attention(): pl.pallas_call(page_attention_kernel, grid_spec=grid_spec, out_shape=jax....  20.8 us
    ppermute x3, starting transfers between devices, passed_along(): return lax.ppermute(block, axis, route)  12.4 us
    ppermute x3, waiting for transfers between devices, passed_along(): return lax.ppermute(block, axis, route)  8.89 us
    unnamed x10, other arithmetic  7.23 us
    dot_general x1, matrix products, project(): jnp.dot(normed, w_query, preferred_element_type=jnp.float32)  4.43 us
    dot_general x1, matrix products, local(): attn_part = jnp.dot(attended, w_out, preferred_element_type=jnp.float32)  3.44 us
  transfers between devices with their start and end apart: 5, of which 3 were waited for; matrix products, arithmetic and copies ran while one was open for 29% of the time, Pallas kernels for 0%

profile of v5, /device:TPU:1, one launch (start us, length us, event | category | flops | bytes accessed | tf_op | source)
XLA Modules:
  0.0 165.1 jit_solution(3991906076128871026)
XLA Ops:
  7.2 1.8 %pad_maximum_fusion.6 = bf16[256,512]{1,0:T(8,128)(2,1)} fusion(bf16[256,256]{1,0:T(8,128)(2,1)} %param.31, bf16[256,256]{1,0:T(8,128)(2,1)} %param.30), kind=kLoop, calls=%fused_computation.24 | loop fusion | flops 524288 | bytes 524288 | tf_op jit(solution)/shard_map/concatenate | solution.py:248
  9.1 0.7 copy.46
  10.0 0.7 sub.120
  10.7 1.5 fusion
  12.2 1.0 fusion.2
  13.8 0.8 copy.45
  15.5 0.8 select_reduce_fusion
  16.3 1.1 multiply_bitcast_fusion
  18.0 0.7 pad_maximum_fusion.5
  18.8 4.6 %collective-permute-start = (bf16[256,512]{1,0:T(8,128)(2,1)}, bf16[256,512]{1,0:T(8,128)(2,1)}, u32[]{:S(2)}, u32[]{:S(2)}) collective-permute-start(bf16[256,512]{1,0:T(8,128)(2,1)} %pad_maximum_fusion.5), channel_id=1, source_target_pairs={{0,1},{1,2},{2,3},{3,4},{4,5},{5,6},{6,7},{7,8},{8,9},{9,10},{10,1... | collective-permute-start | bytes 786440 | tf_op jit(solution)/shard_map/ppermute | solution.py:24
  23.4 3.2 %collective-permute-start.2 = (bf16[256,512]{1,0:T(8,128)(2,1)}, bf16[256,512]{1,0:T(8,128)(2,1)}, u32[]{:S(2)}, u32[]{:S(2)}) collective-permute-start(bf16[256,512]{1,0:T(8,128)(2,1)} %pad_maximum_fusion.5), channel_id=1, source_target_pairs={{0,4},{1,5},{2,6},{3,7},{4,8},{5,9},{6,10},{7,11},{8,12},{9,13},{1... | collective-permute-start | bytes 786440 | tf_op jit(solution)/shard_map/ppermute | solution.py:24
  26.6 0.7 reshape_reshape.2
  27.3 4.4 %fusion.28 = f32[256,1024]{1,0:T(8,128)} fusion(bf16[256,2048]{1,0:T(8,128)(2,1)S(1)} %fusion.2, bf16[2048,1024]{1,0:T(8,128)(2,1)} %param.20), kind=kOutput, calls=%fused_computation.128 | convolution fusion | flops 1073741824 | bytes 6291456 | tf_op jit(solution)/shard_map/dot_general | solution.py:58
  31.7 1.7 %reshape.389 = f32[256,4,256]{2,1,0:T(4,128)S(1)} reshape(f32[256,1024]{1,0:T(8,128)} %fusion.28) | data formatting | bytes 2097152 | tf_op jit(solution)/shard_map/reshape | solution.py:58
  33.5 0.7 convert_element_type.83
  34.2 1.3 and_reduce_fusion
  35.8 1.1 multiply_cosine_fusion
  36.9 1.0 multiply_multiply_fusion
  38.3 0.9 pad_maximum_fusion.1.q_ref
  40.3 2.7 %multiply_reduce_fusion.1 = (f32[256]{0:T(256)S(1)}, f32[256,2048]{1,0:T(8,128)}) fusion(bf16[64,2048]{1,0:T(8,128)(2,1)S(1)} %copy-done.7, bf16[256,2048]{1,0:T(8,128)(2,1)S(1)} %fusion.2, bf16[2048,64]{0,1:T(8,128)(2,1)S(1)} %copy-done.8), kind=kOutput, calls=%fused_computation.9 | convolution fusion | flops 135282432 | bytes 3671040 | tf_op jit(solution)/shard_map/dot_general | solution.py:316
  43.7 0.7 constant_dynamic-update-slice_fusion.7
  44.3 0.7 constant_dynamic-update-slice_fusion.5
  45.0 0.7 constant_dynamic-update-slice_fusion.3
  45.7 1.3 constant_dynamic-update-slice_fusion.8
  47.0 1.3 constant_dynamic-update-slice_fusion.6
  48.3 1.3 constant_dynamic-update-slice_fusion.4
  49.6 1.3 constant_dynamic-update-slice_fusion.2
  50.9 1.3 constant_dynamic-update-slice_fusion
  52.2 1.5 convolution_convert_fusion
  53.7 0.8 fusion.26
  55.1 0.7 dynamic_slice.21
  55.8 2.5 %add_add_fusion = f32[256,1024]{1,0:T(8,128)} fusion(f32[256,2048]{1,0:T(8,128)} %get-tuple-element.57, s32[]{:T(128)} %select_n.57, f32[1024]{0:T(1024)S(1)} %dynamic_slice.21, f32[256]{0:T(256)} %add_rsqrt_fusion.4, bf16[256,2048]{1,0:T(8,128)(2,1)S(1)} %fusion.2, bf16[256,2048]{1,0:T(8,128)(2,1)S(1)} %copy-done.4), kind=kLoop, calls=%fused_computation.16 | loop fusion | flops 1572864 | bytes 3150852 | tf_op jit(solution)/shard_map/add | solution.py:320
  58.4 1.8 %pad_maximum_fusion.2 = bf16[512,512]{1,0:T(8,128)(2,1)} fusion(bf16[256,512]{1,0:T(8,128)(2,1)} %collective-permute-done, bf16[256,256]{1,0:T(8,128)(2,1)S(1)} %multiply_convert_fusion.1, bf16[256,128]{1,0:T(8,128)(2,1)S(1)} %bitcast.38, bf16[256,128]{1,0:T(8,128)(2,1)S(1)} %bitcast.35), kind=kLoop, calls=%fused_computation.18 | loop fusion | flops 2097152 | bytes 1048576 | tf_op jit(solution)/shard_map/concatenate | solution.py:283
  60.2 4.5 %collective-permute-start.1 = (bf16[512,512]{1,0:T(8,128)(2,1)}, bf16[512,512]{1,0:T(8,128)(2,1)S(1)}, u32[]{:S(2)}, u32[]{:S(2)}) collective-permute-start(bf16[512,512]{1,0:T(8,128)(2,1)} %pad_maximum_fusion.2), channel_id=1, source_target_pairs={{0,2},{1,3},{2,4},{3,5},{4,6},{5,7},{6,8},{7,9},{8,10},{9,11},{10,... | collective-permute-start | bytes 1572872 | tf_op jit(solution)/shard_map/ppermute | solution.py:24
  64.8 1.6 reshape.387
  66.4 0.7 reshape.388
  67.2 0.8 broadcast_in_dim.17
  69.2 8.9 %collective-permute-done.1 = bf16[512,512]{1,0:T(8,128)(2,1)S(1)} collective-permute-done((bf16[512,512]{1,0:T(8,128)(2,1)}, bf16[512,512]{1,0:T(8,128)(2,1)S(1)}, u32[]{:S(2)}, u32[]{:S(2)}) %collective-permute-start.1) | collective-permute-done | bytes 524320 | tf_op jit(solution)/shard_map/ppermute | solution.py:24
  78.1 1.1 pad_maximum_fusion
  79.3 46.4 %all-gather.2.cloned.1.call-done = bf16[16384,512]{1,0:T(8,128)(2,1)} async-done(((bf16[256,512]{1,0:T(8,128)(2,1)}), bf16[16384,512]{1,0:T(8,128)(2,1)}) %all-gather.2.cloned.1.call-update) | async-done | bytes 16777232 | tf_op jit(solution)/shard_map/all_gather | solution.py:249
  125.7 1.0 copy-done.1
  126.8 20.8 %shard_map.193 = bf16[2,512,256]{2,1,0:T(8,128)(2,1)S(1)} custom-call(s32[2,32]{1,0:T(2,128)S(1)} %broadcast_select_fusion.table_ref, bf16[2,512,256]{2,1,0:T(8,128)(2,1)S(1)} %copy-done.1, s32[2,512,1]{2,1,0:T(8,128)S(1)} %broadcast_in_dim_reshape.8.row_req_ref, s32[2,512,1]{2,1,0:T(8,128)S(1)} %broadcast_in_dim_reshape.9.row_pos_ref, ...), custom_call_target="tpu_custom_call" | custom-call | flops 5637144576 | bytes 9437184 | tf_op jit(solution)/shard_map/pallas_call | solution.py:211
  147.5 0.8 copy-done.2
  148.3 1.4 reshape.393
  149.7 3.4 %fusion.27 = (bf16[256,2048]{1,0:T(8,128)(2,1)S(1)}, f32[256,2048]{1,0:T(8,128)S(1)}) fusion(bf16[256,1024]{1,0:T(8,128)(2,1)S(1)} %reshape.393, bf16[1024,2048]{1,0:T(8,128)(2,1)} %param.25), kind=kOutput, calls=%fused_computation.127 | convolution fusion | flops 1074266112 | bytes 7864320 | tf_op jit(solution)/shard_map/dot_general | solution.py:336
  153.7 2.3 %collective-permute-done.3 = bf16[256,2048]{1,0:T(8,128)(2,1)S(1)} collective-permute-done((bf16[256,2048]{1,0:T(8,128)(2,1)S(1)}, bf16[256,2048]{1,0:T(8,128)(2,1)S(1)}, u32[]{:S(2)}, u32[]{:S(2)}) %collective-permute-start.3) | collective-permute-done | bytes 1048608 | tf_op jit(solution)/shard_map/ppermute | solution.py:337
  156.4 0.9 copy-done.5
  157.2 1.0 multiply_convert_fusion
  (89 shorter events, 7.6 us)
Async XLA Ops:
  7.2 6.1 %copy-start = (bf16[2048,256]{1,0:T(8,128)(2,1)S(1)}, bf16[2048,256]{1,0:T(8,128)(2,1)}, u32[]{:S(2)}) copy-start(bf16[2048,256]{1,0:T(8,128)(2,1)} %param.21) | copy-start | bytes 3145732
  7.2 5.0 %copy-start.3 = (bf16[256,2048]{1,0:T(8,128)(2,1)S(1)}, bf16[256,2048]{1,0:T(8,128)(2,1)}, u32[]{:S(2)}) copy-start(bf16[256,2048]{1,0:T(8,128)(2,1)} %param.18) | copy-start | bytes 3145732
  7.2 118.5 %all-gather.2.cloned.1.call-start = ((), (), s32[]{:S(2)}) async-start(), calls=%async_computation | async-start | bytes 17039360 | tf_op jit(solution)/shard_map/all_gather | solution.py:249
  13.2 1.4 copy-start.6
  13.8 1.7 %copy-start.17 = (s32[32]{0:T(128)S(1)}, s32[32]{0:T(128)}, u32[]{:S(2)}) copy-start(s32[32]{0:T(128)} %param.34) | copy-start | bytes 388
  13.8 2.5 %copy-start.15 = (f32[256]{0:T(256)S(1)}, f32[256]{0:T(256)}, u32[]{:S(2)}) copy-start(f32[256]{0:T(256)} %param.24) | copy-start | bytes 3076
  15.4 16.3 %copy-start.14 = (f32[128]{0:T(128)}, f32[128]{0:T(128)S(1)}, u32[]{:S(2)}) copy-start(f32[128]{0:T(128)S(1)} %negate_power_fusion) | copy-start | bytes 1540
  18.8 39.6 %collective-permute-start = (bf16[256,512]{1,0:T(8,128)(2,1)}, bf16[256,512]{1,0:T(8,128)(2,1)}, u32[]{:S(2)}, u32[]{:S(2)}) collective-permute-start(bf16[256,512]{1,0:T(8,128)(2,1)} %pad_maximum_fusion.5), channel_id=1, source_target_pairs={{0,1},{1,2},{2,3},{3,4},{4,5},{5,6},{6,7},{7,8},{8,9},{9,10},{10,1... | collective-permute-start | bytes 786440 | tf_op jit(solution)/shard_map/ppermute | solution.py:24
  23.4 45.8 %collective-permute-start.2 = (bf16[256,512]{1,0:T(8,128)(2,1)}, bf16[256,512]{1,0:T(8,128)(2,1)}, u32[]{:S(2)}, u32[]{:S(2)}) collective-permute-start(bf16[256,512]{1,0:T(8,128)(2,1)} %pad_maximum_fusion.5), channel_id=1, source_target_pairs={{0,4},{1,5},{2,6},{3,7},{4,8},{5,9},{6,10},{7,11},{8,12},{9,13},{1... | collective-permute-start | bytes 786440 | tf_op jit(solution)/shard_map/ppermute | solution.py:24
  36.9 2.2 %copy-start.21 = (s32[2]{0:T(128)S(1)}, s32[2]{0:T(128)}, u32[]{:S(2)}) copy-start(s32[2]{0:T(128)} %param.35) | copy-start | bytes 28
  38.0 2.3 %copy-start.7 = (bf16[64,2048]{1,0:T(8,128)(2,1)S(1)}, bf16[64,2048]{1,0:T(8,128)(2,1)}, u32[]{:S(2)}) copy-start(bf16[64,2048]{1,0:T(8,128)(2,1)} %param.28) | copy-start | bytes 786436
  38.0 2.3 %copy-start.8 = (bf16[2048,64]{0,1:T(8,128)(2,1)S(1)}, bf16[2048,64]{0,1:T(8,128)(2,1)}, u32[]{:S(2)}) copy-start(bf16[2048,64]{0,1:T(8,128)(2,1)} %param.27) | copy-start | bytes 786436
  39.1 11.7 %copy-start.12 = (s32[256]{0:T(256)S(1)}, s32[256]{0:T(256)}, u32[]{:S(2)}) copy-start(s32[256]{0:T(256)} %get-tuple-element.12) | copy-start | bytes 3076
  39.2 13.0 %copy-start.9 = (bf16[2,32768]{1,0:T(2,128)(2,1)S(1)}, bf16[2,32768]{1,0:T(2,128)(2,1)}, u32[]{:S(2)}) copy-start(bf16[2,32768]{1,0:T(2,128)(2,1)} %reshape_reshape.2) | copy-start | bytes 393220
  43.1 11.5 %copy-start.16 = (s32[256]{0:T(256)S(1)}, s32[256]{0:T(256)}, u32[]{:S(2)}) copy-start(s32[256]{0:T(256)} %get-tuple-element.29) | copy-start | bytes 3076
  43.1 12.8 %copy-start.4 = (bf16[256,2048]{1,0:T(8,128)(2,1)S(1)}, bf16[256,2048]{1,0:T(8,128)(2,1)}, u32[]{:S(2)}) copy-start(bf16[256,2048]{1,0:T(8,128)(2,1)} %param.18) | copy-start | bytes 3145732
  55.8 8.9 %copy-start.13 = (s32[256]{0:T(256)S(1)}, s32[256]{0:T(256)}, u32[]{:S(2)}) copy-start(s32[256]{0:T(256)} %get-tuple-element.11) | copy-start | bytes 3076
  55.8 8.9 %copy-start.20 = (s32[2]{0:T(128)S(1)}, s32[2]{0:T(128)}, u32[]{:S(2)}) copy-start(s32[2]{0:T(128)} %fusion.22) | copy-start | bytes 28
  55.8 11.3 %copy-start.10 = (s32[1280]{0:T(1024)S(1)}, s32[1280]{0:T(1024)}, u32[]{:S(2)}) copy-start(s32[1280]{0:T(1024)} %constant_dynamic-update-slice_fusion) | copy-start | bytes 15364
  58.4 9.8 %copy-start.11 = (s32[2,128]{1,0:T(2,128)S(1)}, s32[2,128]{1,0:T(2,128)}, u32[]{:S(2)}) copy-start(s32[2,128]{1,0:T(2,128)} %bitcast_subtract_fusion) | copy-start | bytes 3076
  58.4 10.1 %copy-start.18 = (s32[128]{0:T(128)S(1)}, s32[128]{0:T(128)}, u32[]{:S(2)}) copy-start(s32[128]{0:T(128)} %param.32) | copy-start | bytes 1540
  58.4 10.7 %copy-start.19 = (pred[2]{0:T(512)(128)(4,1)S(1)}, pred[2]{0:T(512)(128)(4,1)}, u32[]{:S(2)}) copy-start(pred[2]{0:T(512)(128)(4,1)} %and_reduce_fusion) | copy-start | bytes 10
  60.2 17.9 %collective-permute-start.1 = (bf16[512,512]{1,0:T(8,128)(2,1)}, bf16[512,512]{1,0:T(8,128)(2,1)S(1)}, u32[]{:S(2)}, u32[]{:S(2)}) collective-permute-start(bf16[512,512]{1,0:T(8,128)(2,1)} %pad_maximum_fusion.2), channel_id=1, source_target_pairs={{0,2},{1,3},{2,4},{3,5},{4,6},{5,7},{6,8},{7,9},{8,10},{9,11},{10,... | collective-permute-start | bytes 1572872 | tf_op jit(solution)/shard_map/ppermute | solution.py:24
  125.7 1.0 copy-start.1
  147.5 0.8 copy-start.2
  153.1 2.9 %collective-permute-start.3 = (bf16[256,2048]{1,0:T(8,128)(2,1)S(1)}, bf16[256,2048]{1,0:T(8,128)(2,1)S(1)}, u32[]{:S(2)}, u32[]{:S(2)}) collective-permute-start(bf16[256,2048]{1,0:T(8,128)(2,1)S(1)} %get-tuple-element.62), channel_id=1, source_target_pairs={{0,64},{64,0},{1,65},{65,1},{2,66},{66,2},{3,67},{67,3},{4,68},{68... | collective-permute-start | bytes 3145736 | tf_op jit(solution)/shard_map/ppermute | solution.py:337
  156.0 1.2 copy-start.5
  156.0 1.2 dynamic-slice-start
Sparse Core Ops, SparseCore 0:
  10.9 114.8 all-gather.1

commit v6 on v5

--- a/solution.py
+++ b/solution.py
@@ -172,7 +172,7 @@
                 suffix_weights.astype(jnp.bfloat16), suffix_values_ref[...],
                 preferred_element_type=jnp.float32,
             )
-            out_ref[0, r : r + chunk, :] = (mixture / row_total).astype(out_ref.dtype)
+            out_ref[0, :, r * 2 : r * 2 + HEAD_SIZE] = (mixture / row_total).astype(out_ref.dtype)
 
 
 def page_attention(table, q, row_req, row_pos, key_req, key_pos, suffix_keys, suffix_values, slot_pages):
@@ -199,7 +199,7 @@
             pl.BlockSpec((suffix_rows, HEAD_SIZE), lambda p, j, t: (0, 0)),
         ]
         + [slot_spec(i) for i in range(PAGES_PER_STEP)],
-        out_specs=pl.BlockSpec((1, rows, HEAD_SIZE), lambda p, j, t: (p, 0, 0)),
+        out_specs=pl.BlockSpec((1, PAGE_TOKENS, rows // PAGE_TOKENS * HEAD_SIZE), lambda p, j, t: (p, 0, 0)),
         scratch_shapes=[
             pltpu.VMEM((rows, PREFIX_PAGES * PAGE_TOKENS), jnp.float32),
             pltpu.VMEM((PREFIX_PAGES * PAGE_TOKENS, HEAD_SIZE), jnp.bfloat16),
@@ -211,7 +211,7 @@
     return pl.pallas_call(
         page_attention_kernel,
         grid_spec=grid_spec,
-        out_shape=jax.ShapeDtypeStruct((pages, rows, HEAD_SIZE), jnp.bfloat16),
+        out_shape=jax.ShapeDtypeStruct((pages, PAGE_TOKENS, rows // PAGE_TOKENS * HEAD_SIZE), jnp.bfloat16),
         compiler_params=pltpu.CompilerParams(
             dimension_semantics=("arbitrary", "arbitrary"), vmem_limit_bytes=48 * 1024 * 1024
         ),
@@ -318,15 +318,15 @@
         laurel_full
     ) * columns(laurel_gain)
     resident = columns(tokens).astype(jnp.float32) + laurel
-    flat_queries = page_queries.reshape(pages_here, heads_rows, HEAD_SIZE)
+    flat_queries = jnp.swapaxes(page_queries, 1, 2).reshape(pages_here, heads_rows, HEAD_SIZE)
     resident, suffix_key_cache, suffix_value_cache, flat_queries = lax.optimization_barrier(
         (resident, suffix_key_cache, suffix_value_cache, flat_queries)
     )
     attended = page_attention(
         chosen,
         flat_queries,
-        jnp.repeat(page_requests, heads, axis=1)[..., None],
-        jnp.repeat(page_positions, heads, axis=1)[..., None],
+        jnp.tile(page_requests, (1, heads))[..., None],
+        jnp.tile(page_positions, (1, heads))[..., None],
         key_requests[None, :],
         key_positions[None, :],
         suffix_keys,

time: 166 us -> 168 us (1.012)
  waiting for transfers between devices: 57.6 us -> 68.6 us
  other arithmetic: 31.3 us -> 21.3 us
    all_gather x1, waiting for transfers between devices: 46.4 us -> 56.5 us  [local(): every_slot = lax.all_gather(prefix_both, 'page', axis=0, tiled=True)]
    unnamed x10, other arithmetic: 7.23 us -> 0.06 us
    dot_general x1, matrix products: 3.44 us -> 1.28 us  [local(): attn_part = jnp.dot(attended, w_out, preferred_element_type=jnp.float32)]
    reduce_sum x3, other arithmetic: 2.21 us -> 4.1 us  [rms_scale(): jnp.mean(values * values, axis=-1, keepdims=True) + epsilon]
  transfers between devices with their start and end apart: 5 -> 5, of which waited for: 3 -> 3; matrix products, arithmetic and copies ran while one was open for 29% -> 26% of each run, Pallas kernels for 0% -> 0%
where the time goes in v6:
time: 168 us; the launch traced here: 167 us
  waiting for transfers between devices  68.6 us (41%)
  other arithmetic  21.3 us (13%)
  Pallas kernels  21 us (12%)
  local copies, waits for them, and re-layouts  15 us (9%)
  between operations  14.5 us (9%)
  starting transfers between devices  13.6 us (8%)
  matrix products  13.4 us (8%)
    all_gather x1, waiting for transfers between devices, local(): every_slot = lax.all_gather(prefix_both, 'page', axis=0, tiled=True)  56.5 us
    pallas_call x1, Pallas kernels, page_attention(): pl.pallas_call(page_attention_kernel, grid_spec=grid_spec, out_shape=jax....  21 us
    ppermute x3, starting transfers between devices, passed_along(): return lax.ppermute(block, axis, route)  12.6 us
    ppermute x3, waiting for transfers between devices, passed_along(): return lax.ppermute(block, axis, route)  9.82 us
    dot_general x1, matrix products, project(): jnp.dot(normed, w_query, preferred_element_type=jnp.float32)  4.5 us
    reduce_sum x3, other arithmetic, rms_scale(): jnp.mean(values * values, axis=-1, keepdims=True) + epsilon  4.1 us
    dot_general x1, matrix products, local(): jnp.dot(low_rank, laurel_right, preferred_element_type=jnp.float32)  3.76 us
  transfers between devices with their start and end apart: 5, of which 3 were waited for; matrix products, arithmetic and copies ran while one was open for 26% of the time, Pallas kernels for 0%

profile of v6, /device:TPU:1, one launch (start us, length us, event | category | flops | bytes accessed | tf_op | source)
XLA Modules:
  0.0 167.4 jit_solution(17507331813211267424)
XLA Ops:
  7.2 1.8 %pad_maximum_fusion.5 = bf16[256,512]{1,0:T(8,128)(2,1)} fusion(bf16[256,256]{1,0:T(8,128)(2,1)} %param.31, bf16[256,256]{1,0:T(8,128)(2,1)} %param.30), kind=kLoop, calls=%fused_computation.25 | loop fusion | flops 524288 | bytes 524288 | tf_op jit(solution)/shard_map/concatenate | solution.py:248
  9.1 0.7 copy.55
  10.0 0.7 sub.129
  10.7 1.5 fusion
  12.2 1.0 fusion.2
  13.2 0.5 multiply_reduce_fusion.4
  13.8 0.8 copy.54
  14.6 1.8 %multiply_reduce_fusion.3 = (f32[256]{0:T(256)S(1)}, f32[256,256]{0,1:T(8,128)S(1)}) fusion(bf16[256,2048]{1,0:T(8,128)(2,1)S(1)} %fusion.2, bf16[2048,256]{1,0:T(8,128)(2,1)} %param.22), kind=kOutput, calls=%fused_computation.27 | convolution fusion | flops 268566272 | bytes 2360320 | tf_op jit(solution)/shard_map/dot_general | solution.py:68
  16.4 0.8 copy.56
  17.4 0.2 select_reduce_fusion
  17.6 1.0 multiply_bitcast_fusion
  18.6 0.6 fusion.11
  19.2 1.1 multiply_convert_fusion.1
  20.3 0.7 pad_maximum_fusion.4
  21.1 4.6 %collective-permute-start = (bf16[256,512]{1,0:T(8,128)(2,1)}, bf16[256,512]{1,0:T(8,128)(2,1)}, u32[]{:S(2)}, u32[]{:S(2)}) collective-permute-start(bf16[256,512]{1,0:T(8,128)(2,1)} %pad_maximum_fusion.4), channel_id=1, source_target_pairs={{0,1},{1,2},{2,3},{3,4},{4,5},{5,6},{6,7},{7,8},{8,9},{9,10},{10,1... | collective-permute-start | bytes 786440 | tf_op jit(solution)/shard_map/ppermute | solution.py:24
  25.7 3.2 %collective-permute-start.2 = (bf16[256,512]{1,0:T(8,128)(2,1)}, bf16[256,512]{1,0:T(8,128)(2,1)}, u32[]{:S(2)}, u32[]{:S(2)}) collective-permute-start(bf16[256,512]{1,0:T(8,128)(2,1)} %pad_maximum_fusion.4), channel_id=1, source_target_pairs={{0,4},{1,5},{2,6},{3,7},{4,8},{5,9},{6,10},{7,11},{8,12},{9,13},{1... | collective-permute-start | bytes 786440 | tf_op jit(solution)/shard_map/ppermute | solution.py:24
  28.9 0.7 reshape_reshape.4
  29.6 4.5 %fusion.29 = f32[256,1024]{1,0:T(8,128)} fusion(bf16[256,2048]{1,0:T(8,128)(2,1)S(1)} %fusion.2, bf16[2048,1024]{1,0:T(8,128)(2,1)} %param.20), kind=kOutput, calls=%fused_computation.129 | convolution fusion | flops 1073741824 | bytes 6291456 | tf_op jit(solution)/shard_map/dot_general | solution.py:58
  34.1 2.7 %reshape.421 = f32[256,4,256]{2,1,0:T(4,128)} reshape(f32[256,1024]{1,0:T(8,128)} %fusion.29) | data formatting | bytes 2097152 | tf_op jit(solution)/shard_map/reshape | solution.py:58
  36.8 2.2 %multiply_reduce_fusion.2 = f32[256,4]{1,0:T(8,128)} fusion(f32[256,4,256]{2,1,0:T(4,128)} %reshape.421), kind=kLoop, calls=%fused_computation.16 | loop fusion | flops 523264 | bytes 1052672 | tf_op jit(solution)/shard_map/reduce_sum | solution.py:28
  39.1 1.0 copy.57
  40.0 0.7 pad_maximum_fusion.6
  40.7 1.6 convert_element_type.83
  42.4 0.5 multiply_cosine_fusion
  43.0 1.4 fusion.4
  44.6 0.9 maximum_bitcast_fusion
  45.5 3.8 %multiply_reduce_fusion.1 = (f32[256]{0:T(256)S(1)}, f32[256,2048]{1,0:T(8,128)}) fusion(bf16[64,2048]{1,0:T(8,128)(2,1)} %param.28, bf16[256,2048]{1,0:T(8,128)(2,1)S(1)} %fusion.2, bf16[2048,64]{0,1:T(8,128)(2,1)} %param.27), kind=kOutput, calls=%fused_computation.9 | convolution fusion | flops 135282432 | bytes 3671040 | tf_op jit(solution)/shard_map/dot_general | solution.py:316
  49.4 1.6 convolution_convert_fusion
  50.9 0.9 fusion.27
  52.0 2.5 %add_add_fusion = f32[256,1024]{1,0:T(8,128)} fusion(f32[256,2048]{1,0:T(8,128)} %get-tuple-element.57, s32[]{:T(128)} %select_n.57, f32[1024]{0:T(1024)S(1)} %dynamic_slice.21, f32[256]{0:T(256)S(1)} %add_rsqrt_fusion.4, bf16[256,2048]{1,0:T(8,128)(2,1)S(1)} %fusion.2, bf16[256,2048]{1,0:T(8,128)(2,1)S(1)} %copy-done.2), kind=kLoop, calls=%fused_computation.17 | loop fusion | flops 1572864 | bytes 3150852 | tf_op jit(solution)/shard_map/add | solution.py:320
  54.5 1.1 pad_maximum_fusion.1
  55.6 4.8 %collective-permute-start.1 = (bf16[512,512]{1,0:T(8,128)(2,1)S(1)}, bf16[512,512]{1,0:T(8,128)(2,1)S(1)}, u32[]{:S(2)}, u32[]{:S(2)}) collective-permute-start(bf16[512,512]{1,0:T(8,128)(2,1)S(1)} %pad_maximum_fusion.1), channel_id=1, source_target_pairs={{0,2},{1,3},{2,4},{3,5},{4,6},{5,7},{6,8},{7,9},{8,10},{9,11},{10,... | collective-permute-start | bytes 1572872 | tf_op jit(solution)/shard_map/ppermute | solution.py:24
  60.5 0.7 reshape.419
  61.2 0.7 reshape.420
  62.0 0.3 tile.18.row_req_ref
  62.4 1.1 tile.19.row_pos_ref
  63.6 0.6 gather_fusion
  64.2 9.8 %collective-permute-done.1 = bf16[512,512]{1,0:T(8,128)(2,1)S(1)} collective-permute-done((bf16[512,512]{1,0:T(8,128)(2,1)S(1)}, bf16[512,512]{1,0:T(8,128)(2,1)S(1)}, u32[]{:S(2)}, u32[]{:S(2)}) %collective-permute-start.1) | collective-permute-done | bytes 524320 | tf_op jit(solution)/shard_map/ppermute | solution.py:24
  74.0 1.1 pad_maximum_fusion
  75.3 56.5 %all-gather.2.cloned.1.call-done = bf16[16384,512]{1,0:T(8,128)(2,1)} async-done(((bf16[256,512]{1,0:T(8,128)(2,1)}), bf16[16384,512]{1,0:T(8,128)(2,1)}) %all-gather.2.cloned.1.call-update) | async-done | bytes 16777232 | tf_op jit(solution)/shard_map/all_gather | solution.py:249
  131.7 1.0 copy-done.1
  132.8 21.0 %shard_map.193 = bf16[2,128,1024]{2,1,0:T(8,128)(2,1)S(1)} custom-call(s32[2,32]{1,0:T(2,128)S(1)} %broadcast_select_fusion.table_ref, bf16[2,512,256]{2,1,0:T(8,128)(2,1)S(1)} %bitcast.35, s32[2,512,1]{2,1,0:T(8,128)S(1)} %tile.18.row_req_ref, s32[2,512,1]{2,1,0:T(8,128)S(1)} %copy-done.1, s32[1,1280]{1,0:T(1,128)S(1)} %broadcast_in_dim.13.key_req_ref, ...), custom_call_target="tpu_custom_call" | custom-call | flops 5637144576 | bytes 9437184 | tf_op jit(solution)/shard_map/pallas_call | solution.py:211
  153.8 1.3 fusion.28
  155.1 0.9 collective-permute-start.3
  156.0 2.3 %collective-permute-done.3 = bf16[256,2048]{1,0:T(8,128)(2,1)S(1)} collective-permute-done((bf16[256,2048]{1,0:T(8,128)(2,1)S(1)}, bf16[256,2048]{1,0:T(8,128)(2,1)S(1)}, u32[]{:S(2)}, u32[]{:S(2)}) %collective-permute-start.3) | collective-permute-done | bytes 1048608 | tf_op jit(solution)/shard_map/ppermute | solution.py:337
  158.3 0.4 multiply_reduce_fusion
  158.7 0.9 copy-done.3
  159.5 1.0 multiply_convert_fusion
  (82 shorter events, 1.2 us)
Async XLA Ops:
  7.2 6.1 %copy-start = (bf16[2048,256]{1,0:T(8,128)(2,1)S(1)}, bf16[2048,256]{1,0:T(8,128)(2,1)}, u32[]{:S(2)}) copy-start(bf16[2048,256]{1,0:T(8,128)(2,1)} %param.21) | copy-start | bytes 3145732
  7.2 5.0 %copy-start.2 = (bf16[256,2048]{1,0:T(8,128)(2,1)S(1)}, bf16[256,2048]{1,0:T(8,128)(2,1)}, u32[]{:S(2)}) copy-start(bf16[256,2048]{1,0:T(8,128)(2,1)} %param.18) | copy-start | bytes 3145732
  7.2 124.5 %all-gather.2.cloned.1.call-start = ((), (), s32[]{:S(2)}) async-start(), calls=%async_computation | async-start | bytes 17039360 | tf_op jit(solution)/shard_map/all_gather | solution.py:249
  13.8 3.6 %copy-start.15 = (s32[32]{0:T(128)S(1)}, s32[32]{0:T(128)}, u32[]{:S(2)}) copy-start(s32[32]{0:T(128)} %param.34) | copy-start | bytes 388
  13.8 3.8 %copy-start.13 = (f32[256]{0:T(256)S(1)}, f32[256]{0:T(256)}, u32[]{:S(2)}) copy-start(f32[256]{0:T(256)} %param.24) | copy-start | bytes 3076
  19.2 35.3 %copy-start.8 = (bf16[256,1,128]{2,0,1:T(8,128)(2,1)}, bf16[256,1,128]{2,0,1:T(8,128)(2,1)S(1)}, u32[]{:S(2)}) copy-start(bf16[256,1,128]{2,0,1:T(8,128)(2,1)S(1)} %get-tuple-element.47) | copy-start | bytes 196612
  20.3 34.2 %copy-start.5 = (bf16[256,256]{1,0:T(8,128)(2,1)}, bf16[256,256]{1,0:T(8,128)(2,1)S(1)}, u32[]{:S(2)}) copy-start(bf16[256,256]{1,0:T(8,128)(2,1)S(1)} %multiply_convert_fusion.1) | copy-start | bytes 393220
  21.1 33.5 %collective-permute-start = (bf16[256,512]{1,0:T(8,128)(2,1)}, bf16[256,512]{1,0:T(8,128)(2,1)}, u32[]{:S(2)}, u32[]{:S(2)}) collective-permute-start(bf16[256,512]{1,0:T(8,128)(2,1)} %pad_maximum_fusion.4), channel_id=1, source_target_pairs={{0,1},{1,2},{2,3},{3,4},{4,5},{5,6},{6,7},{7,8},{8,9},{9,10},{10,1... | collective-permute-start | bytes 786440 | tf_op jit(solution)/shard_map/ppermute | solution.py:24
  25.7 38.5 %collective-permute-start.2 = (bf16[256,512]{1,0:T(8,128)(2,1)}, bf16[256,512]{1,0:T(8,128)(2,1)}, u32[]{:S(2)}, u32[]{:S(2)}) collective-permute-start(bf16[256,512]{1,0:T(8,128)(2,1)} %pad_maximum_fusion.4), channel_id=1, source_target_pairs={{0,4},{1,5},{2,6},{3,7},{4,8},{5,9},{6,10},{7,11},{8,12},{9,13},{1... | collective-permute-start | bytes 786440 | tf_op jit(solution)/shard_map/ppermute | solution.py:24
  34.1 8.9 %copy-start.14 = (f32[256]{0:T(256)S(1)}, f32[256]{0:T(256)}, u32[]{:S(2)}) copy-start(f32[256]{0:T(256)} %param.23) | copy-start | bytes 3076
  43.0 2.5 %copy-start.17 = (s32[2]{0:T(128)S(1)}, s32[2]{0:T(128)}, u32[]{:S(2)}) copy-start(s32[2]{0:T(128)} %param.35) | copy-start | bytes 28
  45.5 6.5 %copy-start.12 = (f32[2048]{0:T(1024)S(1)}, f32[2048]{0:T(1024)}, u32[]{:S(2)}) copy-start(f32[2048]{0:T(1024)} %param.29) | copy-start | bytes 24580
  51.9 8.5 %copy-start.7 = (bf16[2,4,128,256]{3,2,0,1:T(8,128)(2,1)S(1)}, bf16[2,4,128,256]{3,2,0,1:T(8,128)(2,1)}, u32[]{:S(2)}) copy-start(bf16[2,4,128,256]{3,2,0,1:T(8,128)(2,1)} %maximum_bitcast_fusion) | copy-start | bytes 1572868
  54.5 6.0 %copy-start.11 = (bf16[2,32768]{1,0:T(2,128)(2,1)S(1)}, bf16[2,32768]{1,0:T(2,128)(2,1)}, u32[]{:S(2)}) copy-start(bf16[2,32768]{1,0:T(2,128)(2,1)} %get-tuple-element.49) | copy-start | bytes 393220
  54.5 6.7 %copy-start.10 = (bf16[2,32768]{1,0:T(2,128)(2,1)S(1)}, bf16[2,32768]{1,0:T(2,128)(2,1)}, u32[]{:S(2)}) copy-start(bf16[2,32768]{1,0:T(2,128)(2,1)} %get-tuple-element.48) | copy-start | bytes 393220
  54.5 9.0 %copy-start.16 = (s32[128]{0:T(128)S(1)}, s32[128]{0:T(128)}, u32[]{:S(2)}) copy-start(s32[128]{0:T(128)} %param.32) | copy-start | bytes 1540
  55.6 18.4 %copy-start.6 = (bf16[256,256]{1,0:T(8,128)(2,1)S(1)}, bf16[256,256]{1,0:T(8,128)(2,1)}, u32[]{:S(2)}) copy-start(bf16[256,256]{1,0:T(8,128)(2,1)} %copy-done.5) | copy-start | bytes 393220
  55.6 18.4 %copy-start.9 = (bf16[256,1,128]{2,0,1:T(8,128)(2,1)S(1)}, bf16[256,1,128]{2,0,1:T(8,128)(2,1)}, u32[]{:S(2)}) copy-start(bf16[256,1,128]{2,0,1:T(8,128)(2,1)} %copy-done.8) | copy-start | bytes 196612
  55.6 18.4 %collective-permute-start.1 = (bf16[512,512]{1,0:T(8,128)(2,1)S(1)}, bf16[512,512]{1,0:T(8,128)(2,1)S(1)}, u32[]{:S(2)}, u32[]{:S(2)}) collective-permute-start(bf16[512,512]{1,0:T(8,128)(2,1)S(1)} %pad_maximum_fusion.1), channel_id=1, source_target_pairs={{0,2},{1,3},{2,4},{3,5},{4,6},{5,7},{6,8},{7,9},{8,10},{9,11},{10,... | collective-permute-start | bytes 1572872 | tf_op jit(solution)/shard_map/ppermute | solution.py:24
  131.7 1.0 copy-start.1
  132.8 21.0 %copy-start.4 = (bf16[1024,2048]{1,0:T(8,128)(2,1)S(1)}, bf16[1024,2048]{1,0:T(8,128)(2,1)}, u32[]{:S(2)}) copy-start(bf16[1024,2048]{1,0:T(8,128)(2,1)} %param.25) | copy-start | bytes 12582916
  155.1 3.2 %collective-permute-start.3 = (bf16[256,2048]{1,0:T(8,128)(2,1)S(1)}, bf16[256,2048]{1,0:T(8,128)(2,1)S(1)}, u32[]{:S(2)}, u32[]{:S(2)}) collective-permute-start(bf16[256,2048]{1,0:T(8,128)(2,1)S(1)} %get-tuple-element.62), channel_id=1, source_target_pairs={{0,64},{64,0},{1,65},{65,1},{2,66},{66,2},{3,67},{67,3},{4,68},{68... | collective-permute-start | bytes 3145736 | tf_op jit(solution)/shard_map/ppermute | solution.py:337
  158.3 1.2 copy-start.3
  158.3 1.2 dynamic-slice-start
Sparse Core Ops, SparseCore 0:
  10.9 120.7 all-gather.1

commit v7 on v5

--- a/solution.py
+++ b/solution.py
@@ -126,7 +126,7 @@
 ):
     slot_refs = rest[:PAGES_PER_STEP]
     out_ref = rest[PAGES_PER_STEP]
-    scores_buf, values_buf = rest[PAGES_PER_STEP + 1 :]
+    scores_buf, values_buf, stage_buf = rest[PAGES_PER_STEP + 1 :]
     step = pl.program_id(1)
     last = pl.num_programs(1) - 1
     contract_last = (((1,), (1,)), ((), ()))
@@ -172,7 +172,18 @@
                 suffix_weights.astype(jnp.bfloat16), suffix_values_ref[...],
                 preferred_element_type=jnp.float32,
             )
-            out_ref[0, r : r + chunk, :] = (mixture / row_total).astype(out_ref.dtype)
+            result = mixture / row_total
+            lanes = 128
+            halves = HEAD_SIZE // lanes
+            for c in range(halves):
+                stage_buf[c] = result[:, c * lanes : (c + 1) * lanes]
+            heads = out_ref.shape[2] // HEAD_SIZE
+            tokens_here = chunk // heads
+            for h in range(heads):
+                for c in range(halves):
+                    out_ref[0, pl.ds(r // heads, tokens_here), pl.ds(h * HEAD_SIZE + c * lanes, lanes)] = stage_buf[
+                        c, pl.ds(h, tokens_here, stride=heads), :
+                    ].astype(out_ref.dtype)
 
 
 def page_attention(table, q, row_req, row_pos, key_req, key_pos, suffix_keys, suffix_values, slot_pages):
@@ -199,10 +210,11 @@
             pl.BlockSpec((suffix_rows, HEAD_SIZE), lambda p, j, t: (0, 0)),
         ]
         + [slot_spec(i) for i in range(PAGES_PER_STEP)],
-        out_specs=pl.BlockSpec((1, rows, HEAD_SIZE), lambda p, j, t: (p, 0, 0)),
+        out_specs=pl.BlockSpec((1, PAGE_TOKENS, rows // PAGE_TOKENS * HEAD_SIZE), lambda p, j, t: (p, 0, 0)),
         scratch_shapes=[
             pltpu.VMEM((rows, PREFIX_PAGES * PAGE_TOKENS), jnp.float32),
             pltpu.VMEM((PREFIX_PAGES * PAGE_TOKENS, HEAD_SIZE), jnp.bfloat16),
+            pltpu.VMEM((HEAD_SIZE // 128, 128, 128), jnp.float32),
         ],
     )
     keys_total = PREFIX_PAGES * PAGE_TOKENS + suffix_rows
@@ -211,7 +223,7 @@
     return pl.pallas_call(
         page_attention_kernel,
         grid_spec=grid_spec,
-        out_shape=jax.ShapeDtypeStruct((pages, rows, HEAD_SIZE), jnp.bfloat16),
+        out_shape=jax.ShapeDtypeStruct((pages, PAGE_TOKENS, rows // PAGE_TOKENS * HEAD_SIZE), jnp.bfloat16),
         compiler_params=pltpu.CompilerParams(
             dimension_semantics=("arbitrary", "arbitrary"), vmem_limit_bytes=48 * 1024 * 1024
         ),

time: 166 us -> 168 us (1.012)
  waiting for transfers between devices: 57.6 us -> 75.3 us
  other arithmetic: 31.3 us -> 18.1 us
  matrix products: 13.2 us -> 11.1 us
  local copies, waits for them, and re-layouts: 14.8 us -> 13.1 us
    all_gather x1, waiting for transfers between devices: 46.4 us -> 59.7 us  [local(): every_slot = lax.all_gather(prefix_both, 'page', axis=0, tiled=True)]
    unnamed x10, other arithmetic: 7.23 us -> 0.06 us
    ppermute x3, waiting for transfers between devices: 8.89 us -> 13.4 us  [passed_along(): return lax.ppermute(block, axis, route)]
    dot_general x1, matrix products: 3.44 us -> 1.28 us  [local(): attn_part = jnp.dot(attended, w_out, preferred_element_type=jnp.float32)]
  transfers between devices with their start and end apart: 5 -> 5, of which waited for: 3 -> 3; matrix products, arithmetic and copies ran while one was open for 29% -> 21% of each run, Pallas kernels for 0% -> 0%
where the time goes in v7:
time: 168 us; the launch traced here: 167 us
  waiting for transfers between devices  75.3 us (45%)
  Pallas kernels  21.4 us (13%)
  other arithmetic  18.1 us (11%)
  between operations  14.6 us (9%)
  starting transfers between devices  13.5 us (8%)
  local copies, waits for them, and re-layouts  13.1 us (8%)
  matrix products  11.1 us (7%)
    all_gather x1, waiting for transfers between devices, local(): every_slot = lax.all_gather(prefix_both, 'page', axis=0, tiled=True)  59.7 us
    pallas_call x1, Pallas kernels, page_attention(): pl.pallas_call(page_attention_kernel, grid_spec=grid_spec, out_shape=jax....  21.4 us
    ppermute x3, waiting for transfers between devices, passed_along(): return lax.ppermute(block, axis, route)  13.4 us
    ppermute x3, starting transfers between devices, passed_along(): return lax.ppermute(block, axis, route)  12.5 us
    dot_general x1, matrix products, project(): jnp.dot(normed, w_query, preferred_element_type=jnp.float32)  4.43 us
  transfers between devices with their start and end apart: 5, of which 3 were waited for; matrix products, arithmetic and copies ran while one was open for 21% of the time, Pallas kernels for 0%

profile of v7, /device:TPU:1, one launch (start us, length us, event | category | flops | bytes accessed | tf_op | source)
XLA Modules:
  0.0 167.2 jit_solution(12521989590500685374)
XLA Ops:
  7.2 1.8 %pad_maximum_fusion.6 = bf16[256,512]{1,0:T(8,128)(2,1)} fusion(bf16[256,256]{1,0:T(8,128)(2,1)} %param.31, bf16[256,256]{1,0:T(8,128)(2,1)} %param.30), kind=kLoop, calls=%fused_computation.24 | loop fusion | flops 524288 | bytes 524288 | tf_op jit(solution)/shard_map/concatenate | solution.py:260
  9.1 0.7 copy.46
  10.0 0.7 sub.120
  10.7 1.5 fusion
  12.2 1.0 fusion.2
  13.3 0.5 multiply_reduce_fusion.4
  13.8 0.8 copy.45
  14.7 0.5 multiply_reduce_fusion.3
  15.2 0.1 copy.47
  15.5 0.2 select_reduce_fusion
  15.7 1.1 multiply_bitcast_fusion
  16.7 0.6 fusion.10
  17.5 0.7 pad_maximum_fusion.5
  18.2 4.6 %collective-permute-start = (bf16[256,512]{1,0:T(8,128)(2,1)}, bf16[256,512]{1,0:T(8,128)(2,1)}, u32[]{:S(2)}, u32[]{:S(2)}) collective-permute-start(bf16[256,512]{1,0:T(8,128)(2,1)} %pad_maximum_fusion.5), channel_id=1, source_target_pairs={{0,1},{1,2},{2,3},{3,4},{4,5},{5,6},{6,7},{7,8},{8,9},{9,10},{10,1... | collective-permute-start | bytes 786440 | tf_op jit(solution)/shard_map/ppermute | solution.py:24
  22.8 3.2 %collective-permute-start.2 = (bf16[256,512]{1,0:T(8,128)(2,1)}, bf16[256,512]{1,0:T(8,128)(2,1)}, u32[]{:S(2)}, u32[]{:S(2)}) collective-permute-start(bf16[256,512]{1,0:T(8,128)(2,1)} %pad_maximum_fusion.5), channel_id=1, source_target_pairs={{0,4},{1,5},{2,6},{3,7},{4,8},{5,9},{6,10},{7,11},{8,12},{9,13},{1... | collective-permute-start | bytes 786440 | tf_op jit(solution)/shard_map/ppermute | solution.py:24
  26.0 0.7 reshape_reshape.2
  26.7 4.4 %fusion.28 = f32[256,1024]{1,0:T(8,128)} fusion(bf16[256,2048]{1,0:T(8,128)(2,1)S(1)} %fusion.2, bf16[2048,1024]{1,0:T(8,128)(2,1)} %param.20), kind=kOutput, calls=%fused_computation.128 | convolution fusion | flops 1073741824 | bytes 6291456 | tf_op jit(solution)/shard_map/dot_general | solution.py:58
  31.2 1.7 %reshape.389 = f32[256,4,256]{2,1,0:T(4,128)S(1)} reshape(f32[256,1024]{1,0:T(8,128)} %fusion.28) | data formatting | bytes 2097152 | tf_op jit(solution)/shard_map/reshape | solution.py:58
  32.9 0.7 pad_maximum_fusion.7
  33.5 1.6 convert_element_type.83
  35.1 0.1 and_reduce_fusion
  35.2 0.3 multiply_reduce_fusion.2
  35.6 0.5 multiply_cosine_fusion
  36.2 0.3 multiply_multiply_fusion
  36.6 0.3 subtract_convert_fusion
  36.9 0.9 pad_maximum_fusion.1.q_ref
  37.7 2.7 %multiply_reduce_fusion.1 = (f32[256]{0:T(256)S(1)}, f32[256,2048]{1,0:T(8,128)}) fusion(bf16[64,2048]{1,0:T(8,128)(2,1)S(1)} %copy-done.11, bf16[256,2048]{1,0:T(8,128)(2,1)S(1)} %fusion.2, bf16[2048,64]{0,1:T(8,128)(2,1)S(1)} %copy-done.12), kind=kOutput, calls=%fused_computation.9 | convolution fusion | flops 135282432 | bytes 3671040 | tf_op jit(solution)/shard_map/dot_general | solution.py:328
  40.6 1.6 convolution_convert_fusion
  42.2 0.9 fusion.26
  43.3 2.5 %add_add_fusion = f32[256,1024]{1,0:T(8,128)} fusion(f32[256,2048]{1,0:T(8,128)} %get-tuple-element.57, s32[]{:T(128)} %select_n.57, f32[1024]{0:T(1024)S(1)} %dynamic_slice.21, f32[256]{0:T(256)S(1)} %add_rsqrt_fusion.4, bf16[256,2048]{1,0:T(8,128)(2,1)S(1)} %fusion.2, bf16[256,2048]{1,0:T(8,128)(2,1)S(1)} %copy-done.3), kind=kLoop, calls=%fused_computation.16 | loop fusion | flops 1572864 | bytes 3150852 | tf_op jit(solution)/shard_map/add | solution.py:332
  45.8 1.8 %pad_maximum_fusion.2 = bf16[512,512]{1,0:T(8,128)(2,1)} fusion(bf16[256,512]{1,0:T(8,128)(2,1)} %collective-permute-done, bf16[256,256]{1,0:T(8,128)(2,1)S(1)} %multiply_convert_fusion.1, bf16[256,128]{1,0:T(8,128)(2,1)S(1)} %bitcast.40, bf16[256,128]{1,0:T(8,128)(2,1)S(1)} %bitcast.37), kind=kLoop, calls=%fused_computation.18 | loop fusion | flops 2097152 | bytes 1048576 | tf_op jit(solution)/shard_map/concatenate | solution.py:295
  47.6 4.7 %collective-permute-start.1 = (bf16[512,512]{1,0:T(8,128)(2,1)}, bf16[512,512]{1,0:T(8,128)(2,1)S(1)}, u32[]{:S(2)}, u32[]{:S(2)}) collective-permute-start(bf16[512,512]{1,0:T(8,128)(2,1)} %pad_maximum_fusion.2), channel_id=1, source_target_pairs={{0,2},{1,3},{2,4},{3,5},{4,6},{5,7},{6,8},{7,9},{8,10},{9,11},{10,... | collective-permute-start | bytes 1572872 | tf_op jit(solution)/shard_map/ppermute | solution.py:24
  52.3 1.6 reshape.387
  53.9 1.6 reshape.388
  55.7 0.2 broadcast_in_dim_reshape.8.row_req_ref
  56.0 0.2 broadcast_in_dim_reshape.9.row_pos_ref
  56.3 0.6 gather_fusion
  56.9 13.4 %collective-permute-done.1 = bf16[512,512]{1,0:T(8,128)(2,1)S(1)} collective-permute-done((bf16[512,512]{1,0:T(8,128)(2,1)}, bf16[512,512]{1,0:T(8,128)(2,1)S(1)}, u32[]{:S(2)}, u32[]{:S(2)}) %collective-permute-start.1) | collective-permute-done | bytes 524320 | tf_op jit(solution)/shard_map/ppermute | solution.py:24
  70.3 1.1 pad_maximum_fusion
  71.5 59.7 %all-gather.2.cloned.1.call-done = bf16[16384,512]{1,0:T(8,128)(2,1)} async-done(((bf16[256,512]{1,0:T(8,128)(2,1)}), bf16[16384,512]{1,0:T(8,128)(2,1)}) %all-gather.2.cloned.1.call-update) | async-done | bytes 16777232 | tf_op jit(solution)/shard_map/all_gather | solution.py:261
  131.1 1.0 copy-done.1
  132.2 21.4 %shard_map.193 = bf16[2,128,1024]{2,1,0:T(8,128)(2,1)S(1)} custom-call(s32[2,32]{1,0:T(2,128)S(1)} %broadcast_select_fusion.table_ref, bf16[2,512,256]{2,1,0:T(8,128)(2,1)S(1)} %copy-done.1, s32[2,512,1]{2,1,0:T(8,128)S(1)} %broadcast_in_dim_reshape.8.row_req_ref, s32[2,512,1]{2,1,0:T(8,128)S(1)} %broadcast_in_dim_reshape.9.row_pos_ref, ...), custom_call_target="tpu_custom_call" | custom-call | flops 5637144576 | bytes 9437184 | tf_op jit(solution)/shard_map/pallas_call | solution.py:223
  153.6 1.3 fusion.27
  154.9 0.9 collective-permute-start.3
  155.8 2.3 %collective-permute-done.3 = bf16[256,2048]{1,0:T(8,128)(2,1)S(1)} collective-permute-done((bf16[256,2048]{1,0:T(8,128)(2,1)S(1)}, bf16[256,2048]{1,0:T(8,128)(2,1)S(1)}, u32[]{:S(2)}, u32[]{:S(2)}) %collective-permute-start.3) | collective-permute-done | bytes 1048608 | tf_op jit(solution)/shard_map/ppermute | solution.py:349
  158.1 0.4 multiply_reduce_fusion
  158.5 0.9 copy-done.4
  159.3 1.0 multiply_convert_fusion
  (82 shorter events, 1.2 us)
Async XLA Ops:
  7.2 6.1 %copy-start = (bf16[2048,256]{1,0:T(8,128)(2,1)S(1)}, bf16[2048,256]{1,0:T(8,128)(2,1)}, u32[]{:S(2)}) copy-start(bf16[2048,256]{1,0:T(8,128)(2,1)} %param.21) | copy-start | bytes 3145732
  7.2 5.0 %copy-start.2 = (bf16[256,2048]{1,0:T(8,128)(2,1)S(1)}, bf16[256,2048]{1,0:T(8,128)(2,1)}, u32[]{:S(2)}) copy-start(bf16[256,2048]{1,0:T(8,128)(2,1)} %param.18) | copy-start | bytes 3145732
  7.2 123.9 %all-gather.2.cloned.1.call-start = ((), (), s32[]{:S(2)}) async-start(), calls=%async_computation | async-start | bytes 17039360 | tf_op jit(solution)/shard_map/all_gather | solution.py:261
  13.2 1.4 copy-start.10
  13.8 1.6 copy-start.16
  13.8 1.9 %copy-start.14 = (f32[256]{0:T(256)S(1)}, f32[256]{0:T(256)}, u32[]{:S(2)}) copy-start(f32[256]{0:T(256)} %param.24) | copy-start | bytes 3076
  17.3 28.4 %copy-start.8 = (bf16[256,1,128]{2,0,1:T(8,128)(2,1)}, bf16[256,1,128]{2,0,1:T(8,128)(2,1)S(1)}, u32[]{:S(2)}) copy-start(bf16[256,1,128]{2,0,1:T(8,128)(2,1)S(1)} %get-tuple-element.47) | copy-start | bytes 196612
  17.4 28.3 %copy-start.6 = (bf16[256,256]{1,0:T(8,128)(2,1)}, bf16[256,256]{1,0:T(8,128)(2,1)S(1)}, u32[]{:S(2)}) copy-start(bf16[256,256]{1,0:T(8,128)(2,1)S(1)} %multiply_convert_fusion.1) | copy-start | bytes 393220
  18.2 27.6 %collective-permute-start = (bf16[256,512]{1,0:T(8,128)(2,1)}, bf16[256,512]{1,0:T(8,128)(2,1)}, u32[]{:S(2)}, u32[]{:S(2)}) collective-permute-start(bf16[256,512]{1,0:T(8,128)(2,1)} %pad_maximum_fusion.5), channel_id=1, source_target_pairs={{0,1},{1,2},{2,3},{3,4},{4,5},{5,6},{6,7},{7,8},{8,9},{9,10},{10,1... | collective-permute-start | bytes 786440 | tf_op jit(solution)/shard_map/ppermute | solution.py:24
  22.8 34.1 %collective-permute-start.2 = (bf16[256,512]{1,0:T(8,128)(2,1)}, bf16[256,512]{1,0:T(8,128)(2,1)}, u32[]{:S(2)}, u32[]{:S(2)}) collective-permute-start(bf16[256,512]{1,0:T(8,128)(2,1)} %pad_maximum_fusion.5), channel_id=1, source_target_pairs={{0,4},{1,5},{2,6},{3,7},{4,8},{5,9},{6,10},{7,11},{8,12},{9,13},{1... | collective-permute-start | bytes 786440 | tf_op jit(solution)/shard_map/ppermute | solution.py:24
  31.2 5.0 %copy-start.15 = (f32[256]{0:T(256)S(1)}, f32[256]{0:T(256)}, u32[]{:S(2)}) copy-start(f32[256]{0:T(256)} %param.23) | copy-start | bytes 3076
  36.2 1.5 copy-start.18
  36.5 1.2 copy-start.11
  36.6 1.2 copy-start.12
  37.7 5.5 %copy-start.13 = (f32[2048]{0:T(1024)S(1)}, f32[2048]{0:T(1024)}, u32[]{:S(2)}) copy-start(f32[2048]{0:T(1024)} %param.29) | copy-start | bytes 24580
  40.5 2.8 %copy-start.3 = (bf16[256,2048]{1,0:T(8,128)(2,1)S(1)}, bf16[256,2048]{1,0:T(8,128)(2,1)}, u32[]{:S(2)}) copy-start(bf16[256,2048]{1,0:T(8,128)(2,1)} %param.18) | copy-start | bytes 3145732
  45.8 10.4 %copy-start.17 = (s32[128]{0:T(128)S(1)}, s32[128]{0:T(128)}, u32[]{:S(2)}) copy-start(s32[128]{0:T(128)} %param.32) | copy-start | bytes 1540
  47.6 22.7 %copy-start.7 = (bf16[256,256]{1,0:T(8,128)(2,1)S(1)}, bf16[256,256]{1,0:T(8,128)(2,1)}, u32[]{:S(2)}) copy-start(bf16[256,256]{1,0:T(8,128)(2,1)} %copy-done.6) | copy-start | bytes 393220
  47.6 22.7 %copy-start.9 = (bf16[256,1,128]{2,0,1:T(8,128)(2,1)S(1)}, bf16[256,1,128]{2,0,1:T(8,128)(2,1)}, u32[]{:S(2)}) copy-start(bf16[256,1,128]{2,0,1:T(8,128)(2,1)} %copy-done.8) | copy-start | bytes 196612
  47.6 22.7 %collective-permute-start.1 = (bf16[512,512]{1,0:T(8,128)(2,1)}, bf16[512,512]{1,0:T(8,128)(2,1)S(1)}, u32[]{:S(2)}, u32[]{:S(2)}) collective-permute-start(bf16[512,512]{1,0:T(8,128)(2,1)} %pad_maximum_fusion.2), channel_id=1, source_target_pairs={{0,2},{1,3},{2,4},{3,5},{4,6},{5,7},{6,8},{7,9},{8,10},{9,11},{10,... | collective-permute-start | bytes 1572872 | tf_op jit(solution)/shard_map/ppermute | solution.py:24
  131.1 1.0 copy-start.1
  132.2 21.4 %copy-start.5 = (bf16[1024,2048]{1,0:T(8,128)(2,1)S(1)}, bf16[1024,2048]{1,0:T(8,128)(2,1)}, u32[]{:S(2)}) copy-start(bf16[1024,2048]{1,0:T(8,128)(2,1)} %param.25) | copy-start | bytes 12582916
  154.9 3.2 %collective-permute-start.3 = (bf16[256,2048]{1,0:T(8,128)(2,1)S(1)}, bf16[256,2048]{1,0:T(8,128)(2,1)S(1)}, u32[]{:S(2)}, u32[]{:S(2)}) collective-permute-start(bf16[256,2048]{1,0:T(8,128)(2,1)S(1)} %get-tuple-element.62), channel_id=1, source_target_pairs={{0,64},{64,0},{1,65},{65,1},{2,66},{66,2},{3,67},{67,3},{4,68},{68... | collective-permute-start | bytes 3145736 | tf_op jit(solution)/shard_map/ppermute | solution.py:349
  158.1 1.2 copy-start.4
  158.1 1.2 dynamic-slice-start
Sparse Core Ops, SparseCore 0:
  10.9 120.2 all-gather.1

commit v8 on v7

--- a/solution.py
+++ b/solution.py
@@ -331,14 +331,22 @@
     ) * columns(laurel_gain)
     resident = columns(tokens).astype(jnp.float32) + laurel
     flat_queries = page_queries.reshape(pages_here, heads_rows, HEAD_SIZE)
-    resident, suffix_key_cache, suffix_value_cache, flat_queries = lax.optimization_barrier(
-        (resident, suffix_key_cache, suffix_value_cache, flat_queries)
+    row_requests = jnp.repeat(page_requests, heads, axis=1)[..., None]
+    row_positions = jnp.repeat(page_positions, heads, axis=1)[..., None]
+    (
+        resident, suffix_key_cache, suffix_value_cache, flat_queries,
+        row_requests, row_positions, suffix_keys, suffix_values,
+    ) = lax.optimization_barrier(
+        (
+            resident, suffix_key_cache, suffix_value_cache, flat_queries,
+            row_requests, row_positions, suffix_keys, suffix_values,
+        )
     )
     attended = page_attention(
         chosen,
         flat_queries,
-        jnp.repeat(page_requests, heads, axis=1)[..., None],
-        jnp.repeat(page_positions, heads, axis=1)[..., None],
+        row_requests,
+        row_positions,
         key_requests[None, :],
         key_positions[None, :],
         suffix_keys,

time: 168 us -> 168 us (level)
  waiting for transfers between devices: 75.3 us -> 69.7 us
  other arithmetic: 18.1 us -> 21.2 us
    ppermute x3, waiting for transfers between devices: 13.4 us -> 10.5 us  [passed_along(): return lax.ppermute(block, axis, route)]
    all_gather x1, waiting for transfers between devices: 59.7 us -> 56.9 us  [local(): every_slot = lax.all_gather(prefix_both, 'page', axis=0, tiled=True)]
  transfers between devices with their start and end apart: 5 -> 5, of which waited for: 3 -> 3; matrix products, arithmetic and copies ran while one was open for 21% -> 25% of each run, Pallas kernels for 0% -> 0%
where the time goes in v8:
time: 168 us; the launch traced here: 167 us
  waiting for transfers between devices  69.7 us (41%)
  other arithmetic  21.2 us (13%)
  Pallas kernels  21 us (12%)
  between operations  14.6 us (9%)
  local copies, waits for them, and re-layouts  14.1 us (8%)
  starting transfers between devices  13.9 us (8%)
  matrix products  12.1 us (7%)
    all_gather x1, waiting for transfers between devices, local(): every_slot = lax.all_gather(prefix_both, 'page', axis=0, tiled=True)  56.9 us
    pallas_call x1, Pallas kernels, page_attention(): pl.pallas_call(page_attention_kernel, grid_spec=grid_spec, out_shape=jax....  21 us
    ppermute x3, starting transfers between devices, passed_along(): return lax.ppermute(block, axis, route)  12.9 us
    ppermute x3, waiting for transfers between devices, passed_along(): return lax.ppermute(block, axis, route)  10.5 us
    dot_general x1, matrix products, project(): jnp.dot(normed, w_query, preferred_element_type=jnp.float32)  4.43 us
    dot_general x1, matrix products, local(): jnp.dot(low_rank, laurel_right, preferred_element_type=jnp.float32)  3.77 us
  transfers between devices with their start and end apart: 5, of which 3 were waited for; matrix products, arithmetic and copies ran while one was open for 25% of the time, Pallas kernels for 0%

profile of v8, /device:TPU:1, one launch (start us, length us, event | category | flops | bytes accessed | tf_op | source)
XLA Modules:
  0.0 166.7 jit_solution(3278108785404643719)
XLA Ops:
  7.2 1.8 %pad_maximum_fusion.6 = bf16[256,512]{1,0:T(8,128)(2,1)} fusion(bf16[256,256]{1,0:T(8,128)(2,1)} %param.31, bf16[256,256]{1,0:T(8,128)(2,1)} %param.30), kind=kLoop, calls=%fused_computation.24 | loop fusion | flops 524288 | bytes 524288 | tf_op jit(solution)/shard_map/concatenate | solution.py:260
  9.1 0.7 copy.46
  10.0 0.7 sub.120
  10.7 1.5 fusion
  12.2 1.0 fusion.2
  13.2 0.5 multiply_reduce_fusion.4
  13.8 0.8 copy.45
  14.6 0.5 multiply_reduce_fusion.3
  15.4 0.8 select_reduce_fusion
  16.3 1.1 multiply_bitcast_fusion
  17.3 0.6 fusion.10
  18.0 0.7 pad_maximum_fusion.5
  18.7 4.6 %collective-permute-start = (bf16[256,512]{1,0:T(8,128)(2,1)}, bf16[256,512]{1,0:T(8,128)(2,1)}, u32[]{:S(2)}, u32[]{:S(2)}) collective-permute-start(bf16[256,512]{1,0:T(8,128)(2,1)} %pad_maximum_fusion.5), channel_id=1, source_target_pairs={{0,1},{1,2},{2,3},{3,4},{4,5},{5,6},{6,7},{7,8},{8,9},{9,10},{10,1... | collective-permute-start | bytes 786440 | tf_op jit(solution)/shard_map/ppermute | solution.py:24
  23.4 3.2 %collective-permute-start.2 = (bf16[256,512]{1,0:T(8,128)(2,1)}, bf16[256,512]{1,0:T(8,128)(2,1)}, u32[]{:S(2)}, u32[]{:S(2)}) collective-permute-start(bf16[256,512]{1,0:T(8,128)(2,1)} %pad_maximum_fusion.5), channel_id=1, source_target_pairs={{0,4},{1,5},{2,6},{3,7},{4,8},{5,9},{6,10},{7,11},{8,12},{9,13},{1... | collective-permute-start | bytes 786440 | tf_op jit(solution)/shard_map/ppermute | solution.py:24
  26.6 0.7 reshape_reshape.2
  27.3 4.4 %fusion.28 = f32[256,1024]{1,0:T(8,128)} fusion(bf16[256,2048]{1,0:T(8,128)(2,1)S(1)} %fusion.2, bf16[2048,1024]{1,0:T(8,128)(2,1)} %param.20), kind=kOutput, calls=%fused_computation.128 | convolution fusion | flops 1073741824 | bytes 6291456 | tf_op jit(solution)/shard_map/dot_general | solution.py:58
  31.7 1.7 %reshape.389 = f32[256,4,256]{2,1,0:T(4,128)S(1)} reshape(f32[256,1024]{1,0:T(8,128)} %fusion.28) | data formatting | bytes 2097152 | tf_op jit(solution)/shard_map/reshape | solution.py:58
  33.4 0.7 convert_element_type.83
  34.1 0.7 reshape.391
  34.9 0.8 fusion.22
  35.7 0.6 gather_fusion
  36.2 0.8 and_reduce_fusion
  37.0 1.0 multiply_reduce_fusion.2
  38.1 0.7 broadcast_subtract_fusion
  38.8 3.8 %multiply_reduce_fusion.1 = (f32[256]{0:T(256)S(1)}, f32[256,2048]{1,0:T(8,128)}) fusion(bf16[64,2048]{1,0:T(8,128)(2,1)} %param.28, bf16[256,2048]{1,0:T(8,128)(2,1)S(1)} %fusion.2, bf16[2048,64]{0,1:T(8,128)(2,1)} %param.27), kind=kOutput, calls=%fused_computation.9 | convolution fusion | flops 135282432 | bytes 3671040 | tf_op jit(solution)/shard_map/dot_general | solution.py:328
  42.8 0.9 add_rsqrt_fusion
  43.8 1.6 convolution_convert_fusion
  45.4 0.5 multiply_cosine_fusion
  45.9 0.3 multiply_multiply_fusion
  46.3 0.9 fusion.26
  47.2 0.3 subtract_convert_fusion
  47.5 1.9 %pad_maximum_fusion.2 = bf16[512,512]{1,0:T(8,128)(2,1)} fusion(bf16[256,512]{1,0:T(8,128)(2,1)} %collective-permute-done, bf16[256,256]{1,0:T(8,128)(2,1)S(1)} %multiply_convert_fusion.1, bf16[256,128]{1,0:T(8,128)(2,1)S(1)} %bitcast.40, bf16[256,128]{1,0:T(8,128)(2,1)S(1)} %bitcast.37), kind=kLoop, calls=%fused_computation.18 | loop fusion | flops 2097152 | bytes 1048576 | tf_op jit(solution)/shard_map/concatenate | solution.py:295
  49.3 5.1 %collective-permute-start.1 = (bf16[512,512]{1,0:T(8,128)(2,1)}, bf16[512,512]{1,0:T(8,128)(2,1)}, u32[]{:S(2)}, u32[]{:S(2)}) collective-permute-start(bf16[512,512]{1,0:T(8,128)(2,1)} %pad_maximum_fusion.2), channel_id=1, source_target_pairs={{0,2},{1,3},{2,4},{3,5},{4,6},{5,7},{6,8},{7,9},{8,10},{9,11},{10,... | collective-permute-start | bytes 1572872 | tf_op jit(solution)/shard_map/ppermute | solution.py:24
  54.5 1.7 reshape.387
  56.1 1.6 reshape.388
  58.3 2.6 %add_add_fusion = f32[256,1024]{1,0:T(8,128)} fusion(f32[256,2048]{1,0:T(8,128)} %get-tuple-element.65, s32[]{:T(128)} %select_n.57, f32[1024]{0:T(1024)S(1)} %dynamic_slice.21, f32[256]{0:T(256)S(1)} %add_rsqrt_fusion.4, bf16[256,2048]{1,0:T(8,128)(2,1)S(1)} %fusion.2, bf16[256,2048]{1,0:T(8,128)(2,1)} %param.18), kind=kLoop, calls=%fused_computation.16 | loop fusion | flops 1572864 | bytes 3150852 | tf_op jit(solution)/shard_map/add | solution.py:332
  60.9 10.5 %collective-permute-done.1 = bf16[512,512]{1,0:T(8,128)(2,1)} collective-permute-done((bf16[512,512]{1,0:T(8,128)(2,1)}, bf16[512,512]{1,0:T(8,128)(2,1)}, u32[]{:S(2)}, u32[]{:S(2)}) %collective-permute-start.1) | collective-permute-done | bytes 524320 | tf_op jit(solution)/shard_map/ppermute | solution.py:24
  71.4 1.3 pad_maximum_fusion
  73.0 1.0 copy.51.row_pos_ref
  74.1 56.9 %all-gather.2.cloned.1.call-done = bf16[16384,512]{1,0:T(8,128)(2,1)} async-done(((bf16[256,512]{1,0:T(8,128)(2,1)}), bf16[16384,512]{1,0:T(8,128)(2,1)}) %all-gather.2.cloned.1.call-update) | async-done | bytes 16777232 | tf_op jit(solution)/shard_map/all_gather | solution.py:261
  131.0 1.0 copy-done.1
  132.0 21.0 %shard_map.193 = bf16[2,128,1024]{2,1,0:T(8,128)(2,1)S(1)} custom-call(s32[2,32]{1,0:T(2,128)S(1)} %broadcast_select_fusion.table_ref, bf16[2,512,256]{2,1,0:T(8,128)(2,1)S(1)} %pad_maximum_fusion.1.q_ref, s32[2,512,1]{2,1,0:T(8,128)S(1)} %copy.50.row_req_ref, s32[2,512,1]{2,1,0:T(8,128)S(1)} %copy-done.1, s32[1,1280]{1,0:T(1,128)S(1)} %broadcast_in_dim.19.key_req_ref, ...), custom_call_target="tpu_custom_call" | custom-call | flops 5637144576 | bytes 9437184 | tf_op jit(solution)/shard_map/pallas_call | solution.py:223
  153.1 1.3 fusion.27
  154.4 0.9 collective-permute-start.3
  155.3 2.3 %collective-permute-done.3 = bf16[256,2048]{1,0:T(8,128)(2,1)S(1)} collective-permute-done((bf16[256,2048]{1,0:T(8,128)(2,1)S(1)}, bf16[256,2048]{1,0:T(8,128)(2,1)S(1)}, u32[]{:S(2)}, u32[]{:S(2)}) %collective-permute-start.3) | collective-permute-done | bytes 1048608 | tf_op jit(solution)/shard_map/ppermute | solution.py:357
  157.6 0.4 multiply_reduce_fusion
  158.0 0.9 copy-done.3
  158.8 1.0 multiply_convert_fusion
  (100 shorter events, 1.7 us)
Async XLA Ops:
  7.2 6.1 %copy-start = (bf16[2048,256]{1,0:T(8,128)(2,1)S(1)}, bf16[2048,256]{1,0:T(8,128)(2,1)}, u32[]{:S(2)}) copy-start(bf16[2048,256]{1,0:T(8,128)(2,1)} %param.21) | copy-start | bytes 3145732
  7.2 5.0 %copy-start.2 = (bf16[256,2048]{1,0:T(8,128)(2,1)S(1)}, bf16[256,2048]{1,0:T(8,128)(2,1)}, u32[]{:S(2)}) copy-start(bf16[256,2048]{1,0:T(8,128)(2,1)} %param.18) | copy-start | bytes 3145732
  7.2 123.8 %all-gather.2.cloned.1.call-start = ((), (), s32[]{:S(2)}) async-start(), calls=%async_computation | async-start | bytes 17039360 | tf_op jit(solution)/shard_map/all_gather | solution.py:261
  13.2 1.4 copy-start.5
  13.8 1.7 copy-start.26
  13.8 2.5 %copy-start.24 = (f32[256]{0:T(256)S(1)}, f32[256]{0:T(256)}, u32[]{:S(2)}) copy-start(f32[256]{0:T(256)} %param.24) | copy-start | bytes 3076
  15.3 16.3 %copy-start.21 = (f32[128]{0:T(128)}, f32[128]{0:T(128)S(1)}, u32[]{:S(2)}) copy-start(f32[128]{0:T(128)S(1)} %negate_power_fusion) | copy-start | bytes 1540
  18.7 28.7 %collective-permute-start = (bf16[256,512]{1,0:T(8,128)(2,1)}, bf16[256,512]{1,0:T(8,128)(2,1)}, u32[]{:S(2)}, u32[]{:S(2)}) collective-permute-start(bf16[256,512]{1,0:T(8,128)(2,1)} %pad_maximum_fusion.5), channel_id=1, source_target_pairs={{0,1},{1,2},{2,3},{3,4},{4,5},{5,6},{6,7},{7,8},{8,9},{9,10},{10,1... | collective-permute-start | bytes 786440 | tf_op jit(solution)/shard_map/ppermute | solution.py:24
  23.4 37.6 %collective-permute-start.2 = (bf16[256,512]{1,0:T(8,128)(2,1)}, bf16[256,512]{1,0:T(8,128)(2,1)}, u32[]{:S(2)}, u32[]{:S(2)}) collective-permute-start(bf16[256,512]{1,0:T(8,128)(2,1)} %pad_maximum_fusion.5), channel_id=1, source_target_pairs={{0,4},{1,5},{2,6},{3,7},{4,8},{5,9},{6,10},{7,11},{8,12},{9,13},{1... | collective-permute-start | bytes 786440 | tf_op jit(solution)/shard_map/ppermute | solution.py:24
  38.0 4.6 %copy-start.18 = (s32[256]{0:T(256)S(1)}, s32[256]{0:T(256)}, u32[]{:S(2)}) copy-start(s32[256]{0:T(256)} %get-tuple-element.41) | copy-start | bytes 3076
  38.0 4.6 %copy-start.17 = (s32[256]{0:T(256)S(1)}, s32[256]{0:T(256)}, u32[]{:S(2)}) copy-start(s32[256]{0:T(256)} %get-tuple-element.44) | copy-start | bytes 3076
  38.0 4.7 %copy-start.6 = (s32[1280]{0:T(1024)S(1)}, s32[1280]{0:T(1024)}, u32[]{:S(2)}) copy-start(s32[1280]{0:T(1024)} %custom-call.1) | copy-start | bytes 15364
  38.0 4.7 %copy-start.19 = (s32[256]{0:T(256)S(1)}, s32[256]{0:T(256)}, u32[]{:S(2)}) copy-start(s32[256]{0:T(256)} %get-tuple-element.36) | copy-start | bytes 3076
  38.0 4.7 %copy-start.20 = (s32[256]{0:T(256)S(1)}, s32[256]{0:T(256)}, u32[]{:S(2)}) copy-start(s32[256]{0:T(256)} %get-tuple-element.37) | copy-start | bytes 3076
  38.0 4.7 %copy-start.13 = (s32[256]{0:T(256)S(1)}, s32[256]{0:T(256)}, u32[]{:S(2)}) copy-start(s32[256]{0:T(256)} %get-tuple-element.39) | copy-start | bytes 3076
  38.0 4.7 %copy-start.14 = (s32[256]{0:T(256)S(1)}, s32[256]{0:T(256)}, u32[]{:S(2)}) copy-start(s32[256]{0:T(256)} %get-tuple-element.40) | copy-start | bytes 3076
  38.0 4.7 %copy-start.11 = (s32[256]{0:T(256)S(1)}, s32[256]{0:T(256)}, u32[]{:S(2)}) copy-start(s32[256]{0:T(256)} %get-tuple-element.42) | copy-start | bytes 3076
  38.1 4.7 %copy-start.12 = (s32[256]{0:T(256)S(1)}, s32[256]{0:T(256)}, u32[]{:S(2)}) copy-start(s32[256]{0:T(256)} %get-tuple-element.43) | copy-start | bytes 3076
  38.1 4.7 %copy-start.9 = (s32[256]{0:T(256)S(1)}, s32[256]{0:T(256)}, u32[]{:S(2)}) copy-start(s32[256]{0:T(256)} %get-tuple-element.45) | copy-start | bytes 3076
  38.1 4.7 %copy-start.10 = (s32[256]{0:T(256)S(1)}, s32[256]{0:T(256)}, u32[]{:S(2)}) copy-start(s32[256]{0:T(256)} %get-tuple-element.46) | copy-start | bytes 3076
  38.1 4.7 %copy-start.7 = (s32[256]{0:T(256)S(1)}, s32[256]{0:T(256)}, u32[]{:S(2)}) copy-start(s32[256]{0:T(256)} %get-tuple-element.20) | copy-start | bytes 3076
  38.1 4.7 %copy-start.8 = (s32[256]{0:T(256)S(1)}, s32[256]{0:T(256)}, u32[]{:S(2)}) copy-start(s32[256]{0:T(256)} %get-tuple-element.21) | copy-start | bytes 3076
  38.8 6.6 %copy-start.22 = (f32[128]{0:T(128)S(1)}, f32[128]{0:T(128)}, u32[]{:S(2)}) copy-start(f32[128]{0:T(128)} %copy-done.21) | copy-start | bytes 1540
  38.8 7.1 %copy-start.25 = (f32[256]{0:T(256)S(1)}, f32[256]{0:T(256)}, u32[]{:S(2)}) copy-start(f32[256]{0:T(256)} %param.23) | copy-start | bytes 3076
  43.8 3.4 %copy-start.16 = (s32[256]{0:T(256)S(1)}, s32[256]{0:T(256)}, u32[]{:S(2)}) copy-start(s32[256]{0:T(256)} %get-tuple-element.47) | copy-start | bytes 3076
  46.3 8.1 %copy-start.15 = (s32[256]{0:T(256)S(1)}, s32[256]{0:T(256)}, u32[]{:S(2)}) copy-start(s32[256]{0:T(256)} %get-tuple-element.19) | copy-start | bytes 3076
  47.2 11.1 %copy-start.23 = (f32[2048]{0:T(1024)S(1)}, f32[2048]{0:T(1024)}, u32[]{:S(2)}) copy-start(f32[2048]{0:T(1024)} %param.29) | copy-start | bytes 24580
  49.3 22.1 %collective-permute-start.1 = (bf16[512,512]{1,0:T(8,128)(2,1)}, bf16[512,512]{1,0:T(8,128)(2,1)}, u32[]{:S(2)}, u32[]{:S(2)}) collective-permute-start(bf16[512,512]{1,0:T(8,128)(2,1)} %pad_maximum_fusion.2), channel_id=1, source_target_pairs={{0,2},{1,3},{2,4},{3,5},{4,6},{5,7},{6,8},{7,9},{8,10},{9,11},{10,... | collective-permute-start | bytes 1572872 | tf_op jit(solution)/shard_map/ppermute | solution.py:24
  131.0 1.0 copy-start.1
  132.0 21.0 %copy-start.4 = (bf16[1024,2048]{1,0:T(8,128)(2,1)S(1)}, bf16[1024,2048]{1,0:T(8,128)(2,1)}, u32[]{:S(2)}) copy-start(bf16[1024,2048]{1,0:T(8,128)(2,1)} %param.25) | copy-start | bytes 12582916
  154.4 3.2 %collective-permute-start.3 = (bf16[256,2048]{1,0:T(8,128)(2,1)S(1)}, bf16[256,2048]{1,0:T(8,128)(2,1)S(1)}, u32[]{:S(2)}, u32[]{:S(2)}) collective-permute-start(bf16[256,2048]{1,0:T(8,128)(2,1)S(1)} %get-tuple-element.70), channel_id=1, source_target_pairs={{0,64},{64,0},{1,65},{65,1},{2,66},{66,2},{3,67},{67,3},{4,68},{68... | collective-permute-start | bytes 3145736 | tf_op jit(solution)/shard_map/ppermute | solution.py:357
  157.6 1.2 copy-start.3
  157.6 1.2 dynamic-slice-start
Sparse Core Ops, SparseCore 0:
  10.9 120.0 all-gather.1

commit v9 on v5

--- a/solution.py
+++ b/solution.py
@@ -334,9 +334,14 @@
         slot_pages,
     ).reshape(tok_count, -1)
     attn_part = jnp.dot(attended, w_out, preferred_element_type=jnp.float32)
-    partner_part = lax.ppermute(attn_part.astype(jnp.bfloat16), "kv", [(0, 1), (1, 0)])
-    summed_out = attn_part + partner_part.astype(jnp.float32)
-    attn_branch = columns(summed_out) * rms_scale(summed_out) * columns(post_gain)
+    swap = [(0, 1), (1, 0)]
+    partner_cols = lax.dynamic_slice_in_dim(attn_part, (1 - kv_index) * half_width, half_width, 1)
+    received = lax.ppermute(partner_cols.astype(jnp.bfloat16), "kv", swap)
+    summed_half = columns(attn_part) + received.astype(jnp.float32)
+    squares_here = jnp.sum(summed_half * summed_half, axis=-1)
+    squares_there = lax.ppermute(squares_here, "kv", swap)
+    attn_scale = lax.rsqrt((squares_here + squares_there) / model_width + epsilon)[:, None]
+    attn_branch = summed_half * attn_scale * columns(post_gain)
     layer_out = ((resident + attn_branch) * 2.0 ** (-0.5)).astype(jnp.bfloat16)
     return (layer_out, suffix_key_cache, suffix_value_cache)
 

time: 166 us -> 166 us (level)
  transfers between devices with their start and end apart: 5 -> 6, of which waited for: 3 -> 4; matrix products, arithmetic and copies ran while one was open for 29% -> 29% of each run, Pallas kernels for 0% -> 0%
where the time goes in v9:
time: 166 us
  waiting for transfers between devices  57.7 us (35%)
  other arithmetic  31.2 us (19%)
  Pallas kernels  21.6 us (13%)
  between operations  14.5 us (9%)
  local copies, waits for them, and re-layouts  14 us (8%)
  starting transfers between devices  13.4 us (8%)
  matrix products  13.2 us (8%)
    all_gather x1, waiting for transfers between devices, local(): every_slot = lax.all_gather(prefix_both, 'page', axis=0, tiled=True)  46.4 us
    pallas_call x1, Pallas kernels, page_attention(): pl.pallas_call(page_attention_kernel, grid_spec=grid_spec, out_shape=jax....  21.6 us
    ppermute x3, starting transfers between devices, passed_along(): return lax.ppermute(block, axis, route)  12.4 us
    ppermute x3, waiting for transfers between devices, passed_along(): return lax.ppermute(block, axis, route)  8.89 us
    unnamed x10, other arithmetic  7.23 us
    dot_general x1, matrix products, project(): jnp.dot(normed, w_query, preferred_element_type=jnp.float32)  4.43 us
    dot_general x1, matrix products, local(): attn_part = jnp.dot(attended, w_out, preferred_element_type=jnp.float32)  3.44 us
  transfers between devices with their start and end apart: 6, of which 4 were waited for; matrix products, arithmetic and copies ran while one was open for 29% of the time, Pallas kernels for 0%

profile of v9, /device:TPU:1, one launch (start us, length us, event | category | flops | bytes accessed | tf_op | source)
XLA Modules:
  0.0 165.6 jit_solution(13009589565814742263)
XLA Ops:
  7.2 1.8 %pad_maximum_fusion.6 = bf16[256,512]{1,0:T(8,128)(2,1)} fusion(bf16[256,256]{1,0:T(8,128)(2,1)} %param.31, bf16[256,256]{1,0:T(8,128)(2,1)} %param.30), kind=kLoop, calls=%fused_computation.25 | loop fusion | flops 524288 | bytes 524288 | tf_op jit(solution)/shard_map/concatenate | solution.py:248
  9.1 0.7 copy.46
  10.0 0.7 sub.123
  10.7 1.5 fusion
  12.2 1.0 fusion.2
  13.8 0.8 copy.45
  15.5 0.8 select_reduce_fusion
  16.3 1.1 multiply_bitcast_fusion
  18.0 0.7 pad_maximum_fusion.5
  18.8 4.6 %collective-permute-start = (bf16[256,512]{1,0:T(8,128)(2,1)}, bf16[256,512]{1,0:T(8,128)(2,1)}, u32[]{:S(2)}, u32[]{:S(2)}) collective-permute-start(bf16[256,512]{1,0:T(8,128)(2,1)} %pad_maximum_fusion.5), channel_id=1, source_target_pairs={{0,1},{1,2},{2,3},{3,4},{4,5},{5,6},{6,7},{7,8},{8,9},{9,10},{10,1... | collective-permute-start | bytes 786440 | tf_op jit(solution)/shard_map/ppermute | solution.py:24
  23.4 3.2 %collective-permute-start.2 = (bf16[256,512]{1,0:T(8,128)(2,1)}, bf16[256,512]{1,0:T(8,128)(2,1)}, u32[]{:S(2)}, u32[]{:S(2)}) collective-permute-start(bf16[256,512]{1,0:T(8,128)(2,1)} %pad_maximum_fusion.5), channel_id=1, source_target_pairs={{0,4},{1,5},{2,6},{3,7},{4,8},{5,9},{6,10},{7,11},{8,12},{9,13},{1... | collective-permute-start | bytes 786440 | tf_op jit(solution)/shard_map/ppermute | solution.py:24
  26.6 0.7 reshape_reshape.2
  27.3 4.4 %fusion.27 = f32[256,1024]{1,0:T(8,128)} fusion(bf16[256,2048]{1,0:T(8,128)(2,1)S(1)} %fusion.2, bf16[2048,1024]{1,0:T(8,128)(2,1)} %param.20), kind=kOutput, calls=%fused_computation.128 | convolution fusion | flops 1073741824 | bytes 6291456 | tf_op jit(solution)/shard_map/dot_general | solution.py:58
  31.7 1.7 %reshape.382 = f32[256,4,256]{2,1,0:T(4,128)S(1)} reshape(f32[256,1024]{1,0:T(8,128)} %fusion.27) | data formatting | bytes 2097152 | tf_op jit(solution)/shard_map/reshape | solution.py:58
  33.5 0.7 convert_element_type.83
  34.2 1.3 and_reduce_fusion
  35.8 1.1 multiply_cosine_fusion
  36.9 1.0 multiply_multiply_fusion
  38.3 0.9 pad_maximum_fusion.1.q_ref
  40.3 2.7 %multiply_reduce_fusion = (f32[256]{0:T(256)S(1)}, f32[256,2048]{1,0:T(8,128)}) fusion(bf16[64,2048]{1,0:T(8,128)(2,1)S(1)} %copy-done.7, bf16[256,2048]{1,0:T(8,128)(2,1)S(1)} %fusion.2, bf16[2048,64]{0,1:T(8,128)(2,1)S(1)} %copy-done.8), kind=kOutput, calls=%fused_computation.7 | convolution fusion | flops 135282432 | bytes 3671040 | tf_op jit(solution)/shard_map/dot_general | solution.py:316
  43.7 0.7 constant_dynamic-update-slice_fusion.7
  44.3 0.7 constant_dynamic-update-slice_fusion.5
  45.0 0.7 constant_dynamic-update-slice_fusion.3
  45.7 1.3 constant_dynamic-update-slice_fusion.8
  47.0 1.3 constant_dynamic-update-slice_fusion.6
  48.3 1.3 constant_dynamic-update-slice_fusion.4
  49.6 1.3 constant_dynamic-update-slice_fusion.2
  50.9 1.3 constant_dynamic-update-slice_fusion
  52.2 1.5 convolution_convert_fusion
  53.7 0.8 fusion.26
  55.1 0.7 dynamic_slice.24
  55.8 2.5 %add_add_fusion = f32[256,1024]{1,0:T(8,128)} fusion(f32[256,2048]{1,0:T(8,128)} %get-tuple-element.55, s32[]{:T(128)} %select_n.60, f32[1024]{0:T(1024)S(1)} %dynamic_slice.24, f32[256]{0:T(256)} %add_rsqrt_fusion.4, bf16[256,2048]{1,0:T(8,128)(2,1)S(1)} %fusion.2, bf16[256,2048]{1,0:T(8,128)(2,1)S(1)} %copy-done.4), kind=kLoop, calls=%fused_computation.17 | loop fusion | flops 1572864 | bytes 3150852 | tf_op jit(solution)/shard_map/add | solution.py:320
  58.4 1.8 %pad_maximum_fusion.2 = bf16[512,512]{1,0:T(8,128)(2,1)} fusion(bf16[256,512]{1,0:T(8,128)(2,1)} %collective-permute-done, bf16[256,256]{1,0:T(8,128)(2,1)S(1)} %multiply_convert_fusion.1, bf16[256,128]{1,0:T(8,128)(2,1)S(1)} %bitcast.38, bf16[256,128]{1,0:T(8,128)(2,1)S(1)} %bitcast.35), kind=kLoop, calls=%fused_computation.19 | loop fusion | flops 2097152 | bytes 1048576 | tf_op jit(solution)/shard_map/concatenate | solution.py:283
  60.2 4.5 %collective-permute-start.1 = (bf16[512,512]{1,0:T(8,128)(2,1)}, bf16[512,512]{1,0:T(8,128)(2,1)S(1)}, u32[]{:S(2)}, u32[]{:S(2)}) collective-permute-start(bf16[512,512]{1,0:T(8,128)(2,1)} %pad_maximum_fusion.2), channel_id=1, source_target_pairs={{0,2},{1,3},{2,4},{3,5},{4,6},{5,7},{6,8},{7,9},{8,10},{9,11},{10,... | collective-permute-start | bytes 1572872 | tf_op jit(solution)/shard_map/ppermute | solution.py:24
  64.8 1.6 reshape.380
  66.4 0.7 reshape.381
  67.2 0.8 broadcast_in_dim.17
  69.2 8.9 %collective-permute-done.1 = bf16[512,512]{1,0:T(8,128)(2,1)S(1)} collective-permute-done((bf16[512,512]{1,0:T(8,128)(2,1)}, bf16[512,512]{1,0:T(8,128)(2,1)S(1)}, u32[]{:S(2)}, u32[]{:S(2)}) %collective-permute-start.1) | collective-permute-done | bytes 524320 | tf_op jit(solution)/shard_map/ppermute | solution.py:24
  78.1 1.1 pad_maximum_fusion
  79.3 46.4 %all-gather.2.cloned.1.call-done = bf16[16384,512]{1,0:T(8,128)(2,1)} async-done(((bf16[256,512]{1,0:T(8,128)(2,1)}), bf16[16384,512]{1,0:T(8,128)(2,1)}) %all-gather.2.cloned.1.call-update) | async-done | bytes 16777232 | tf_op jit(solution)/shard_map/all_gather | solution.py:249
  125.7 1.0 copy-done.1
  126.8 21.6 %shard_map.193 = bf16[2,512,256]{2,1,0:T(8,128)(2,1)S(1)} custom-call(s32[2,32]{1,0:T(2,128)S(1)} %broadcast_select_fusion.table_ref, bf16[2,512,256]{2,1,0:T(8,128)(2,1)S(1)} %copy-done.1, s32[2,512,1]{2,1,0:T(8,128)S(1)} %broadcast_in_dim_reshape.8.row_req_ref, s32[2,512,1]{2,1,0:T(8,128)S(1)} %broadcast_in_dim_reshape.9.row_pos_ref, ...), custom_call_target="tpu_custom_call" | custom-call | flops 5637144576 | bytes 9437184 | tf_op jit(solution)/shard_map/pallas_call | solution.py:211
  148.3 0.8 copy-done.2
  149.1 1.4 reshape.386
  150.5 3.4 %fusion.28 = f32[256,2048]{1,0:T(8,128)S(1)} fusion(bf16[256,1024]{1,0:T(8,128)(2,1)S(1)} %reshape.386, bf16[1024,2048]{1,0:T(8,128)(2,1)} %param.25), kind=kOutput, calls=%fused_computation.129 | convolution fusion | flops 1073741824 | bytes 6815744 | tf_op jit(solution)/shard_map/dot_general | solution.py:336
  154.6 1.5 collective-permute-done.3
  156.8 0.8 collective-permute-done.4
  157.7 1.1 multiply_convert_fusion
  (92 shorter events, 8.0 us)
Async XLA Ops:
  7.2 6.1 %copy-start = (bf16[2048,256]{1,0:T(8,128)(2,1)S(1)}, bf16[2048,256]{1,0:T(8,128)(2,1)}, u32[]{:S(2)}) copy-start(bf16[2048,256]{1,0:T(8,128)(2,1)} %param.21) | copy-start | bytes 3145732
  7.2 5.0 %copy-start.3 = (bf16[256,2048]{1,0:T(8,128)(2,1)S(1)}, bf16[256,2048]{1,0:T(8,128)(2,1)}, u32[]{:S(2)}) copy-start(bf16[256,2048]{1,0:T(8,128)(2,1)} %param.18) | copy-start | bytes 3145732
  7.2 118.5 %all-gather.2.cloned.1.call-start = ((), (), s32[]{:S(2)}) async-start(), calls=%async_computation | async-start | bytes 17039360 | tf_op jit(solution)/shard_map/all_gather | solution.py:249
  13.2 1.4 copy-start.6
  13.8 1.7 %copy-start.17 = (s32[32]{0:T(128)S(1)}, s32[32]{0:T(128)}, u32[]{:S(2)}) copy-start(s32[32]{0:T(128)} %param.34) | copy-start | bytes 388
  13.8 2.5 %copy-start.15 = (f32[256]{0:T(256)S(1)}, f32[256]{0:T(256)}, u32[]{:S(2)}) copy-start(f32[256]{0:T(256)} %param.24) | copy-start | bytes 3076
  15.4 16.3 %copy-start.14 = (f32[128]{0:T(128)}, f32[128]{0:T(128)S(1)}, u32[]{:S(2)}) copy-start(f32[128]{0:T(128)S(1)} %negate_power_fusion) | copy-start | bytes 1540
  18.8 39.6 %collective-permute-start = (bf16[256,512]{1,0:T(8,128)(2,1)}, bf16[256,512]{1,0:T(8,128)(2,1)}, u32[]{:S(2)}, u32[]{:S(2)}) collective-permute-start(bf16[256,512]{1,0:T(8,128)(2,1)} %pad_maximum_fusion.5), channel_id=1, source_target_pairs={{0,1},{1,2},{2,3},{3,4},{4,5},{5,6},{6,7},{7,8},{8,9},{9,10},{10,1... | collective-permute-start | bytes 786440 | tf_op jit(solution)/shard_map/ppermute | solution.py:24
  23.4 45.8 %collective-permute-start.2 = (bf16[256,512]{1,0:T(8,128)(2,1)}, bf16[256,512]{1,0:T(8,128)(2,1)}, u32[]{:S(2)}, u32[]{:S(2)}) collective-permute-start(bf16[256,512]{1,0:T(8,128)(2,1)} %pad_maximum_fusion.5), channel_id=1, source_target_pairs={{0,4},{1,5},{2,6},{3,7},{4,8},{5,9},{6,10},{7,11},{8,12},{9,13},{1... | collective-permute-start | bytes 786440 | tf_op jit(solution)/shard_map/ppermute | solution.py:24
  36.9 2.2 %copy-start.21 = (s32[2]{0:T(128)S(1)}, s32[2]{0:T(128)}, u32[]{:S(2)}) copy-start(s32[2]{0:T(128)} %param.35) | copy-start | bytes 28
  38.0 2.3 %copy-start.7 = (bf16[64,2048]{1,0:T(8,128)(2,1)S(1)}, bf16[64,2048]{1,0:T(8,128)(2,1)}, u32[]{:S(2)}) copy-start(bf16[64,2048]{1,0:T(8,128)(2,1)} %param.28) | copy-start | bytes 786436
  38.0 2.3 %copy-start.8 = (bf16[2048,64]{0,1:T(8,128)(2,1)S(1)}, bf16[2048,64]{0,1:T(8,128)(2,1)}, u32[]{:S(2)}) copy-start(bf16[2048,64]{0,1:T(8,128)(2,1)} %param.27) | copy-start | bytes 786436
  39.1 11.7 %copy-start.12 = (s32[256]{0:T(256)S(1)}, s32[256]{0:T(256)}, u32[]{:S(2)}) copy-start(s32[256]{0:T(256)} %get-tuple-element.12) | copy-start | bytes 3076
  39.2 13.0 %copy-start.9 = (bf16[2,32768]{1,0:T(2,128)(2,1)S(1)}, bf16[2,32768]{1,0:T(2,128)(2,1)}, u32[]{:S(2)}) copy-start(bf16[2,32768]{1,0:T(2,128)(2,1)} %reshape_reshape.2) | copy-start | bytes 393220
  43.1 11.5 %copy-start.16 = (s32[256]{0:T(256)S(1)}, s32[256]{0:T(256)}, u32[]{:S(2)}) copy-start(s32[256]{0:T(256)} %get-tuple-element.29) | copy-start | bytes 3076
  43.1 12.8 %copy-start.4 = (bf16[256,2048]{1,0:T(8,128)(2,1)S(1)}, bf16[256,2048]{1,0:T(8,128)(2,1)}, u32[]{:S(2)}) copy-start(bf16[256,2048]{1,0:T(8,128)(2,1)} %param.18) | copy-start | bytes 3145732
  55.8 8.9 %copy-start.13 = (s32[256]{0:T(256)S(1)}, s32[256]{0:T(256)}, u32[]{:S(2)}) copy-start(s32[256]{0:T(256)} %get-tuple-element.11) | copy-start | bytes 3076
  55.8 8.9 %copy-start.20 = (s32[2]{0:T(128)S(1)}, s32[2]{0:T(128)}, u32[]{:S(2)}) copy-start(s32[2]{0:T(128)} %fusion.22) | copy-start | bytes 28
  55.8 11.3 %copy-start.10 = (s32[1280]{0:T(1024)S(1)}, s32[1280]{0:T(1024)}, u32[]{:S(2)}) copy-start(s32[1280]{0:T(1024)} %constant_dynamic-update-slice_fusion) | copy-start | bytes 15364
  58.4 9.8 %copy-start.11 = (s32[2,128]{1,0:T(2,128)S(1)}, s32[2,128]{1,0:T(2,128)}, u32[]{:S(2)}) copy-start(s32[2,128]{1,0:T(2,128)} %bitcast_subtract_fusion) | copy-start | bytes 3076
  58.4 10.1 %copy-start.18 = (s32[128]{0:T(128)S(1)}, s32[128]{0:T(128)}, u32[]{:S(2)}) copy-start(s32[128]{0:T(128)} %param.32) | copy-start | bytes 1540
  58.4 10.7 %copy-start.19 = (pred[2]{0:T(512)(128)(4,1)S(1)}, pred[2]{0:T(512)(128)(4,1)}, u32[]{:S(2)}) copy-start(pred[2]{0:T(512)(128)(4,1)} %and_reduce_fusion) | copy-start | bytes 10
  60.2 17.9 %collective-permute-start.1 = (bf16[512,512]{1,0:T(8,128)(2,1)}, bf16[512,512]{1,0:T(8,128)(2,1)S(1)}, u32[]{:S(2)}, u32[]{:S(2)}) collective-permute-start(bf16[512,512]{1,0:T(8,128)(2,1)} %pad_maximum_fusion.2), channel_id=1, source_target_pairs={{0,2},{1,3},{2,4},{3,5},{4,6},{5,7},{6,8},{7,9},{8,10},{9,11},{10,... | collective-permute-start | bytes 1572872 | tf_op jit(solution)/shard_map/ppermute | solution.py:24
  125.7 1.0 copy-start.1
  148.3 0.8 copy-start.2
  153.9 3.7 %copy-start.5 = (f32[256,1024]{1,0:T(8,128)S(1)}, f32[256,1024]{1,0:T(8,128)}, u32[]{:S(2)}) copy-start(f32[256,1024]{1,0:T(8,128)} %add_add_fusion) | copy-start | bytes 3145732
  153.9 3.7 %dynamic-slice-start = ((f32[2048]{0:T(1024)}, s32[]{:T(128)}), f32[1024]{0:T(1024)S(1)}, s32[]{:S(2)}) async-start(f32[2048]{0:T(1024)} %param.26, s32[]{:T(128)} %select_n.60), calls=%async_computation.1 | async-start | bytes 8704 | tf_op jit(solution)/shard_map/dynamic_slice | solution.py:313
  154.0 2.1 %collective-permute-start.3 = (bf16[256,1024]{1,0:T(8,128)(2,1)S(1)}, bf16[256,1024]{1,0:T(8,128)(2,1)S(1)}, u32[]{:S(2)}, u32[]{:S(2)}) collective-permute-start(bf16[256,1024]{1,0:T(8,128)(2,1)S(1)} %dynamic-slice_convert_fusion), channel_id=1, source_target_pairs={{0,64},{64,0},{1,65},{65,1},{2,66},{66,2},{3,67},{67,3},{4,68},{68... | collective-permute-start | bytes 1572872 | tf_op jit(solution)/shard_map/ppermute | solution.py:339
  156.4 1.3 collective-permute-start.4
Sparse Core Ops, SparseCore 0:
  10.9 114.8 all-gather.1
